TPU v7x, 256 devices: a whole 4x4x8 slice. The times are simulated.
256 devices in a mesh: member: 8 (over z_hi, core), tile: 32 (over y, x, z_lo).
Axes of the slice: x: 4, y: 4, z: 8 (z_hi: 4, z_lo: 2; z = z_hi * 2 + z_lo), core: 2. Of those that a mesh axis runs over, the one named last changes fastest.
Arguments:
- upsampled_coarse: bfloat16 [128, 32, 256], P('tile'), may hold values from -6 to 6
- target: bfloat16 [128, 32, 256], P('tile'), may hold values from -6 to 6
- seeds: int32 [16], P('member'), may hold values from 0 to 63
- band_row: int32 [1], replicated, may hold values from 0 to 1920
- noise_bank: float32 [64, 16], replicated, may hold values from -5 to 5
- cond_weight: float32 [16, 256], replicated, may hold values from -1.5 to 1.5
- conv_in: bfloat16 [3, 3, 32, 128], replicated, may hold values from -0.375 to 0.375
- conv_mid: bfloat16 [3, 3, 128, 128], replicated, may hold values from -0.1875 to 0.1875
- conv_out: bfloat16 [3, 3, 128, 128], replicated, may hold values from -0.1875 to 0.1875
- head_weight: bfloat16 [128, 32], replicated, may hold values from -0.5 to 0.5
- per_quantity_offset: float32 [32], replicated, may hold values from -3 to 3
Outputs:
- crps_map: float32 [128, 32, 256], P('tile', 'member')
- conv_grad: float32 [3, 3, 128, 128], replicated
- head_grad: float32 [128, 32], replicated
- bias_grad: float32 [32], replicated
Inputs may be any that keep to these rules, and one draw needn't show every extreme that they name: `band_row`: the band lies inside the grid.
All inputs are finite; a program needn't handle non-finite values.
Results may differ from a plain program's by a relative error of at most 0.0015.
Values may be sent and summed in bfloat16 or wider, within the bound.
No kernel may reach another device: no remote copies, remote signals or barrier semaphores. Data moves between devices by JAX's collectives and lax.ppermute only.
A program may use at most 64 MiB of HBM per device.

v0:
```python
import math

import jax
import jax.numpy as jnp
from jax import lax
from jax.sharding import PartitionSpec as P

GRID_ROWS = 2048


def extended(x, sides, width):
    for axis, dim in sides:
        devices, length = (lax.axis_size(axis), x.shape[dim])
        up = [(i, (i + 1) % devices) for i in range(devices - 1)]
        down = [(j, i) for i, j in up]
        last = lax.slice_in_dim(x, length - width, length, axis=dim)
        first = lax.slice_in_dim(x, 0, width, axis=dim)
        before = lax.ppermute(last, axis, up)
        after = lax.ppermute(first, axis, down)
        x = jnp.concatenate([before, x, after], axis=dim)
    return x


def input_conv(padded, kernel):
    out_rows = padded.shape[0] - 2
    col_count = padded.shape[2]
    wide = jnp.pad(padded, ((0, 0), (0, 0), (1, 1)))
    summed = jnp.zeros((out_rows, col_count, kernel.shape[3]), jnp.float32)
    for i in range(3):
        for j in range(3):
            summed = summed + jnp.einsum(
                "rkw,kc->rwc",
                wide[i : i + out_rows, :, j : j + col_count],
                kernel[i, j],
                preferred_element_type=jnp.float32,
            )
    return summed


def feature_conv(padded, kernel):
    out_rows = padded.shape[1] - 2
    col_count = padded.shape[2]
    wide = jnp.pad(padded, ((0, 0), (0, 0), (1, 1), (0, 0)))
    summed = jnp.zeros((padded.shape[0], out_rows, col_count, kernel.shape[3]), jnp.float32)
    for i in range(3):
        for j in range(3):
            summed = summed + jnp.einsum(
                "mrwc,cd->mrwd",
                wide[:, i : i + out_rows, j : j + col_count],
                kernel[i, j],
                preferred_element_type=jnp.float32,
            )
    return summed


def condition(base, cond_scale, cond_shift):
    average = jnp.mean(base, axis=-1, keepdims=True)
    centred = base - average
    spread = jnp.mean(centred * centred, axis=-1, keepdims=True)
    normed = centred * lax.rsqrt(spread + 1e-05)
    mixed = normed[None] * (1.0 + cond_scale[:, None, None, :]) + cond_shift[:, None, None, :]
    return jax.nn.gelu(mixed).astype(jnp.bfloat16)


def abs_terms(probe, sample_group_predictions):

    def abs_single(member_index):
        return jnp.sum(jnp.abs(member_index[None] - sample_group_predictions), axis=0)

    return lax.map(abs_single, probe)


def sign_terms(probe, sample_group_predictions):

    def sign_single(member_index):
        return jnp.sum(jnp.sign(member_index[None] - sample_group_predictions), axis=0)

    return lax.map(sign_single, probe)


def on_device(
    upsampled_coarse,
    target,
    seeds,
    band_row,
    noise_bank,
    cond_weight,
    conv_in,
    conv_mid,
    conv_out,
    head_weight,
    per_quantity_offset,
):
    channels = conv_mid.shape[3]
    row_count = upsampled_coarse.shape[0]
    var_count = upsampled_coarse.shape[1]
    col_count = upsampled_coarse.shape[2]
    tile_count = lax.axis_size("tile")
    tile_at = lax.axis_index("tile")
    band_rows = row_count * tile_count
    selector = (seeds[:, None] == jnp.arange(noise_bank.shape[0], dtype=jnp.int32)[None]).astype(
        jnp.float32
    )
    noise_vec = jnp.dot(selector, noise_bank, precision=lax.Precision.HIGHEST)
    random_latent_gain = jnp.dot(noise_vec, cond_weight, precision=lax.Precision.HIGHEST)
    cond_scale = random_latent_gain[:, :channels]
    cond_shift = random_latent_gain[:, channels:]
    input_padded = extended(upsampled_coarse, (("tile", 0),), 1)
    first_hidden = condition(input_conv(input_padded, conv_in), cond_scale, cond_shift)
    first_padded = extended(first_hidden, (("tile", 1),), 1)
    latent_layer_two = jax.nn.gelu(feature_conv(first_padded, conv_mid)).astype(jnp.bfloat16)
    second_padded = extended(latent_layer_two, (("tile", 1),), 1)
    final_linear_response = feature_conv(second_padded, conv_out)
    latent_layer_three = (
        first_hidden.astype(jnp.float32) + jax.nn.gelu(final_linear_response)
    ).astype(jnp.bfloat16)
    final_layer_result = jnp.einsum(
        "mrwc,cv->mrvw", latent_layer_three, head_weight, preferred_element_type=jnp.float32
    )
    sample_prediction = (
        final_layer_result
        + upsampled_coarse.astype(jnp.float32)[None]
        + per_quantity_offset[None, None, :, None]
    ).astype(jnp.bfloat16)
    row_global = band_row[0] + tile_at * row_count + jnp.arange(row_count, dtype=jnp.int32)
    latitude = math.pi * (row_global.astype(jnp.float32) + 0.5) / GRID_ROWS - math.pi / 2
    row_factor = (jnp.cos(latitude) / (band_rows * col_count))[None, :, None, None]
    var_share = var_count // lax.axis_size("member")
    var_start = lax.axis_index("member") * var_share
    collected_members = lax.all_to_all(
        sample_prediction, "member", split_axis=2, concat_axis=0, tiled=True
    )
    sample_group_predictions = collected_members.astype(jnp.float32)
    member_count = sample_group_predictions.shape[0]
    truth = lax.dynamic_slice_in_dim(target, var_start, var_share, 1).astype(jnp.float32)
    abs_sums = abs_terms(sample_group_predictions, sample_group_predictions)
    sign_sums = sign_terms(sample_group_predictions, sample_group_predictions)
    crps_map = jnp.mean(jnp.abs(sample_group_predictions - truth[None]), axis=0) - jnp.sum(
        abs_sums, axis=0
    ) / (2 * member_count * (member_count - 1))
    cot_share = (
        row_factor
        * (
            jnp.sign(sample_group_predictions - truth[None]) / member_count
            - sign_sums / (member_count * (member_count - 1))
        )
    ).astype(jnp.bfloat16)
    cotangent = lax.all_to_all(cot_share, "member", split_axis=0, concat_axis=2, tiled=True)
    head_grad = jnp.einsum(
        "mrwc,mrvw->cv", latent_layer_three, cotangent, preferred_element_type=jnp.float32
    )
    bias_grad = jnp.sum(cotangent.astype(jnp.float32), axis=(0, 1, 3))
    back = jnp.einsum("mrvw,cv->mrwc", cotangent, head_weight, preferred_element_type=jnp.float32)
    unused_out, pullback = jax.vjp(jax.nn.gelu, final_linear_response)
    d_pre = pullback(back)[0].astype(jnp.bfloat16)
    second_wide = jnp.pad(second_padded, ((0, 0), (0, 0), (1, 1), (0, 0)))
    rows_of = []
    for i in range(3):
        cols_of = []
        for j in range(3):
            cols_of.append(
                jnp.einsum(
                    "mrwc,mrwd->cd",
                    second_wide[:, i : i + row_count, j : j + col_count],
                    d_pre,
                    preferred_element_type=jnp.float32,
                )
            )
        rows_of.append(jnp.stack(cols_of))
    conv_grad = jnp.stack(rows_of)
    conv_grad, head_grad, bias_grad = lax.psum(
        (conv_grad, head_grad, bias_grad), ("member", "tile")
    )
    return (crps_map, conv_grad, head_grad, bias_grad)


def solution(mesh):
    return jax.shard_map(
        on_device,
        mesh=mesh,
        in_specs=(
            P("tile", None, None),
            P("tile", None, None),
            P("member"),
            P(),
            P(),
            P(),
            P(),
            P(),
            P(),
            P(),
            P(),
        ),
        out_specs=(P("tile", "member", None), P(), P(), P()),
        check_vma=False,
    )
```

profile of v0, /device:TPU:1, one launch (start us, length us, event | category | flops | bytes accessed | tf_op | source)
XLA Modules:
  0.0 377.2 jit_solution(10002536229414040195)
XLA Ops:
  7.2 0.8 fusion.156
  8.0 4.3 %collective-permute-start = (bf16[1,32,256]{2,1,0:T(8,128)(2,1)S(1)}, bf16[1,32,256]{2,1,0:T(8,128)(2,1)S(1)}, u32[]{:S(2)}, u32[]{:S(2)}) collective-permute-start(bf16[1,32,256]{2,1,0:T(8,128)(2,1)S(1)} %get-tuple-element.66), channel_id=1, source_target_pairs={{0,1},{1,2},{2,3},{3,4},{4,5},{5,6},{6,7},{7,8},{8,9},{9,10},{10,1... | collective-permute-start | bytes 49160 | tf_op jit(solution)/shard_map/ppermute | solution.py:18
  12.3 1.3 collective-permute-start.1
  13.6 0.9 fusion.142
  14.7 2.1 collective-permute-done.1
  16.8 0.9 fusion.70
  17.8 1.0 fusion.78
  18.8 1.1 fusion.71
  22.9 3.7 collective-permute-start.2
  26.6 1.3 collective-permute-start.3
  27.9 0.6 collective-permute-done.2
  28.5 5.1 %collective-permute-done.3 = bf16[2,1,256,128]{3,2,1,0:T(8,128)(2,1)S(1)} collective-permute-done((bf16[2,1,256,128]{3,2,1,0:T(8,128)(2,1)S(1)}, bf16[2,1,256,128]{3,2,1,0:T(8,128)(2,1)S(1)}, u32[]{:S(2)}, u32[]{:S(2)}) %collective-permute-start.3) | collective-permute-done | bytes 131104 | tf_op jit(solution)/shard_map/ppermute | solution.py:19
  36.8 3.7 collective-permute-start.4
  40.5 1.3 collective-permute-start.5
  42.4 5.2 %collective-permute-done.5 = bf16[2,1,256,128]{3,2,1,0:T(8,128)(2,1)S(1)} collective-permute-done((bf16[2,1,256,128]{3,2,1,0:T(8,128)(2,1)S(1)}, bf16[2,1,256,128]{3,2,1,0:T(8,128)(2,1)S(1)}, u32[]{:S(2)}, u32[]{:S(2)}) %collective-permute-start.5) | collective-permute-done | bytes 131104 | tf_op jit(solution)/shard_map/ppermute | solution.py:19
  50.2 0.6 add_convert_fusion
  51.1 0.8 copy.69
  51.9 10.0 %all-to-all-start = ((bf16[2,4,32,256]{3,1,0,2:T(4,128)(2,1)}), bf16[2,4,32,256]{3,1,0,2:T(4,128)(2,1)S(1)}, u32[]{:S(2)}, u32[]{:S(2)}) async-start(bf16[2,4,32,256]{3,1,0,2:T(4,128)(2,1)} %copy.69), calls=%async_computation | async-start | bytes 262144 | tf_op jit(solution)/shard_map/all_to_all | solution.py:130
  62.5 0.7 dynamic-slice_convert_fusion
  63.3 7.2 %all-to-all-done = bf16[2,4,32,256]{3,1,0,2:T(4,128)(2,1)S(1)} async-done(((bf16[2,4,32,256]{3,1,0,2:T(4,128)(2,1)}), bf16[2,4,32,256]{3,1,0,2:T(4,128)(2,1)S(1)}, u32[]{:S(2)}, u32[]{:S(2)}) %all-to-all-start) | async-done | bytes 131104 | tf_op jit(solution)/shard_map/all_to_all | solution.py:130
  70.6 0.8 broadcast.97.clone.1
  71.4 12.7 %while.21 = (s32[]{:T(128)}, f32[16,4,4,256]{3,2,1,0:T(4,128)}, f32[16,4,4,256]{3,2,1,0:T(4,128)S(1)}, s32[]{:T(128)}) while((s32[]{:T(128)}, f32[16,4,4,256]{3,2,1,0:T(4,128)}, f32[16,4,4,256]{3,2,1,0:T(4,128)S(1)}, s32[]{:T(128)}) %tuple.52), condition=%wide.region_9.10_spmd, body=%wide.region_7.9_spmd.sunk | while | flops 192514 | bytes 361017 | solution.py:78
  84.1 1.8 multiply_convert_fusion
  85.9 4.6 %all-to-all-start.1 = ((bf16[16,4,4,256]{3,2,1,0:T(4,128)(2,1)}), bf16[16,4,4,256]{3,2,1,0:T(4,128)(2,1)S(1)}, u32[]{:S(2)}, u32[]{:S(2)}) async-start(bf16[16,4,4,256]{3,2,1,0:T(4,128)(2,1)} %multiply_convert_fusion), calls=%async_computation.1 | async-start | bytes 262144 | tf_op jit(solution)/shard_map/all_to_all | solution.py:148
  90.5 0.8 broadcast.97.clone
  91.3 11.3 %while.20 = (s32[]{:T(128)}, f32[16,4,4,256]{3,2,1,0:T(4,128)}, f32[16,4,4,256]{3,2,1,0:T(4,128)S(1)}, s32[]{:T(128)}) while((s32[]{:T(128)}, f32[16,4,4,256]{3,2,1,0:T(4,128)}, f32[16,4,4,256]{3,2,1,0:T(4,128)S(1)}, s32[]{:T(128)}) %tuple.53), condition=%wide.region_5.6_spmd, body=%wide.region_3.5_spmd.sunk | while | flops 192514 | bytes 361017 | solution.py:70
  102.6 1.0 reduce_sum.68
  103.8 0.9 fusion.13
  108.9 0.9 pad_maximum_fusion.2
  110.9 82.8 %all-reduce.3 = (f32[128,32]{0,1:T(8,128)}, f32[32]{0:T(128)}) all-reduce(f32[128,32]{0,1:T(8,128)S(1)} %convolution_bitcast_fusion.10, f32[32]{0:T(128)S(1)} %reduce_sum.70), channel_id=1, replica_groups=mesh['member'=8,'tile'=32] {'member','tile'}, use_global_device_ids=true, to_apply=%region_11.12 | all-reduce | flops 4128 | bytes 33024 | tf_op jit(solution)/shard_map/psum | solution.py:171
  193.7 174.7 %all-reduce.6.cloned.1.call-done = f32[3,3,128,128]{3,2,1,0:T(8,128)} async-done(((f32[3,3,128,128]{3,2,1,0:T(8,128)}), f32[3,3,128,128]{3,2,1,0:T(8,128)}) %all-reduce.6.cloned.1.call-update) | async-done | bytes 589840 | tf_op jit(solution)/shard_map/psum | solution.py:171
  368.4 1.9 copy.146
  (184 shorter events, 39.2 us)
Async XLA Ops:
  7.2 7.4 %copy-start = (f32[16,256]{1,0:T(8,128)S(1)}, f32[16,256]{1,0:T(8,128)}, u32[]{:S(2)}) copy-start(f32[16,256]{1,0:T(8,128)} %param.20) | copy-start | bytes 49156
  7.2 12.6 %copy-start.8 = (bf16[3,3,32,128]{3,2,1,0:T(8,128)(2,1)S(1)}, bf16[3,3,32,128]{3,2,1,0:T(8,128)(2,1)}, u32[]{:S(2)}) copy-start(bf16[3,3,32,128]{3,2,1,0:T(8,128)(2,1)} %param.21) | copy-start | bytes 221188
  8.0 6.7 %collective-permute-start = (bf16[1,32,256]{2,1,0:T(8,128)(2,1)S(1)}, bf16[1,32,256]{2,1,0:T(8,128)(2,1)S(1)}, u32[]{:S(2)}, u32[]{:S(2)}) collective-permute-start(bf16[1,32,256]{2,1,0:T(8,128)(2,1)S(1)} %get-tuple-element.66), channel_id=1, source_target_pairs={{0,1},{1,2},{2,3},{3,4},{4,5},{5,6},{6,7},{7,8},{8,9},{9,10},{10,1... | collective-permute-start | bytes 49160 | tf_op jit(solution)/shard_map/ppermute | solution.py:18
  12.3 4.5 %collective-permute-start.1 = (bf16[1,32,256]{2,1,0:T(8,128)(2,1)S(1)}, bf16[1,32,256]{2,1,0:T(8,128)(2,1)S(1)}, u32[]{:S(2)}, u32[]{:S(2)}) collective-permute-start(bf16[1,32,256]{2,1,0:T(8,128)(2,1)S(1)} %get-tuple-element.67), channel_id=1, source_target_pairs={{1,0},{2,1},{3,2},{4,3},{5,4},{6,5},{7,6},{8,7},{9,8},{10,9},{11,1... | collective-permute-start | bytes 49160 | tf_op jit(solution)/shard_map/ppermute | solution.py:19
  20.1 0.8 copy-start.1
  22.9 11.0 %copy-start.7 = (bf16[3,3,128,128]{3,2,1,0:T(8,128)(2,1)S(1)}, bf16[3,3,128,128]{3,2,1,0:T(8,128)(2,1)}, u32[]{:S(2)}) copy-start(bf16[3,3,128,128]{3,2,1,0:T(8,128)(2,1)} %param.22) | copy-start | bytes 884740
  22.9 5.6 %collective-permute-start.2 = (bf16[2,1,256,128]{3,2,1,0:T(8,128)(2,1)S(1)}, bf16[2,1,256,128]{3,2,1,0:T(8,128)(2,1)S(1)}, u32[]{:S(2)}, u32[]{:S(2)}) collective-permute-start(bf16[2,1,256,128]{3,2,1,0:T(8,128)(2,1)S(1)} %get-tuple-element.64), channel_id=1, source_target_pairs={{0,1},{1,2},{2,3},{3,4},{4,5},{5,6},{6,7},{7,8},{8,9},{9,10},{10,1... | collective-permute-start | bytes 393224 | tf_op jit(solution)/shard_map/ppermute | solution.py:18
  26.6 7.0 %collective-permute-start.3 = (bf16[2,1,256,128]{3,2,1,0:T(8,128)(2,1)S(1)}, bf16[2,1,256,128]{3,2,1,0:T(8,128)(2,1)S(1)}, u32[]{:S(2)}, u32[]{:S(2)}) collective-permute-start(bf16[2,1,256,128]{3,2,1,0:T(8,128)(2,1)S(1)} %get-tuple-element.65), channel_id=1, source_target_pairs={{1,0},{2,1},{3,2},{4,3},{5,4},{6,5},{7,6},{8,7},{9,8},{10,9},{11,1... | collective-permute-start | bytes 393224 | tf_op jit(solution)/shard_map/ppermute | solution.py:19
  36.8 11.1 %copy-start.6 = (bf16[3,3,128,128]{3,2,1,0:T(8,128)(2,1)S(1)}, bf16[3,3,128,128]{3,2,1,0:T(8,128)(2,1)}, u32[]{:S(2)}) copy-start(bf16[3,3,128,128]{3,2,1,0:T(8,128)(2,1)} %param.23) | copy-start | bytes 884740
  36.8 5.6 %collective-permute-start.4 = (bf16[2,1,256,128]{3,2,1,0:T(8,128)(2,1)S(1)}, bf16[2,1,256,128]{3,2,1,0:T(8,128)(2,1)S(1)}, u32[]{:S(2)}, u32[]{:S(2)}) collective-permute-start(bf16[2,1,256,128]{3,2,1,0:T(8,128)(2,1)S(1)} %get-tuple-element.62), channel_id=1, source_target_pairs={{0,1},{1,2},{2,3},{3,4},{4,5},{5,6},{6,7},{7,8},{8,9},{9,10},{10,1... | collective-permute-start | bytes 393224 | tf_op jit(solution)/shard_map/ppermute | solution.py:18
  40.5 7.1 %collective-permute-start.5 = (bf16[2,1,256,128]{3,2,1,0:T(8,128)(2,1)S(1)}, bf16[2,1,256,128]{3,2,1,0:T(8,128)(2,1)S(1)}, u32[]{:S(2)}, u32[]{:S(2)}) collective-permute-start(bf16[2,1,256,128]{3,2,1,0:T(8,128)(2,1)S(1)} %get-tuple-element.63), channel_id=1, source_target_pairs={{1,0},{2,1},{3,2},{4,3},{5,4},{6,5},{7,6},{8,7},{9,8},{10,9},{11,1... | collective-permute-start | bytes 393224 | tf_op jit(solution)/shard_map/ppermute | solution.py:19
  42.4 5.7 %copy-start.4 = (bf16[2,1,256,128]{3,2,1,0:T(8,128)(2,1)}, bf16[2,1,256,128]{3,2,1,0:T(8,128)(2,1)S(1)}, u32[]{:S(2)}) copy-start(bf16[2,1,256,128]{3,2,1,0:T(8,128)(2,1)S(1)} %collective-permute-done.4) | copy-start | bytes 393220
  47.6 2.5 copy-start.2
  50.1 0.7 copy-start.9
  50.2 0.7 copy-start.10
  51.9 18.6 %all-to-all-start = ((bf16[2,4,32,256]{3,1,0,2:T(4,128)(2,1)}), bf16[2,4,32,256]{3,1,0,2:T(4,128)(2,1)S(1)}, u32[]{:S(2)}, u32[]{:S(2)}) async-start(bf16[2,4,32,256]{3,1,0,2:T(4,128)(2,1)} %copy.69), calls=%async_computation | async-start | bytes 262144 | tf_op jit(solution)/shard_map/all_to_all | solution.py:130
  85.9 17.7 %all-to-all-start.1 = ((bf16[16,4,4,256]{3,2,1,0:T(4,128)(2,1)}), bf16[16,4,4,256]{3,2,1,0:T(4,128)(2,1)S(1)}, u32[]{:S(2)}, u32[]{:S(2)}) async-start(bf16[16,4,4,256]{3,2,1,0:T(4,128)(2,1)} %multiply_convert_fusion), calls=%async_computation.1 | async-start | bytes 262144 | tf_op jit(solution)/shard_map/all_to_all | solution.py:148
  90.5 277.9 %all-reduce.6.cloned.1.call-start = ((), (), s32[]{:S(2)}) async-start(), calls=%async_computation.2 | async-start | bytes 1179648 | tf_op jit(solution)/shard_map/psum | solution.py:171
  106.8 0.9 copy-start.3
  107.7 0.9 copy-start.5
Sparse Core Ops, SparseCore 0:
  110.0 258.3 all-reduce.5
where the time goes:
time: 378 us; the launch traced here: 377 us
  waiting for transfers between devices  196 us (52%)
  blocking collectives  82.8 us (22%)
  starting transfers between devices  30.2 us (8%)
  local copies, waits for them, and re-layouts  27.1 us (7%)
  matrix products  15.2 us (4%)
  between operations  15.2 us (4%)
  other arithmetic  11.1 us (3%)
    psum x1, waiting for transfers between devices, on_device(): lax.psum((conv_grad, head_grad, bias_grad), ('member', 'tile'))  175 us
    psum x1, blocking collectives, on_device(): lax.psum((conv_grad, head_grad, bias_grad), ('member', 'tile'))  82.8 us
    dynamic_update_slice x32, local copies, waits for them, and re-layouts, abs_terms(): return lax.map(abs_single, probe)  19.5 us
    ppermute x3, waiting for transfers between devices, extended(): after = lax.ppermute(first, axis, down)  12.4 us
    ppermute x3, starting transfers between devices, extended(): before = lax.ppermute(last, axis, up)  11.7 us
    all_to_all x1, starting transfers between devices, on_device(): lax.all_to_all(sample_prediction, 'member', split_axis=2, concat_axis=0,...  9.99 us
  transfers between devices with their start and end apart: 9, of which 7 were waited for; matrix products, arithmetic and copies ran while one was open for 4% of the time, Pallas kernels for 0%

commit v1 on v0

--- a/solution.py
+++ b/solution.py
@@ -76,6 +76,25 @@
         return jnp.sum(jnp.sign(member_index[None] - sample_group_predictions), axis=0)
 
     return lax.map(sign_single, probe)
+
+
+def all_reduce_sum(parts, axes):
+    devices = 1
+    for axis in axes:
+        devices *= lax.axis_size(axis)
+    flat = jnp.concatenate([p.reshape(-1) for p in parts])
+    total = flat.shape[0]
+    width = -(-total // devices)
+    flat = jnp.pad(flat, (0, width * devices - total)).reshape(devices, width)
+    pieces = lax.all_to_all(flat, axes, 0, 0, tiled=True)
+    own = jnp.sum(pieces, axis=0, keepdims=True)
+    spread = lax.all_to_all(jnp.broadcast_to(own, (devices, width)), axes, 0, 0, tiled=True)
+    spread = spread.reshape(-1)
+    out, at = [], 0
+    for p in parts:
+        out.append(spread[at : at + p.size].reshape(p.shape))
+        at += p.size
+    return tuple(out)
 
 
 def on_device(
@@ -168,9 +187,7 @@
             )
         rows_of.append(jnp.stack(cols_of))
     conv_grad = jnp.stack(rows_of)
-    conv_grad, head_grad, bias_grad = lax.psum(
-        (conv_grad, head_grad, bias_grad), ("member", "tile")
-    )
+    conv_grad, head_grad, bias_grad = all_reduce_sum((conv_grad, head_grad, bias_grad), ("member", "tile"))
     return (crps_map, conv_grad, head_grad, bias_grad)
 
 

time: 378 us -> 169 us (0.45)
  waiting for transfers between devices: 196 us -> 63 us
  blocking collectives: 82.8 us -> 12.4 us
  starting transfers between devices: 30.2 us -> 45.4 us
  local copies, waits for them, and re-layouts: 27.1 us -> 13.4 us
  between operations: 15.2 us -> 1.86 us
  matrix products: 15.2 us -> 20.8 us
    psum x1 -> x0, waiting for transfers between devices: 175 us -> none  [on_device(): lax.psum((conv_grad, head_grad, bias_grad), ('member', 'tile'))]
    psum x1 -> x0, blocking collectives: 82.8 us -> none  [on_device(): lax.psum((conv_grad, head_grad, bias_grad), ('member', 'tile'))]
    all_to_all x1 -> x2, waiting for transfers between devices: 0.01 us -> 42.2 us  [the longest x1 22.5 us: all_reduce_sum(): pieces = lax.all_to_all(flat, axes, 0, 0, tiled=True)]
    dynamic_update_slice x32, local copies, waits for them, and re-layouts: 19.5 us -> 0.4 us  [abs_terms(): return lax.map(abs_single, probe)]
    all_to_all x1 -> x2, starting transfers between devices: 4.57 us -> 19.9 us  [the longest x1 13.2 us: all_reduce_sum(): pieces = lax.all_to_all(flat, axes, 0, 0, tiled=True)]
    all_to_all x0 -> x1, blocking collectives: none -> 12.4 us  [on_device(): lax.all_to_all(cot_share, 'member', split_axis=0, concat_axis=2, tiled=True)]
    slice x0 -> x4, local copies, waits for them, and re-layouts: none -> 4.79 us  [all_reduce_sum(): out.append(spread[at:at + p.size].reshape(p.shape))]
  transfers between devices with their start and end apart: 9 -> 9, of which waited for: 7 -> 8; matrix products, arithmetic and copies ran while one was open for 4% -> 3% of each run, Pallas kernels for 0% -> 0%
where the time goes in v1:
time: 169 us; the launch traced here: 168 us
  waiting for transfers between devices  63 us (37%)
  starting transfers between devices  45.4 us (27%)
  matrix products  20.8 us (12%)
  local copies, waits for them, and re-layouts  13.4 us (8%)
  blocking collectives  12.4 us (7%)
  other arithmetic  9.85 us (6%)
  between operations  1.86 us (1%)
    all_to_all x1, waiting for transfers between devices, all_reduce_sum(): pieces = lax.all_to_all(flat, axes, 0, 0, tiled=True)  22.5 us
    all_to_all x1, waiting for transfers between devices, all_reduce_sum(): lax.all_to_all(jnp.broadcast_to(own, (devices, width)), axes, 0, 0, tiled...  19.7 us
    all_to_all x1, starting transfers between devices, all_reduce_sum(): pieces = lax.all_to_all(flat, axes, 0, 0, tiled=True)  13.2 us
    ppermute x3, waiting for transfers between devices, extended(): after = lax.ppermute(first, axis, down)  12.4 us
    all_to_all x1, blocking collectives, on_device(): lax.all_to_all(cot_share, 'member', split_axis=0, concat_axis=2, tiled=True)  12.4 us
    ppermute x3, starting transfers between devices, extended(): before = lax.ppermute(last, axis, up)  11.6 us
    all_to_all x1, starting transfers between devices, on_device(): lax.all_to_all(sample_prediction, 'member', split_axis=2, concat_axis=0,...  9.95 us
    all_to_all x1, waiting for transfers between devices, on_device(): lax.all_to_all(sample_prediction, 'member', split_axis=2, concat_axis=0,...  7.2 us
  transfers between devices with their start and end apart: 9, of which 8 were waited for; matrix products, arithmetic and copies ran while one was open for 3% of the time, Pallas kernels for 0%

profile of v1, /device:TPU:1, one launch (start us, length us, event | category | flops | bytes accessed | tf_op | source)
XLA Modules:
  0.0 167.6 jit_solution(9422065231385949117)
XLA Ops:
  1.4 4.3 %collective-permute-start = (bf16[1,32,256]{2,1,0:T(8,128)(2,1)S(1)}, bf16[1,32,256]{2,1,0:T(8,128)(2,1)S(1)}, u32[]{:S(2)}, u32[]{:S(2)}) collective-permute-start(bf16[1,32,256]{2,1,0:T(8,128)(2,1)S(1)} %get-tuple-element.72), channel_id=1, source_target_pairs={{0,1},{1,2},{2,3},{3,4},{4,5},{5,6},{6,7},{7,8},{8,9},{9,10},{10,1... | collective-permute-start | bytes 49160 | tf_op jit(solution)/shard_map/ppermute | solution.py:18
  5.8 1.3 collective-permute-start.1
  8.1 2.1 %collective-permute-done.1 = bf16[1,32,256]{2,1,0:T(8,128)(2,1)S(1)} collective-permute-done((bf16[1,32,256]{2,1,0:T(8,128)(2,1)S(1)}, bf16[1,32,256]{2,1,0:T(8,128)(2,1)S(1)}, u32[]{:S(2)}, u32[]{:S(2)}) %collective-permute-start.1) | collective-permute-done | bytes 16416 | tf_op jit(solution)/shard_map/ppermute | solution.py:19
  11.2 1.0 fusion.78
  12.2 1.1 fusion.71
  13.3 1.0 convolution_add_fusion.20
  16.8 3.6 %collective-permute-start.2 = (bf16[2,1,256,128]{3,2,1,0:T(8,128)(2,1)S(1)}, bf16[2,1,256,128]{3,2,1,0:T(8,128)(2,1)S(1)}, u32[]{:S(2)}, u32[]{:S(2)}) collective-permute-start(bf16[2,1,256,128]{3,2,1,0:T(8,128)(2,1)S(1)} %get-tuple-element.70), channel_id=1, source_target_pairs={{0,1},{1,2},{2,3},{3,4},{4,5},{5,6},{6,7},{7,8},{8,9},{9,10},{10,1... | collective-permute-start | bytes 393224 | tf_op jit(solution)/shard_map/ppermute | solution.py:18
  20.4 1.3 collective-permute-start.3
  22.3 5.1 %collective-permute-done.3 = bf16[2,1,256,128]{3,2,1,0:T(8,128)(2,1)S(1)} collective-permute-done((bf16[2,1,256,128]{3,2,1,0:T(8,128)(2,1)S(1)}, bf16[2,1,256,128]{3,2,1,0:T(8,128)(2,1)S(1)}, u32[]{:S(2)}, u32[]{:S(2)}) %collective-permute-start.3) | collective-permute-done | bytes 131104 | tf_op jit(solution)/shard_map/ppermute | solution.py:19
  30.6 3.7 %collective-permute-start.4 = (bf16[2,1,256,128]{3,2,1,0:T(8,128)(2,1)S(1)}, bf16[2,1,256,128]{3,2,1,0:T(8,128)(2,1)S(1)}, u32[]{:S(2)}, u32[]{:S(2)}) collective-permute-start(bf16[2,1,256,128]{3,2,1,0:T(8,128)(2,1)S(1)} %get-tuple-element.68), channel_id=1, source_target_pairs={{0,1},{1,2},{2,3},{3,4},{4,5},{5,6},{6,7},{7,8},{8,9},{9,10},{10,1... | collective-permute-start | bytes 393224 | tf_op jit(solution)/shard_map/ppermute | solution.py:18
  34.3 1.3 collective-permute-start.5
  36.3 5.2 %collective-permute-done.5 = bf16[2,1,256,128]{3,2,1,0:T(8,128)(2,1)S(1)} collective-permute-done((bf16[2,1,256,128]{3,2,1,0:T(8,128)(2,1)S(1)}, bf16[2,1,256,128]{3,2,1,0:T(8,128)(2,1)S(1)}, u32[]{:S(2)}, u32[]{:S(2)}) %collective-permute-start.5) | collective-permute-done | bytes 131104 | tf_op jit(solution)/shard_map/ppermute | solution.py:19
  44.0 1.6 add_convert_fusion
  46.7 9.9 %all-to-all-start = ((bf16[2,4,32,256]{3,1,0,2:T(4,128)(2,1)}), bf16[2,4,32,256]{3,1,0,2:T(4,128)(2,1)S(1)}, u32[]{:S(2)}, u32[]{:S(2)}) async-start(bf16[2,4,32,256]{3,1,0,2:T(4,128)(2,1)} %copy.77), calls=%async_computation | async-start | bytes 262144 | tf_op jit(solution)/shard_map/all_to_all | solution.py:149
  58.1 7.2 %all-to-all-done = bf16[2,4,32,256]{3,1,0,2:T(4,128)(2,1)S(1)} async-done(((bf16[2,4,32,256]{3,1,0,2:T(4,128)(2,1)}), bf16[2,4,32,256]{3,1,0,2:T(4,128)(2,1)S(1)}, u32[]{:S(2)}, u32[]{:S(2)}) %all-to-all-start) | async-done | bytes 131104 | tf_op jit(solution)/shard_map/all_to_all | solution.py:149
  65.5 3.7 %while.21 = (s32[]{:T(128)}, f32[16,4,4,256]{3,2,1,0:T(4,128)S(1)}, f32[16,4,4,256]{3,2,1,0:T(4,128)S(1)}, s32[]{:T(128)}) while((s32[]{:T(128)}, f32[16,4,4,256]{3,2,1,0:T(4,128)S(1)}, f32[16,4,4,256]{3,2,1,0:T(4,128)S(1)}, s32[]{:T(128)}) %tuple.51), condition=%wide.region_9.10_spmd, body=%wide.region_7.9_spmd.sunk | while | flops 192514 | bytes 360509 | solution.py:78
  69.4 12.4 %all_to_all.43 = bf16[16,4,4,256]{3,2,1,0:T(4,128)(2,1)S(1)} all-to-all(bf16[16,4,4,256]{3,2,1,0:T(4,128)(2,1)S(1)} %multiply_convert_fusion), channel_id=1, replica_groups=mesh['member'=8,'tile'=32] {'member'}, dimensions={0} | all-to-all | bytes 262144 | tf_op jit(solution)/shard_map/all_to_all | solution.py:167
  81.9 2.1 %fusion.13 = bf16[2,4,256,128]{3,2,1,0:T(8,128)(2,1)S(1)} fusion(f32[2,4,256,128]{3,2,1,0:T(8,128)} %get-tuple-element.79, bf16[2,4,32,256]{3,2,1,0:T(8,128)(2,1)S(1)} %all_to_all.34, bf16[128,32]{0,1:T(8,128)(2,1)S(1)} %copy-done.9), kind=kOutput, calls=%fused_computation.57 | convolution fusion | flops 22020096 | bytes 1712128 | tf_op jit(solution)/shard_map/mrvw,cv->mrwc/dot_general | solution.py:172
  87.0 1.0 convolution_bitcast_fusion.5
  87.9 1.0 convolution_bitcast_fusion.4
  90.6 1.9 %all_to_all.38 = f32[256,1,593]{2,1,0:T(1,128)} reshape(f32[151808]{0:T(1024)S(1)} %select_maximum_fusion.2) | data formatting | bytes 1214464 | tf_op jit(solution)/shard_map/all_to_all | solution.py:89
  92.5 13.2 %all-to-all-start.2 = ((f32[256,1,593]{2,1,0:T(1,128)}), f32[256,1,593]{2,1,0:T(1,128)S(1)}, u32[]{:S(2)}, u32[]{:S(2)}) async-start(f32[256,1,593]{2,1,0:T(1,128)} %all_to_all.38), calls=%async_computation.2 | async-start | bytes 1310720 | tf_op jit(solution)/shard_map/all_to_all | solution.py:89
  105.6 22.5 %all-to-all-done.2 = f32[256,1,593]{2,1,0:T(1,128)S(1)} async-done(((f32[256,1,593]{2,1,0:T(1,128)}), f32[256,1,593]{2,1,0:T(1,128)S(1)}, u32[]{:S(2)}, u32[]{:S(2)}) %all-to-all-start.2) | async-done | bytes 607264 | tf_op jit(solution)/shard_map/all_to_all | solution.py:89
  128.6 1.2 broadcast_in_dim.8
  129.8 6.8 %all-to-all-start.3 = ((f32[256,1,593]{2,1,0:T(1,128)}), f32[256,1,593]{2,1,0:T(1,128)S(1)}, u32[]{:S(2)}, u32[]{:S(2)}) async-start(f32[256,1,593]{2,1,0:T(1,128)} %broadcast_in_dim.8), calls=%async_computation.3 | async-start | bytes 1310720 | tf_op jit(solution)/shard_map/all_to_all | solution.py:91
  136.7 2.1 %while.20 = (s32[]{:T(128)}, f32[16,4,4,256]{3,2,1,0:T(4,128)S(1)}, f32[16,4,4,256]{3,2,1,0:T(4,128)S(1)}, s32[]{:T(128)}) while((s32[]{:T(128)}, f32[16,4,4,256]{3,2,1,0:T(4,128)S(1)}, f32[16,4,4,256]{3,2,1,0:T(4,128)S(1)}, s32[]{:T(128)}) %tuple.52), condition=%wide.region_5.6_spmd, body=%wide.region_3.5_spmd.sunk | while | flops 192514 | bytes 360509 | solution.py:70
  139.6 19.7 %all-to-all-done.3 = f32[256,1,593]{2,1,0:T(1,128)S(1)} async-done(((f32[256,1,593]{2,1,0:T(1,128)}), f32[256,1,593]{2,1,0:T(1,128)S(1)}, u32[]{:S(2)}, u32[]{:S(2)}) %all-to-all-start.3) | async-done | bytes 607264 | tf_op jit(solution)/shard_map/all_to_all | solution.py:91
  159.2 1.6 reduce.4
  160.9 1.7 %slice.276 = f32[4744,32]{1,0:T(8,128)S(1)} reshape(f32[256,593]{1,0:T(8,128)S(1)} %reduce.4) | data formatting | bytes 1214464 | tf_op jit(solution)/shard_map/slice | solution.py:95
  162.6 1.3 reshape.73
  163.8 1.9 %slice.303 = f32[147456]{0:T(1024)} slice(f32[151808]{0:T(1024)} %reshape.73), slice={[0:147456]} | slice | bytes 1179648 | tf_op jit(solution)/shard_map/slice | solution.py:95
  165.7 1.2 slice.305
  (194 shorter events, 25.9 us)
Async XLA Ops:
  0.6 7.4 %copy-start = (f32[16,256]{1,0:T(8,128)S(1)}, f32[16,256]{1,0:T(8,128)}, u32[]{:S(2)}) copy-start(f32[16,256]{1,0:T(8,128)} %param.20) | copy-start | bytes 49156
  0.6 13.7 %copy-start.5 = (bf16[3,3,32,128]{3,2,1,0:T(8,128)(2,1)S(1)}, bf16[3,3,32,128]{3,2,1,0:T(8,128)(2,1)}, u32[]{:S(2)}) copy-start(bf16[3,3,32,128]{3,2,1,0:T(8,128)(2,1)} %param.21) | copy-start | bytes 221188
  1.4 6.7 %collective-permute-start = (bf16[1,32,256]{2,1,0:T(8,128)(2,1)S(1)}, bf16[1,32,256]{2,1,0:T(8,128)(2,1)S(1)}, u32[]{:S(2)}, u32[]{:S(2)}) collective-permute-start(bf16[1,32,256]{2,1,0:T(8,128)(2,1)S(1)} %get-tuple-element.72), channel_id=1, source_target_pairs={{0,1},{1,2},{2,3},{3,4},{4,5},{5,6},{6,7},{7,8},{8,9},{9,10},{10,1... | collective-permute-start | bytes 49160 | tf_op jit(solution)/shard_map/ppermute | solution.py:18
  5.8 4.5 %collective-permute-start.1 = (bf16[1,32,256]{2,1,0:T(8,128)(2,1)S(1)}, bf16[1,32,256]{2,1,0:T(8,128)(2,1)S(1)}, u32[]{:S(2)}, u32[]{:S(2)}) collective-permute-start(bf16[1,32,256]{2,1,0:T(8,128)(2,1)S(1)} %get-tuple-element.73), channel_id=1, source_target_pairs={{1,0},{2,1},{3,2},{4,3},{5,4},{6,5},{7,6},{8,7},{9,8},{10,9},{11,1... | collective-permute-start | bytes 49160 | tf_op jit(solution)/shard_map/ppermute | solution.py:19
  13.3 1.6 copy-start.1
  16.4 11.3 %copy-start.4 = (bf16[3,3,128,128]{3,2,1,0:T(8,128)(2,1)S(1)}, bf16[3,3,128,128]{3,2,1,0:T(8,128)(2,1)}, u32[]{:S(2)}) copy-start(bf16[3,3,128,128]{3,2,1,0:T(8,128)(2,1)} %param.22) | copy-start | bytes 884740
  16.8 5.5 %collective-permute-start.2 = (bf16[2,1,256,128]{3,2,1,0:T(8,128)(2,1)S(1)}, bf16[2,1,256,128]{3,2,1,0:T(8,128)(2,1)S(1)}, u32[]{:S(2)}, u32[]{:S(2)}) collective-permute-start(bf16[2,1,256,128]{3,2,1,0:T(8,128)(2,1)S(1)} %get-tuple-element.70), channel_id=1, source_target_pairs={{0,1},{1,2},{2,3},{3,4},{4,5},{5,6},{6,7},{7,8},{8,9},{9,10},{10,1... | collective-permute-start | bytes 393224 | tf_op jit(solution)/shard_map/ppermute | solution.py:18
  20.4 7.0 %collective-permute-start.3 = (bf16[2,1,256,128]{3,2,1,0:T(8,128)(2,1)S(1)}, bf16[2,1,256,128]{3,2,1,0:T(8,128)(2,1)S(1)}, u32[]{:S(2)}, u32[]{:S(2)}) collective-permute-start(bf16[2,1,256,128]{3,2,1,0:T(8,128)(2,1)S(1)} %get-tuple-element.71), channel_id=1, source_target_pairs={{1,0},{2,1},{3,2},{4,3},{5,4},{6,5},{7,6},{8,7},{9,8},{10,9},{11,1... | collective-permute-start | bytes 393224 | tf_op jit(solution)/shard_map/ppermute | solution.py:19
  30.6 11.1 %copy-start.2 = (bf16[3,3,128,128]{3,2,1,0:T(8,128)(2,1)S(1)}, bf16[3,3,128,128]{3,2,1,0:T(8,128)(2,1)}, u32[]{:S(2)}) copy-start(bf16[3,3,128,128]{3,2,1,0:T(8,128)(2,1)} %param.23) | copy-start | bytes 884740
  30.6 5.6 %collective-permute-start.4 = (bf16[2,1,256,128]{3,2,1,0:T(8,128)(2,1)S(1)}, bf16[2,1,256,128]{3,2,1,0:T(8,128)(2,1)S(1)}, u32[]{:S(2)}, u32[]{:S(2)}) collective-permute-start(bf16[2,1,256,128]{3,2,1,0:T(8,128)(2,1)S(1)} %get-tuple-element.68), channel_id=1, source_target_pairs={{0,1},{1,2},{2,3},{3,4},{4,5},{5,6},{6,7},{7,8},{8,9},{9,10},{10,1... | collective-permute-start | bytes 393224 | tf_op jit(solution)/shard_map/ppermute | solution.py:18
  34.3 7.1 %collective-permute-start.5 = (bf16[2,1,256,128]{3,2,1,0:T(8,128)(2,1)S(1)}, bf16[2,1,256,128]{3,2,1,0:T(8,128)(2,1)S(1)}, u32[]{:S(2)}, u32[]{:S(2)}) collective-permute-start(bf16[2,1,256,128]{3,2,1,0:T(8,128)(2,1)S(1)} %get-tuple-element.69), channel_id=1, source_target_pairs={{1,0},{2,1},{3,2},{4,3},{5,4},{6,5},{7,6},{8,7},{9,8},{10,9},{11,1... | collective-permute-start | bytes 393224 | tf_op jit(solution)/shard_map/ppermute | solution.py:19
  44.0 1.6 copy-start.9
  44.0 1.6 copy-start.10
  46.7 18.6 %all-to-all-start = ((bf16[2,4,32,256]{3,1,0,2:T(4,128)(2,1)}), bf16[2,4,32,256]{3,1,0,2:T(4,128)(2,1)S(1)}, u32[]{:S(2)}, u32[]{:S(2)}) async-start(bf16[2,4,32,256]{3,1,0,2:T(4,128)(2,1)} %copy.77), calls=%async_computation | async-start | bytes 262144 | tf_op jit(solution)/shard_map/all_to_all | solution.py:149
  88.9 1.0 copy-start.3
  88.9 1.0 copy-start.8
  89.6 0.9 copy-start.6
  89.6 0.9 copy-start.7
  92.5 35.7 %all-to-all-start.2 = ((f32[256,1,593]{2,1,0:T(1,128)}), f32[256,1,593]{2,1,0:T(1,128)S(1)}, u32[]{:S(2)}, u32[]{:S(2)}) async-start(f32[256,1,593]{2,1,0:T(1,128)} %all_to_all.38), calls=%async_computation.2 | async-start | bytes 1310720 | tf_op jit(solution)/shard_map/all_to_all | solution.py:89
  129.8 29.4 %all-to-all-start.3 = ((f32[256,1,593]{2,1,0:T(1,128)}), f32[256,1,593]{2,1,0:T(1,128)S(1)}, u32[]{:S(2)}, u32[]{:S(2)}) async-start(f32[256,1,593]{2,1,0:T(1,128)} %broadcast_in_dim.8), calls=%async_computation.3 | async-start | bytes 1310720 | tf_op jit(solution)/shard_map/all_to_all | solution.py:91

commit v2 on v0

--- a/solution.py
+++ b/solution.py
@@ -76,6 +76,33 @@
         return jnp.sum(jnp.sign(member_index[None] - sample_group_predictions), axis=0)
 
     return lax.map(sign_single, probe)
+
+
+def all_reduce_sum(conv_grad, head_grad, bias_grad, axes):
+    devices = 1
+    for axis in axes:
+        devices *= lax.axis_size(axis)
+    lanes = conv_grad.shape[-1]
+    conv_rows = conv_grad.size // lanes
+    rows = conv_rows + head_grad.shape[1] + 1
+    per = -(-rows // devices)
+    bias_row = jnp.pad(bias_grad, (0, lanes - bias_grad.shape[0]))[None]
+    flat = jnp.concatenate(
+        [
+            conv_grad.reshape(conv_rows, lanes),
+            head_grad.T,
+            bias_row,
+            jnp.zeros((per * devices - rows, lanes), jnp.float32),
+        ]
+    ).reshape(devices, per, lanes)
+    pieces = lax.all_to_all(flat, axes, 0, 0, tiled=True)
+    own = jnp.sum(pieces, axis=0, keepdims=True)
+    spread = lax.all_to_all(jnp.broadcast_to(own, flat.shape), axes, 0, 0, tiled=True)
+    spread = spread.reshape(per * devices, lanes)
+    conv_sum = spread[:conv_rows].reshape(conv_grad.shape)
+    head_sum = spread[conv_rows : conv_rows + head_grad.shape[1]].T
+    bias_sum = spread[conv_rows + head_grad.shape[1], : bias_grad.shape[0]]
+    return conv_sum, head_sum, bias_sum
 
 
 def on_device(
@@ -168,9 +195,7 @@
             )
         rows_of.append(jnp.stack(cols_of))
     conv_grad = jnp.stack(rows_of)
-    conv_grad, head_grad, bias_grad = lax.psum(
-        (conv_grad, head_grad, bias_grad), ("member", "tile")
-    )
+    conv_grad, head_grad, bias_grad = all_reduce_sum(conv_grad, head_grad, bias_grad, ("member", "tile"))
     return (crps_map, conv_grad, head_grad, bias_grad)
 
 

time: 378 us -> 188 us (0.50)
  waiting for transfers between devices: 196 us -> 80 us
  blocking collectives: 82.8 us -> 12.4 us
  starting transfers between devices: 30.2 us -> 45.2 us
  between operations: 15.2 us -> 1.88 us
  local copies, waits for them, and re-layouts: 27.1 us -> 21 us
    psum x1 -> x0, waiting for transfers between devices: 175 us -> none  [on_device(): lax.psum((conv_grad, head_grad, bias_grad), ('member', 'tile'))]
    psum x1 -> x0, blocking collectives: 82.8 us -> none  [on_device(): lax.psum((conv_grad, head_grad, bias_grad), ('member', 'tile'))]
    all_to_all x1 -> x2, waiting for transfers between devices: 0.01 us -> 59.1 us  [the longest x1 31.1 us: all_reduce_sum(): pieces = lax.all_to_all(flat, axes, 0, 0, tiled=True)]
    all_to_all x1 -> x2, starting transfers between devices: 4.57 us -> 19.6 us  [the longest x1 13.2 us: all_reduce_sum(): pieces = lax.all_to_all(flat, axes, 0, 0, tiled=True)]
    all_to_all x0 -> x1, blocking collectives: none -> 12.4 us  [on_device(): lax.all_to_all(cot_share, 'member', split_axis=0, concat_axis=2, tiled=True)]
    dynamic_update_slice x32, local copies, waits for them, and re-layouts: 19.5 us -> 9.94 us  [abs_terms(): return lax.map(abs_single, probe)]
  transfers between devices with their start and end apart: 9 -> 9, of which waited for: 7 -> 8; matrix products, arithmetic and copies ran while one was open for 4% -> 2% of each run, Pallas kernels for 0% -> 0%
where the time goes in v2:
time: 188 us; the launch traced here: 187 us
  waiting for transfers between devices  80 us (43%)
  starting transfers between devices  45.2 us (24%)
  local copies, waits for them, and re-layouts  21 us (11%)
  matrix products  17.1 us (9%)
  blocking collectives  12.4 us (7%)
  other arithmetic  8.91 us (5%)
    all_to_all x1, waiting for transfers between devices, all_reduce_sum(): pieces = lax.all_to_all(flat, axes, 0, 0, tiled=True)  31.1 us
    all_to_all x1, waiting for transfers between devices, all_reduce_sum(): lax.all_to_all(jnp.broadcast_to(own, flat.shape), axes, 0, 0, tiled=True)  28.1 us
    all_to_all x1, starting transfers between devices, all_reduce_sum(): pieces = lax.all_to_all(flat, axes, 0, 0, tiled=True)  13.2 us
    ppermute x3, waiting for transfers between devices, extended(): after = lax.ppermute(first, axis, down)  12.4 us
    all_to_all x1, blocking collectives, on_device(): lax.all_to_all(cot_share, 'member', split_axis=0, concat_axis=2, tiled=True)  12.4 us
    ppermute x3, starting transfers between devices, extended(): before = lax.ppermute(last, axis, up)  11.7 us
    all_to_all x1, starting transfers between devices, on_device(): lax.all_to_all(sample_prediction, 'member', split_axis=2, concat_axis=0,...  9.96 us
    dynamic_update_slice x32, local copies, waits for them, and re-layouts, abs_terms(): return lax.map(abs_single, probe)  9.94 us
  transfers between devices with their start and end apart: 9, of which 8 were waited for; matrix products, arithmetic and copies ran while one was open for 2% of the time, Pallas kernels for 0%

profile of v2, /device:TPU:1, one launch (start us, length us, event | category | flops | bytes accessed | tf_op | source)
XLA Modules:
  0.0 186.9 jit_solution(7912693353618232044)
XLA Ops:
  0.7 0.8 fusion.156
  1.4 4.3 %collective-permute-start = (bf16[1,32,256]{2,1,0:T(8,128)(2,1)S(1)}, bf16[1,32,256]{2,1,0:T(8,128)(2,1)S(1)}, u32[]{:S(2)}, u32[]{:S(2)}) collective-permute-start(bf16[1,32,256]{2,1,0:T(8,128)(2,1)S(1)} %get-tuple-element.64), channel_id=1, source_target_pairs={{0,1},{1,2},{2,3},{3,4},{4,5},{5,6},{6,7},{7,8},{8,9},{9,10},{10,1... | collective-permute-start | bytes 49160 | tf_op jit(solution)/shard_map/ppermute | solution.py:18
  5.8 1.3 collective-permute-start.1
  7.1 0.9 fusion.142
  8.1 2.1 %collective-permute-done.1 = bf16[1,32,256]{2,1,0:T(8,128)(2,1)S(1)} collective-permute-done((bf16[1,32,256]{2,1,0:T(8,128)(2,1)S(1)}, bf16[1,32,256]{2,1,0:T(8,128)(2,1)S(1)}, u32[]{:S(2)}, u32[]{:S(2)}) %collective-permute-start.1) | collective-permute-done | bytes 16416 | tf_op jit(solution)/shard_map/ppermute | solution.py:19
  10.3 0.9 fusion.70
  11.2 1.0 fusion.78
  12.2 1.1 fusion.71
  16.4 3.7 %collective-permute-start.2 = (bf16[2,1,256,128]{3,2,1,0:T(8,128)(2,1)S(1)}, bf16[2,1,256,128]{3,2,1,0:T(8,128)(2,1)S(1)}, u32[]{:S(2)}, u32[]{:S(2)}) collective-permute-start(bf16[2,1,256,128]{3,2,1,0:T(8,128)(2,1)S(1)} %get-tuple-element.62), channel_id=1, source_target_pairs={{0,1},{1,2},{2,3},{3,4},{4,5},{5,6},{6,7},{7,8},{8,9},{9,10},{10,1... | collective-permute-start | bytes 393224 | tf_op jit(solution)/shard_map/ppermute | solution.py:18
  20.1 1.3 collective-permute-start.3
  22.0 5.1 %collective-permute-done.3 = bf16[2,1,256,128]{3,2,1,0:T(8,128)(2,1)S(1)} collective-permute-done((bf16[2,1,256,128]{3,2,1,0:T(8,128)(2,1)S(1)}, bf16[2,1,256,128]{3,2,1,0:T(8,128)(2,1)S(1)}, u32[]{:S(2)}, u32[]{:S(2)}) %collective-permute-start.3) | collective-permute-done | bytes 131104 | tf_op jit(solution)/shard_map/ppermute | solution.py:19
  30.3 3.7 %collective-permute-start.4 = (bf16[2,1,256,128]{3,2,1,0:T(8,128)(2,1)S(1)}, bf16[2,1,256,128]{3,2,1,0:T(8,128)(2,1)S(1)}, u32[]{:S(2)}, u32[]{:S(2)}) collective-permute-start(bf16[2,1,256,128]{3,2,1,0:T(8,128)(2,1)S(1)} %get-tuple-element.60), channel_id=1, source_target_pairs={{0,1},{1,2},{2,3},{3,4},{4,5},{5,6},{6,7},{7,8},{8,9},{9,10},{10,1... | collective-permute-start | bytes 393224 | tf_op jit(solution)/shard_map/ppermute | solution.py:18
  34.0 1.3 collective-permute-start.5
  35.9 5.2 %collective-permute-done.5 = bf16[2,1,256,128]{3,2,1,0:T(8,128)(2,1)S(1)} collective-permute-done((bf16[2,1,256,128]{3,2,1,0:T(8,128)(2,1)S(1)}, bf16[2,1,256,128]{3,2,1,0:T(8,128)(2,1)S(1)}, u32[]{:S(2)}, u32[]{:S(2)}) %collective-permute-start.5) | collective-permute-done | bytes 131104 | tf_op jit(solution)/shard_map/ppermute | solution.py:19
  44.7 0.8 copy.69
  45.4 10.0 %all-to-all-start = ((bf16[2,4,32,256]{3,1,0,2:T(4,128)(2,1)}), bf16[2,4,32,256]{3,1,0,2:T(4,128)(2,1)S(1)}, u32[]{:S(2)}, u32[]{:S(2)}) async-start(bf16[2,4,32,256]{3,1,0,2:T(4,128)(2,1)} %copy.69), calls=%async_computation | async-start | bytes 262144 | tf_op jit(solution)/shard_map/all_to_all | solution.py:157
  56.8 7.2 %all-to-all-done = bf16[2,4,32,256]{3,1,0,2:T(4,128)(2,1)S(1)} async-done(((bf16[2,4,32,256]{3,1,0,2:T(4,128)(2,1)}), bf16[2,4,32,256]{3,1,0,2:T(4,128)(2,1)S(1)}, u32[]{:S(2)}, u32[]{:S(2)}) %all-to-all-start) | async-done | bytes 131104 | tf_op jit(solution)/shard_map/all_to_all | solution.py:157
  64.1 0.8 broadcast.100.clone.1
  64.9 12.7 %while.21 = (s32[]{:T(128)}, f32[16,4,4,256]{3,2,1,0:T(4,128)}, f32[16,4,4,256]{3,2,1,0:T(4,128)S(1)}, s32[]{:T(128)}) while((s32[]{:T(128)}, f32[16,4,4,256]{3,2,1,0:T(4,128)}, f32[16,4,4,256]{3,2,1,0:T(4,128)S(1)}, s32[]{:T(128)}) %tuple.49), condition=%wide.region_9.10_spmd, body=%wide.region_7.9_spmd.sunk | while | flops 192514 | bytes 361017 | solution.py:78
  77.6 1.2 multiply_convert_fusion
  78.8 12.4 %all_to_all.37 = bf16[16,4,4,256]{3,2,1,0:T(4,128)(2,1)S(1)} all-to-all(bf16[16,4,4,256]{3,2,1,0:T(4,128)(2,1)S(1)} %multiply_convert_fusion), channel_id=1, replica_groups=mesh['member'=8,'tile'=32] {'member'}, dimensions={0} | all-to-all | bytes 262144 | tf_op jit(solution)/shard_map/all_to_all | solution.py:175
  91.9 1.6 all_to_all.30
  93.5 1.1 convolution_bitcast_fusion.10
  94.6 1.8 fusion.13
  100.6 1.1 reshape.59
  101.7 13.2 %all-to-all-start.2 = ((f32[256,5,128]{2,1,0:T(8,128)}), f32[256,5,128]{2,1,0:T(8,128)S(1)}, u32[]{:S(2)}, u32[]{:S(2)}) async-start(f32[256,5,128]{2,1,0:T(8,128)} %reshape.59), calls=%async_computation.2 | async-start | bytes 2097152 | tf_op jit(solution)/shard_map/all_to_all | solution.py:98
  114.9 31.1 %all-to-all-done.2 = f32[256,5,128]{2,1,0:T(8,128)S(1)} async-done(((f32[256,5,128]{2,1,0:T(8,128)}), f32[256,5,128]{2,1,0:T(8,128)S(1)}, u32[]{:S(2)}, u32[]{:S(2)}) %all-to-all-start.2) | async-done | bytes 655392 | tf_op jit(solution)/shard_map/all_to_all | solution.py:98
  146.2 1.0 broadcast_in_dim.17
  147.3 6.5 %all-to-all-start.3 = ((f32[256,5,128]{2,1,0:T(8,128)}), f32[256,5,128]{2,1,0:T(8,128)S(1)}, u32[]{:S(2)}, u32[]{:S(2)}) async-start(f32[256,5,128]{2,1,0:T(8,128)} %broadcast_in_dim.17), calls=%async_computation.3 | async-start | bytes 2097152 | tf_op jit(solution)/shard_map/all_to_all | solution.py:100
  153.8 2.1 %while.20 = (s32[]{:T(128)}, f32[16,4,4,256]{3,2,1,0:T(4,128)S(1)}, f32[16,4,4,256]{3,2,1,0:T(4,128)S(1)}, s32[]{:T(128)}) while((s32[]{:T(128)}, f32[16,4,4,256]{3,2,1,0:T(4,128)S(1)}, f32[16,4,4,256]{3,2,1,0:T(4,128)S(1)}, s32[]{:T(128)}) %tuple.50), condition=%wide.region_5.6_spmd, body=%wide.region_3.5_spmd.sunk | while | flops 192514 | bytes 360509 | solution.py:70
  156.7 28.1 %all-to-all-done.3 = f32[256,5,128]{2,1,0:T(8,128)S(1)} async-done(((f32[256,5,128]{2,1,0:T(8,128)}), f32[256,5,128]{2,1,0:T(8,128)S(1)}, u32[]{:S(2)}, u32[]{:S(2)}) %all-to-all-start.3) | async-done | bytes 655392 | tf_op jit(solution)/shard_map/all_to_all | solution.py:100
  184.9 0.9 slice.299
  (192 shorter events, 33.4 us)
Async XLA Ops:
  0.6 7.4 %copy-start = (f32[16,256]{1,0:T(8,128)S(1)}, f32[16,256]{1,0:T(8,128)}, u32[]{:S(2)}) copy-start(f32[16,256]{1,0:T(8,128)} %param.20) | copy-start | bytes 49156
  0.6 12.6 %copy-start.8 = (bf16[3,3,32,128]{3,2,1,0:T(8,128)(2,1)S(1)}, bf16[3,3,32,128]{3,2,1,0:T(8,128)(2,1)}, u32[]{:S(2)}) copy-start(bf16[3,3,32,128]{3,2,1,0:T(8,128)(2,1)} %param.21) | copy-start | bytes 221188
  1.4 6.7 %collective-permute-start = (bf16[1,32,256]{2,1,0:T(8,128)(2,1)S(1)}, bf16[1,32,256]{2,1,0:T(8,128)(2,1)S(1)}, u32[]{:S(2)}, u32[]{:S(2)}) collective-permute-start(bf16[1,32,256]{2,1,0:T(8,128)(2,1)S(1)} %get-tuple-element.64), channel_id=1, source_target_pairs={{0,1},{1,2},{2,3},{3,4},{4,5},{5,6},{6,7},{7,8},{8,9},{9,10},{10,1... | collective-permute-start | bytes 49160 | tf_op jit(solution)/shard_map/ppermute | solution.py:18
  5.8 4.5 %collective-permute-start.1 = (bf16[1,32,256]{2,1,0:T(8,128)(2,1)S(1)}, bf16[1,32,256]{2,1,0:T(8,128)(2,1)S(1)}, u32[]{:S(2)}, u32[]{:S(2)}) collective-permute-start(bf16[1,32,256]{2,1,0:T(8,128)(2,1)S(1)} %get-tuple-element.65), channel_id=1, source_target_pairs={{1,0},{2,1},{3,2},{4,3},{5,4},{6,5},{7,6},{8,7},{9,8},{10,9},{11,1... | collective-permute-start | bytes 49160 | tf_op jit(solution)/shard_map/ppermute | solution.py:19
  13.6 0.8 copy-start.1
  16.3 11.0 %copy-start.7 = (bf16[3,3,128,128]{3,2,1,0:T(8,128)(2,1)S(1)}, bf16[3,3,128,128]{3,2,1,0:T(8,128)(2,1)}, u32[]{:S(2)}) copy-start(bf16[3,3,128,128]{3,2,1,0:T(8,128)(2,1)} %param.22) | copy-start | bytes 884740
  16.4 5.6 %collective-permute-start.2 = (bf16[2,1,256,128]{3,2,1,0:T(8,128)(2,1)S(1)}, bf16[2,1,256,128]{3,2,1,0:T(8,128)(2,1)S(1)}, u32[]{:S(2)}, u32[]{:S(2)}) collective-permute-start(bf16[2,1,256,128]{3,2,1,0:T(8,128)(2,1)S(1)} %get-tuple-element.62), channel_id=1, source_target_pairs={{0,1},{1,2},{2,3},{3,4},{4,5},{5,6},{6,7},{7,8},{8,9},{9,10},{10,1... | collective-permute-start | bytes 393224 | tf_op jit(solution)/shard_map/ppermute | solution.py:18
  20.1 7.0 %collective-permute-start.3 = (bf16[2,1,256,128]{3,2,1,0:T(8,128)(2,1)S(1)}, bf16[2,1,256,128]{3,2,1,0:T(8,128)(2,1)S(1)}, u32[]{:S(2)}, u32[]{:S(2)}) collective-permute-start(bf16[2,1,256,128]{3,2,1,0:T(8,128)(2,1)S(1)} %get-tuple-element.63), channel_id=1, source_target_pairs={{1,0},{2,1},{3,2},{4,3},{5,4},{6,5},{7,6},{8,7},{9,8},{10,9},{11,1... | collective-permute-start | bytes 393224 | tf_op jit(solution)/shard_map/ppermute | solution.py:19
  30.3 11.1 %copy-start.6 = (bf16[3,3,128,128]{3,2,1,0:T(8,128)(2,1)S(1)}, bf16[3,3,128,128]{3,2,1,0:T(8,128)(2,1)}, u32[]{:S(2)}) copy-start(bf16[3,3,128,128]{3,2,1,0:T(8,128)(2,1)} %param.23) | copy-start | bytes 884740
  30.3 5.6 %collective-permute-start.4 = (bf16[2,1,256,128]{3,2,1,0:T(8,128)(2,1)S(1)}, bf16[2,1,256,128]{3,2,1,0:T(8,128)(2,1)S(1)}, u32[]{:S(2)}, u32[]{:S(2)}) collective-permute-start(bf16[2,1,256,128]{3,2,1,0:T(8,128)(2,1)S(1)} %get-tuple-element.60), channel_id=1, source_target_pairs={{0,1},{1,2},{2,3},{3,4},{4,5},{5,6},{6,7},{7,8},{8,9},{9,10},{10,1... | collective-permute-start | bytes 393224 | tf_op jit(solution)/shard_map/ppermute | solution.py:18
  34.0 7.1 %collective-permute-start.5 = (bf16[2,1,256,128]{3,2,1,0:T(8,128)(2,1)S(1)}, bf16[2,1,256,128]{3,2,1,0:T(8,128)(2,1)S(1)}, u32[]{:S(2)}, u32[]{:S(2)}) collective-permute-start(bf16[2,1,256,128]{3,2,1,0:T(8,128)(2,1)S(1)} %get-tuple-element.61), channel_id=1, source_target_pairs={{1,0},{2,1},{3,2},{4,3},{5,4},{6,5},{7,6},{8,7},{9,8},{10,9},{11,1... | collective-permute-start | bytes 393224 | tf_op jit(solution)/shard_map/ppermute | solution.py:19
  35.9 5.7 %copy-start.4 = (bf16[2,1,256,128]{3,2,1,0:T(8,128)(2,1)}, bf16[2,1,256,128]{3,2,1,0:T(8,128)(2,1)S(1)}, u32[]{:S(2)}) copy-start(bf16[2,1,256,128]{3,2,1,0:T(8,128)(2,1)S(1)} %collective-permute-done.4) | copy-start | bytes 393220
  41.1 2.6 %copy-start.2 = (bf16[2,1,256,128]{3,2,1,0:T(8,128)(2,1)}, bf16[2,1,256,128]{3,2,1,0:T(8,128)(2,1)S(1)}, u32[]{:S(2)}) copy-start(bf16[2,1,256,128]{3,2,1,0:T(8,128)(2,1)S(1)} %collective-permute-done.5) | copy-start | bytes 393220
  43.7 0.7 copy-start.9
  43.7 0.7 copy-start.10
  45.4 18.6 %all-to-all-start = ((bf16[2,4,32,256]{3,1,0,2:T(4,128)(2,1)}), bf16[2,4,32,256]{3,1,0,2:T(4,128)(2,1)S(1)}, u32[]{:S(2)}, u32[]{:S(2)}) async-start(bf16[2,4,32,256]{3,1,0,2:T(4,128)(2,1)} %copy.69), calls=%async_computation | async-start | bytes 262144 | tf_op jit(solution)/shard_map/all_to_all | solution.py:157
  98.5 0.9 copy-start.3
  98.8 0.9 copy-start.5
  101.7 44.3 %all-to-all-start.2 = ((f32[256,5,128]{2,1,0:T(8,128)}), f32[256,5,128]{2,1,0:T(8,128)S(1)}, u32[]{:S(2)}, u32[]{:S(2)}) async-start(f32[256,5,128]{2,1,0:T(8,128)} %reshape.59), calls=%async_computation.2 | async-start | bytes 2097152 | tf_op jit(solution)/shard_map/all_to_all | solution.py:98
  147.3 37.5 %all-to-all-start.3 = ((f32[256,5,128]{2,1,0:T(8,128)}), f32[256,5,128]{2,1,0:T(8,128)S(1)}, u32[]{:S(2)}, u32[]{:S(2)}) async-start(f32[256,5,128]{2,1,0:T(8,128)} %broadcast_in_dim.17), calls=%async_computation.3 | async-start | bytes 2097152 | tf_op jit(solution)/shard_map/all_to_all | solution.py:100

commit v3 on v1

--- a/solution.py
+++ b/solution.py
@@ -124,11 +124,14 @@
     random_latent_gain = jnp.dot(noise_vec, cond_weight, precision=lax.Precision.HIGHEST)
     cond_scale = random_latent_gain[:, :channels]
     cond_shift = random_latent_gain[:, channels:]
-    input_padded = extended(upsampled_coarse, (("tile", 0),), 1)
-    first_hidden = condition(input_conv(input_padded, conv_in), cond_scale, cond_shift)
-    first_padded = extended(first_hidden, (("tile", 1),), 1)
-    latent_layer_two = jax.nn.gelu(feature_conv(first_padded, conv_mid)).astype(jnp.bfloat16)
-    second_padded = extended(latent_layer_two, (("tile", 1),), 1)
+    input_padded = extended(upsampled_coarse, (("tile", 0),), 3)
+    band_at = tile_at * row_count + jnp.arange(-2, row_count + 2, dtype=jnp.int32)
+    inside = ((band_at >= 0) & (band_at < band_rows))[None, :, None, None]
+    first_wide = condition(input_conv(input_padded, conv_in), cond_scale, cond_shift)
+    first_wide = jnp.where(inside, first_wide, jnp.zeros_like(first_wide))
+    first_hidden = first_wide[:, 2 : 2 + row_count]
+    second_padded = jax.nn.gelu(feature_conv(first_wide, conv_mid)).astype(jnp.bfloat16)
+    second_padded = jnp.where(inside[:, 1:-1], second_padded, jnp.zeros_like(second_padded))
     final_linear_response = feature_conv(second_padded, conv_out)
     latent_layer_three = (
         first_hidden.astype(jnp.float32) + jax.nn.gelu(final_linear_response)

time: 169 us -> 140 us (0.83)
  waiting for transfers between devices: 63 us -> 50.6 us
  starting transfers between devices: 45.4 us -> 33.8 us
  matrix products: 20.8 us -> 17 us
    ppermute x3 -> x1, waiting for transfers between devices: 12.4 us -> 1.43 us  [extended(): after = lax.ppermute(first, axis, down)]
    ppermute x3 -> x1, starting transfers between devices: 11.6 us -> 4.35 us  [extended(): before = lax.ppermute(last, axis, up)]
    ppermute x3 -> x1, starting transfers between devices: 3.88 us -> 1.29 us  [extended(): after = lax.ppermute(first, axis, down)]
    dot_general x9, matrix products: 5.62 us -> 3.1 us  [on_device(): jnp.einsum('mrwc,mrwd->cd', second_wide[:, i:i + row_count, j:j + col_cou...]
  transfers between devices with their start and end apart: 9 -> 5, of which waited for: 8 -> 4; matrix products, arithmetic and copies ran while one was open for 3% -> 4% of each run, Pallas kernels for 0% -> 0%
where the time goes in v3:
time: 140 us
  waiting for transfers between devices  50.6 us (36%)
  starting transfers between devices  33.8 us (24%)
  matrix products  17 us (12%)
  local copies, waits for them, and re-layouts  13.6 us (10%)
  blocking collectives  12 us (9%)
  other arithmetic  9.99 us (7%)
  between operations  1.75 us (1%)
    all_to_all x1, waiting for transfers between devices, all_reduce_sum(): pieces = lax.all_to_all(flat, axes, 0, 0, tiled=True)  22.5 us
    all_to_all x1, waiting for transfers between devices, all_reduce_sum(): lax.all_to_all(jnp.broadcast_to(own, (devices, width)), axes, 0, 0, tiled...  19.7 us
    all_to_all x1, blocking collectives, on_device(): lax.all_to_all(cot_share, 'member', split_axis=0, concat_axis=2, tiled=True)  12 us
    all_to_all x1, starting transfers between devices, all_reduce_sum(): pieces = lax.all_to_all(flat, axes, 0, 0, tiled=True)  11.8 us
    all_to_all x1, starting transfers between devices, on_device(): lax.all_to_all(sample_prediction, 'member', split_axis=2, concat_axis=0,...  9.65 us
    dot_general x18, matrix products, feature_conv(): jnp.einsum('mrwc,cd->mrwd', wide[:, i:i + out_rows, j:j + col_count], ker...  7.01 us
    all_to_all x1, waiting for transfers between devices, on_device(): lax.all_to_all(sample_prediction, 'member', split_axis=2, concat_axis=0,...  6.9 us
    all_to_all x1, starting transfers between devices, all_reduce_sum(): lax.all_to_all(jnp.broadcast_to(own, (devices, width)), axes, 0, 0, tiled...  6.72 us
  transfers between devices with their start and end apart: 5, of which 4 were waited for; matrix products, arithmetic and copies ran while one was open for 4% of the time, Pallas kernels for 0%

profile of v3, /device:TPU:1, one launch (start us, length us, event | category | flops | bytes accessed | tf_op | source)
XLA Modules:
  0.0 139.7 jit_solution(4340139379712008977)
XLA Ops:
  0.7 0.9 fusion.174
  1.5 4.3 %collective-permute-start = (bf16[3,32,256]{2,1,0:T(8,128)(2,1)S(1)}, bf16[3,32,256]{2,1,0:T(8,128)(2,1)S(1)}, u32[]{:S(2)}, u32[]{:S(2)}) collective-permute-start(bf16[3,32,256]{2,1,0:T(8,128)(2,1)S(1)} %get-tuple-element.71), channel_id=1, source_target_pairs={{0,1},{1,2},{2,3},{3,4},{4,5},{5,6},{6,7},{7,8},{8,9},{9,10},{10,1... | collective-permute-start | bytes 147464 | tf_op jit(solution)/shard_map/ppermute | solution.py:18
  5.9 1.3 collective-permute-start.1
  7.2 0.9 fusion.145
  8.4 0.9 fusion.173
  9.3 1.4 %collective-permute-done.1 = bf16[3,32,256]{2,1,0:T(8,128)(2,1)S(1)} collective-permute-done((bf16[3,32,256]{2,1,0:T(8,128)(2,1)S(1)}, bf16[3,32,256]{2,1,0:T(8,128)(2,1)S(1)}, u32[]{:S(2)}, u32[]{:S(2)}) %collective-permute-start.1) | collective-permute-done | bytes 49184 | tf_op jit(solution)/shard_map/ppermute | solution.py:19
  10.7 1.0 fusion.123
  14.4 0.8 fusion.175
  15.8 0.9 fusion.32
  19.7 1.1 fusion.31
  23.2 0.6 add_convert_fusion
  24.2 0.8 copy.77
  25.0 9.7 %all-to-all-start = ((bf16[2,4,32,256]{3,1,0,2:T(4,128)(2,1)}), bf16[2,4,32,256]{3,1,0,2:T(4,128)(2,1)S(1)}, u32[]{:S(2)}, u32[]{:S(2)}) async-start(bf16[2,4,32,256]{3,1,0,2:T(4,128)(2,1)} %copy.77), calls=%async_computation | async-start | bytes 262144 | tf_op jit(solution)/shard_map/all_to_all | solution.py:152
  35.3 0.7 dynamic-slice_convert_fusion
  36.0 6.9 %all-to-all-done = bf16[2,4,32,256]{3,1,0,2:T(4,128)(2,1)S(1)} async-done(((bf16[2,4,32,256]{3,1,0,2:T(4,128)(2,1)}), bf16[2,4,32,256]{3,1,0,2:T(4,128)(2,1)S(1)}, u32[]{:S(2)}, u32[]{:S(2)}) %all-to-all-start) | async-done | bytes 131104 | tf_op jit(solution)/shard_map/all_to_all | solution.py:152
  43.1 3.7 %while.21 = (s32[]{:T(128)}, f32[16,4,4,256]{3,2,1,0:T(4,128)S(1)}, f32[16,4,4,256]{3,2,1,0:T(4,128)S(1)}, s32[]{:T(128)}) while((s32[]{:T(128)}, f32[16,4,4,256]{3,2,1,0:T(4,128)S(1)}, f32[16,4,4,256]{3,2,1,0:T(4,128)S(1)}, s32[]{:T(128)}) %tuple.50), condition=%wide.region_9.10_spmd, body=%wide.region_7.9_spmd.sunk | while | flops 192514 | bytes 360509 | solution.py:78
  47.1 12.0 %all_to_all.43 = bf16[16,4,4,256]{3,2,1,0:T(4,128)(2,1)S(1)} all-to-all(bf16[16,4,4,256]{3,2,1,0:T(4,128)(2,1)S(1)} %multiply_convert_fusion), channel_id=1, replica_groups=mesh['member'=8,'tile'=32] {'member'}, dimensions={0} | all-to-all | bytes 262144 | tf_op jit(solution)/shard_map/all_to_all | solution.py:170
  59.2 0.9 fusion.39
  64.0 1.9 %all_to_all.38 = f32[256,1,593]{2,1,0:T(1,128)} reshape(f32[151808]{0:T(1024)S(1)} %select_maximum_fusion) | data formatting | bytes 1214464 | tf_op jit(solution)/shard_map/all_to_all | solution.py:89
  65.9 11.8 %all-to-all-start.2 = ((f32[256,1,593]{2,1,0:T(1,128)}), f32[256,1,593]{2,1,0:T(1,128)S(1)}, u32[]{:S(2)}, u32[]{:S(2)}) async-start(f32[256,1,593]{2,1,0:T(1,128)} %all_to_all.38), calls=%async_computation.2 | async-start | bytes 1310720 | tf_op jit(solution)/shard_map/all_to_all | solution.py:89
  77.7 22.5 %all-to-all-done.2 = f32[256,1,593]{2,1,0:T(1,128)S(1)} async-done(((f32[256,1,593]{2,1,0:T(1,128)}), f32[256,1,593]{2,1,0:T(1,128)S(1)}, u32[]{:S(2)}, u32[]{:S(2)}) %all-to-all-start.2) | async-done | bytes 607264 | tf_op jit(solution)/shard_map/all_to_all | solution.py:89
  100.8 1.2 broadcast_in_dim.57
  101.9 6.7 %all-to-all-start.3 = ((f32[256,1,593]{2,1,0:T(1,128)}), f32[256,1,593]{2,1,0:T(1,128)S(1)}, u32[]{:S(2)}, u32[]{:S(2)}) async-start(f32[256,1,593]{2,1,0:T(1,128)} %broadcast_in_dim.57), calls=%async_computation.3 | async-start | bytes 1310720 | tf_op jit(solution)/shard_map/all_to_all | solution.py:91
  108.7 2.1 %while.20 = (s32[]{:T(128)}, f32[16,4,4,256]{3,2,1,0:T(4,128)S(1)}, f32[16,4,4,256]{3,2,1,0:T(4,128)S(1)}, s32[]{:T(128)}) while((s32[]{:T(128)}, f32[16,4,4,256]{3,2,1,0:T(4,128)S(1)}, f32[16,4,4,256]{3,2,1,0:T(4,128)S(1)}, s32[]{:T(128)}) %tuple.51), condition=%wide.region_5.6_spmd, body=%wide.region_3.5_spmd.sunk | while | flops 192514 | bytes 360509 | solution.py:70
  111.0 0.6 copy.93
  111.7 19.7 %all-to-all-done.3 = f32[256,1,593]{2,1,0:T(1,128)S(1)} async-done(((f32[256,1,593]{2,1,0:T(1,128)}), f32[256,1,593]{2,1,0:T(1,128)S(1)}, u32[]{:S(2)}, u32[]{:S(2)}) %all-to-all-start.3) | async-done | bytes 607264 | tf_op jit(solution)/shard_map/all_to_all | solution.py:91
  131.3 1.6 %reduce.4 = f32[256,593]{1,0:T(8,128)S(1)} reduce(f32[256,1,593]{2,1,0:T(1,128)S(1)} %all-to-all-done.3, f32[]{:T(128)} %constant.109), dimensions={1}, to_apply=%all_to_all.37.reduce_sub_computation | reduce | bytes 1214468 | tf_op jit(solution)/shard_map/all_to_all | solution.py:91
  133.0 1.7 %slice.271 = f32[4744,32]{1,0:T(8,128)S(1)} reshape(f32[256,593]{1,0:T(8,128)S(1)} %reduce.4) | data formatting | bytes 1214464 | tf_op jit(solution)/shard_map/slice | solution.py:95
  134.7 1.3 reshape.93
  135.9 1.9 %slice.277 = f32[147456]{0:T(1024)} slice(f32[151808]{0:T(1024)} %reshape.93), slice={[0:147456]} | slice | bytes 1179648 | tf_op jit(solution)/shard_map/slice | solution.py:95
  137.8 1.2 slice.279
  139.0 0.7 copy.94
  (176 shorter events, 19.1 us)
Async XLA Ops:
  0.6 7.5 %copy-start = (f32[16,256]{1,0:T(8,128)S(1)}, f32[16,256]{1,0:T(8,128)}, u32[]{:S(2)}) copy-start(f32[16,256]{1,0:T(8,128)} %param.20) | copy-start | bytes 49156
  0.6 11.1 %copy-start.3 = (bf16[3,3,32,128]{3,2,1,0:T(8,128)(2,1)S(1)}, bf16[3,3,32,128]{3,2,1,0:T(8,128)(2,1)}, u32[]{:S(2)}) copy-start(bf16[3,3,32,128]{3,2,1,0:T(8,128)(2,1)} %param.21) | copy-start | bytes 221188
  1.5 6.8 %collective-permute-start = (bf16[3,32,256]{2,1,0:T(8,128)(2,1)S(1)}, bf16[3,32,256]{2,1,0:T(8,128)(2,1)S(1)}, u32[]{:S(2)}, u32[]{:S(2)}) collective-permute-start(bf16[3,32,256]{2,1,0:T(8,128)(2,1)S(1)} %get-tuple-element.71), channel_id=1, source_target_pairs={{0,1},{1,2},{2,3},{3,4},{4,5},{5,6},{6,7},{7,8},{8,9},{9,10},{10,1... | collective-permute-start | bytes 147464 | tf_op jit(solution)/shard_map/ppermute | solution.py:18
  5.9 4.8 %collective-permute-start.1 = (bf16[3,32,256]{2,1,0:T(8,128)(2,1)S(1)}, bf16[3,32,256]{2,1,0:T(8,128)(2,1)S(1)}, u32[]{:S(2)}, u32[]{:S(2)}) collective-permute-start(bf16[3,32,256]{2,1,0:T(8,128)(2,1)S(1)} %get-tuple-element.70), channel_id=1, source_target_pairs={{1,0},{2,1},{3,2},{4,3},{5,4},{6,5},{7,6},{8,7},{9,8},{10,9},{11,1... | collective-permute-start | bytes 147464 | tf_op jit(solution)/shard_map/ppermute | solution.py:19
  15.8 1.0 copy-start.2
  19.7 1.1 copy-start.1
  23.2 0.7 copy-start.4
  23.2 0.7 copy-start.5
  25.0 18.0 %all-to-all-start = ((bf16[2,4,32,256]{3,1,0,2:T(4,128)(2,1)}), bf16[2,4,32,256]{3,1,0,2:T(4,128)(2,1)S(1)}, u32[]{:S(2)}, u32[]{:S(2)}) async-start(bf16[2,4,32,256]{3,1,0,2:T(4,128)(2,1)} %copy.77), calls=%async_computation | async-start | bytes 262144 | tf_op jit(solution)/shard_map/all_to_all | solution.py:152
  65.9 34.4 %all-to-all-start.2 = ((f32[256,1,593]{2,1,0:T(1,128)}), f32[256,1,593]{2,1,0:T(1,128)S(1)}, u32[]{:S(2)}, u32[]{:S(2)}) async-start(f32[256,1,593]{2,1,0:T(1,128)} %all_to_all.38), calls=%async_computation.2 | async-start | bytes 1310720 | tf_op jit(solution)/shard_map/all_to_all | solution.py:89
  101.9 29.4 %all-to-all-start.3 = ((f32[256,1,593]{2,1,0:T(1,128)}), f32[256,1,593]{2,1,0:T(1,128)S(1)}, u32[]{:S(2)}, u32[]{:S(2)}) async-start(f32[256,1,593]{2,1,0:T(1,128)} %broadcast_in_dim.57), calls=%async_computation.3 | async-start | bytes 1310720 | tf_op jit(solution)/shard_map/all_to_all | solution.py:91

commit v4 on v3

--- a/solution.py
+++ b/solution.py
@@ -84,7 +84,7 @@
         devices *= lax.axis_size(axis)
     flat = jnp.concatenate([p.reshape(-1) for p in parts])
     total = flat.shape[0]
-    width = -(-total // devices)
+    width = -(-total // (devices * 128)) * 128
     flat = jnp.pad(flat, (0, width * devices - total)).reshape(devices, width)
     pieces = lax.all_to_all(flat, axes, 0, 0, tiled=True)
     own = jnp.sum(pieces, axis=0, keepdims=True)
@@ -155,8 +155,9 @@
     sample_group_predictions = collected_members.astype(jnp.float32)
     member_count = sample_group_predictions.shape[0]
     truth = lax.dynamic_slice_in_dim(target, var_start, var_share, 1).astype(jnp.float32)
-    abs_sums = abs_terms(sample_group_predictions, sample_group_predictions)
-    sign_sums = sign_terms(sample_group_predictions, sample_group_predictions)
+    pair_differ = sample_group_predictions[:, None] - sample_group_predictions[None, :]
+    abs_sums = jnp.sum(jnp.abs(pair_differ), axis=1)
+    sign_sums = jnp.sum(jnp.sign(pair_differ), axis=1)
     crps_map = jnp.mean(jnp.abs(sample_group_predictions - truth[None]), axis=0) - jnp.sum(
         abs_sums, axis=0
     ) / (2 * member_count * (member_count - 1))
@@ -190,7 +191,8 @@
             )
         rows_of.append(jnp.stack(cols_of))
     conv_grad = jnp.stack(rows_of)
-    conv_grad, head_grad, bias_grad = all_reduce_sum((conv_grad, head_grad, bias_grad), ("member", "tile"))
+    conv_grad, head_grad_t, bias_grad = all_reduce_sum((conv_grad, head_grad.T, bias_grad), ("member", "tile"))
+    head_grad = head_grad_t.T
     return (crps_map, conv_grad, head_grad, bias_grad)
 
 

time: 140 us -> 130 us (0.929)
  blocking collectives: 12 us -> 46.2 us
  waiting for transfers between devices: 50.6 us -> 30.3 us
  starting transfers between devices: 33.8 us -> 22 us
  local copies, waits for them, and re-layouts: 13.6 us -> 6.36 us
  other arithmetic: 9.99 us -> 6.31 us
    all_to_all x0 -> x1, blocking collectives: none -> 34.2 us  [all_reduce_sum(): pieces = lax.all_to_all(flat, axes, 0, 0, tiled=True)]
    all_to_all x1 -> x0, waiting for transfers between devices: 22.5 us -> none  [all_reduce_sum(): pieces = lax.all_to_all(flat, axes, 0, 0, tiled=True)]
    all_to_all x1 -> x0, starting transfers between devices: 11.8 us -> none  [all_reduce_sum(): pieces = lax.all_to_all(flat, axes, 0, 0, tiled=True)]
    slice x4 -> x2, local copies, waits for them, and re-layouts: 4.78 us -> 1.36 us  [all_reduce_sum(): out.append(spread[at:at + p.size].reshape(p.shape))]
    all_to_all x1, waiting for transfers between devices: 19.7 us -> 21.9 us  [all_reduce_sum(): lax.all_to_all(jnp.broadcast_to(own, (devices, width)), axes, 0, 0, tiled...]
    reduce_sum x33 -> x1, other arithmetic: 4.34 us -> 2.28 us  [on_device(): sign_sums = jnp.sum(jnp.sign(pair_differ), axis=1)]
    all_to_all x1 -> x0, local copies, waits for them, and re-layouts: 1.87 us -> none  [all_reduce_sum(): pieces = lax.all_to_all(flat, axes, 0, 0, tiled=True)]
    all_to_all x1 -> x0, other arithmetic: 1.62 us -> none  [all_reduce_sum(): lax.all_to_all(jnp.broadcast_to(own, (devices, width)), axes, 0, 0, tiled...]
  transfers between devices with their start and end apart: 5 -> 4, of which waited for: 4 -> 3; matrix products, arithmetic and copies ran while one was open for 4% -> 3% of each run, Pallas kernels for 0% -> 0%
where the time goes in v4:
time: 130 us
  blocking collectives  46.2 us (36%)
  waiting for transfers between devices  30.3 us (23%)
  starting transfers between devices  22 us (17%)
  matrix products  16.9 us (13%)
  local copies, waits for them, and re-layouts  6.36 us (5%)
  other arithmetic  6.31 us (5%)
  between operations  1.71 us (1%)
    all_to_all x1, blocking collectives, all_reduce_sum(): pieces = lax.all_to_all(flat, axes, 0, 0, tiled=True)  34.2 us
    all_to_all x1, waiting for transfers between devices, all_reduce_sum(): lax.all_to_all(jnp.broadcast_to(own, (devices, width)), axes, 0, 0, tiled...  21.9 us
    all_to_all x1, blocking collectives, on_device(): lax.all_to_all(cot_share, 'member', split_axis=0, concat_axis=2, tiled=True)  12 us
    all_to_all x1, starting transfers between devices, on_device(): lax.all_to_all(sample_prediction, 'member', split_axis=2, concat_axis=0,...  9.65 us
    dot_general x18, matrix products, feature_conv(): jnp.einsum('mrwc,cd->mrwd', wide[:, i:i + out_rows, j:j + col_count], ker...  7.01 us
    all_to_all x1, waiting for transfers between devices, on_device(): lax.all_to_all(sample_prediction, 'member', split_axis=2, concat_axis=0,...  6.9 us
    all_to_all x1, starting transfers between devices, all_reduce_sum(): lax.all_to_all(jnp.broadcast_to(own, (devices, width)), axes, 0, 0, tiled...  6.71 us
    dot_general x9, matrix products, input_conv(): jnp.einsum('rkw,kc->rwc', wide[i:i + out_rows, :, j:j + col_count], kerne...  4.4 us
  transfers between devices with their start and end apart: 4, of which 3 were waited for; matrix products, arithmetic and copies ran while one was open for 3% of the time, Pallas kernels for 0%

profile of v4, /device:TPU:1, one launch (start us, length us, event | category | flops | bytes accessed | tf_op | source)
XLA Modules:
  0.0 129.7 jit_solution(1793712658379191222)
XLA Ops:
  0.7 0.9 fusion.174
  1.5 4.3 %collective-permute-start = (bf16[3,32,256]{2,1,0:T(8,128)(2,1)S(1)}, bf16[3,32,256]{2,1,0:T(8,128)(2,1)S(1)}, u32[]{:S(2)}, u32[]{:S(2)}) collective-permute-start(bf16[3,32,256]{2,1,0:T(8,128)(2,1)S(1)} %get-tuple-element.21), channel_id=1, source_target_pairs={{0,1},{1,2},{2,3},{3,4},{4,5},{5,6},{6,7},{7,8},{8,9},{9,10},{10,1... | collective-permute-start | bytes 147464 | tf_op jit(solution)/shard_map/ppermute | solution.py:18
  5.9 1.3 collective-permute-start.1
  7.2 0.9 fusion.145
  8.4 0.9 fusion.173
  9.3 1.4 %collective-permute-done.1 = bf16[3,32,256]{2,1,0:T(8,128)(2,1)S(1)} collective-permute-done((bf16[3,32,256]{2,1,0:T(8,128)(2,1)S(1)}, bf16[3,32,256]{2,1,0:T(8,128)(2,1)S(1)}, u32[]{:S(2)}, u32[]{:S(2)}) %collective-permute-start.1) | collective-permute-done | bytes 49184 | tf_op jit(solution)/shard_map/ppermute | solution.py:19
  10.7 1.0 fusion.123
  12.5 0.4 fusion.78
  12.9 0.4 fusion.79
  13.2 0.4 fusion.80
  13.6 0.4 fusion.81
  14.4 0.8 fusion.175
  15.8 0.9 fusion.34
  19.0 0.4 fusion.52
  19.7 1.1 fusion.33
  23.2 0.6 add_convert_fusion
  24.2 0.8 copy.84
  25.0 9.7 %all-to-all-start = ((bf16[2,4,32,256]{3,1,0,2:T(4,128)(2,1)}), bf16[2,4,32,256]{3,1,0,2:T(4,128)(2,1)S(1)}, u32[]{:S(2)}, u32[]{:S(2)}) async-start(bf16[2,4,32,256]{3,1,0,2:T(4,128)(2,1)} %copy.84), calls=%async_computation | async-start | bytes 262144 | tf_op jit(solution)/shard_map/all_to_all | solution.py:152
  35.3 0.7 dynamic-slice_convert_fusion
  36.1 6.9 %all-to-all-done = bf16[2,4,32,256]{3,1,0,2:T(4,128)(2,1)S(1)} async-done(((bf16[2,4,32,256]{3,1,0,2:T(4,128)(2,1)}), bf16[2,4,32,256]{3,1,0,2:T(4,128)(2,1)S(1)}, u32[]{:S(2)}, u32[]{:S(2)}) %all-to-all-start) | async-done | bytes 131104 | tf_op jit(solution)/shard_map/all_to_all | solution.py:152
  43.2 2.3 %fusion.1 = (f32[16,4,4,256]{3,2,1,0:T(4,128)S(1)}, f32[4,4,256]{2,1,0:T(4,128)S(1)}) fusion(f32[16,4,4,256]{3,0,2,1:T(8,128)S(1)} %copy.87, f32[16,4,4,256]{3,2,1,0:T(4,128)S(1)} %bitcast.306), kind=kLoop, calls=%fused_computation.3 | loop fusion | flops 5173248 | bytes 802816 | tf_op jit(solution)/shard_map/reduce_sum | solution.py:160
  45.8 12.0 %all_to_all.42 = bf16[16,4,4,256]{3,2,1,0:T(4,128)(2,1)S(1)} all-to-all(bf16[16,4,4,256]{3,2,1,0:T(4,128)(2,1)S(1)} %multiply_convert_fusion), channel_id=1, replica_groups=mesh['member'=8,'tile'=32] {'member'}, dimensions={0} | all-to-all | bytes 262144 | tf_op jit(solution)/shard_map/all_to_all | solution.py:171
  57.9 0.9 fusion.41
  62.5 34.2 %all_to_all.43 = f32[256,1,640]{2,1,0:T(1,128)S(1)} all-to-all(f32[256,1,640]{2,1,0:T(1,128)S(1)} %bitcast.307), channel_id=1, replica_groups=mesh['member'=8,'tile'=32] {'member','tile'}, dimensions={0} | all-to-all | bytes 1310720 | tf_op jit(solution)/shard_map/all_to_all | solution.py:89
  96.7 0.5 reduce_sum.76
  97.2 1.2 broadcast_in_dim.29
  98.4 6.7 %all-to-all-start.3 = ((f32[256,1,640]{2,1,0:T(1,128)}), f32[256,1,640]{2,1,0:T(1,128)S(1)}, u32[]{:S(2)}, u32[]{:S(2)}) async-start(f32[256,1,640]{2,1,0:T(1,128)} %broadcast_in_dim.29), calls=%async_computation.3 | async-start | bytes 1310720 | tf_op jit(solution)/shard_map/all_to_all | solution.py:91
  105.2 0.6 copy.100
  105.8 21.9 %all-to-all-done.3 = f32[256,1,640]{2,1,0:T(1,128)S(1)} async-done(((f32[256,1,640]{2,1,0:T(1,128)}), f32[256,1,640]{2,1,0:T(1,128)S(1)}, u32[]{:S(2)}, u32[]{:S(2)}) %all-to-all-start.3) | async-done | bytes 655392 | tf_op jit(solution)/shard_map/all_to_all | solution.py:91
  127.8 0.9 slice.277
  128.6 0.5 slice.279
  129.1 0.6 slice_bitcast_fusion
  (70 shorter events, 11.6 us)
Async XLA Ops:
  0.6 7.5 %copy-start = (f32[16,256]{1,0:T(8,128)S(1)}, f32[16,256]{1,0:T(8,128)}, u32[]{:S(2)}) copy-start(f32[16,256]{1,0:T(8,128)} %param.16) | copy-start | bytes 49156
  0.6 11.1 %copy-start.3 = (bf16[3,3,32,128]{3,2,1,0:T(8,128)(2,1)S(1)}, bf16[3,3,32,128]{3,2,1,0:T(8,128)(2,1)}, u32[]{:S(2)}) copy-start(bf16[3,3,32,128]{3,2,1,0:T(8,128)(2,1)} %param.17) | copy-start | bytes 221188
  1.5 6.8 %collective-permute-start = (bf16[3,32,256]{2,1,0:T(8,128)(2,1)S(1)}, bf16[3,32,256]{2,1,0:T(8,128)(2,1)S(1)}, u32[]{:S(2)}, u32[]{:S(2)}) collective-permute-start(bf16[3,32,256]{2,1,0:T(8,128)(2,1)S(1)} %get-tuple-element.21), channel_id=1, source_target_pairs={{0,1},{1,2},{2,3},{3,4},{4,5},{5,6},{6,7},{7,8},{8,9},{9,10},{10,1... | collective-permute-start | bytes 147464 | tf_op jit(solution)/shard_map/ppermute | solution.py:18
  5.9 4.8 %collective-permute-start.1 = (bf16[3,32,256]{2,1,0:T(8,128)(2,1)S(1)}, bf16[3,32,256]{2,1,0:T(8,128)(2,1)S(1)}, u32[]{:S(2)}, u32[]{:S(2)}) collective-permute-start(bf16[3,32,256]{2,1,0:T(8,128)(2,1)S(1)} %get-tuple-element.20), channel_id=1, source_target_pairs={{1,0},{2,1},{3,2},{4,3},{5,4},{6,5},{7,6},{8,7},{9,8},{10,9},{11,1... | collective-permute-start | bytes 147464 | tf_op jit(solution)/shard_map/ppermute | solution.py:19
  15.8 1.0 copy-start.2
  19.7 1.1 copy-start.1
  23.2 0.7 copy-start.4
  23.2 0.7 copy-start.5
  25.0 18.0 %all-to-all-start = ((bf16[2,4,32,256]{3,1,0,2:T(4,128)(2,1)}), bf16[2,4,32,256]{3,1,0,2:T(4,128)(2,1)S(1)}, u32[]{:S(2)}, u32[]{:S(2)}) async-start(bf16[2,4,32,256]{3,1,0,2:T(4,128)(2,1)} %copy.84), calls=%async_computation | async-start | bytes 262144 | tf_op jit(solution)/shard_map/all_to_all | solution.py:152
  98.4 29.4 %all-to-all-start.3 = ((f32[256,1,640]{2,1,0:T(1,128)}), f32[256,1,640]{2,1,0:T(1,128)S(1)}, u32[]{:S(2)}, u32[]{:S(2)}) async-start(f32[256,1,640]{2,1,0:T(1,128)} %broadcast_in_dim.29), calls=%async_computation.3 | async-start | bytes 1310720 | tf_op jit(solution)/shard_map/all_to_all | solution.py:91

commit v5 on v4

--- a/solution.py
+++ b/solution.py
@@ -3,9 +3,10 @@
 import jax
 import jax.numpy as jnp
 from jax import lax
-from jax.sharding import PartitionSpec as P
+from jax.sharding import Mesh, PartitionSpec as P
 
 GRID_ROWS = 2048
+MEMBER = ("group", "core")
 
 
 def extended(x, sides, width):
@@ -78,18 +79,24 @@
     return lax.map(sign_single, probe)
 
 
-def all_reduce_sum(parts, axes):
-    devices = 1
-    for axis in axes:
-        devices *= lax.axis_size(axis)
+def all_reduce_sum(parts):
+    peers = ("group", "tile")
+    devices = lax.axis_size("group") * lax.axis_size("tile")
     flat = jnp.concatenate([p.reshape(-1) for p in parts])
     total = flat.shape[0]
-    width = -(-total // (devices * 128)) * 128
-    flat = jnp.pad(flat, (0, width * devices - total)).reshape(devices, width)
-    pieces = lax.all_to_all(flat, axes, 0, 0, tiled=True)
+    width = -(-total // (2 * devices * 128)) * 128
+    flat = jnp.pad(flat, (0, 2 * width * devices - total)).reshape(2, devices * width)
+    core = lax.axis_index("core")
+    swap = [(0, 1), (1, 0)]
+    first = core == 0
+    keep = jnp.where(first, flat[0], flat[1])
+    half = keep + lax.ppermute(jnp.where(first, flat[1], flat[0]), "core", swap)
+    pieces = lax.all_to_all(half.reshape(devices, width), peers, 0, 0, tiled=True)
     own = jnp.sum(pieces, axis=0, keepdims=True)
-    spread = lax.all_to_all(jnp.broadcast_to(own, (devices, width)), axes, 0, 0, tiled=True)
-    spread = spread.reshape(-1)
+    summed = lax.all_to_all(jnp.broadcast_to(own, (devices, width)), peers, 0, 0, tiled=True)
+    summed = summed.reshape(-1)
+    other = lax.ppermute(summed, "core", swap)
+    spread = jnp.where(first, jnp.concatenate([summed, other]), jnp.concatenate([other, summed]))
     out, at = [], 0
     for p in parts:
         out.append(spread[at : at + p.size].reshape(p.shape))
@@ -147,10 +154,10 @@
     row_global = band_row[0] + tile_at * row_count + jnp.arange(row_count, dtype=jnp.int32)
     latitude = math.pi * (row_global.astype(jnp.float32) + 0.5) / GRID_ROWS - math.pi / 2
     row_factor = (jnp.cos(latitude) / (band_rows * col_count))[None, :, None, None]
-    var_share = var_count // lax.axis_size("member")
-    var_start = lax.axis_index("member") * var_share
+    var_share = var_count // (lax.axis_size("group") * lax.axis_size("core"))
+    var_start = lax.axis_index(MEMBER) * var_share
     collected_members = lax.all_to_all(
-        sample_prediction, "member", split_axis=2, concat_axis=0, tiled=True
+        sample_prediction, MEMBER, split_axis=2, concat_axis=0, tiled=True
     )
     sample_group_predictions = collected_members.astype(jnp.float32)
     member_count = sample_group_predictions.shape[0]
@@ -168,7 +175,7 @@
             - sign_sums / (member_count * (member_count - 1))
         )
     ).astype(jnp.bfloat16)
-    cotangent = lax.all_to_all(cot_share, "member", split_axis=0, concat_axis=2, tiled=True)
+    cotangent = lax.all_to_all(cot_share, MEMBER, split_axis=0, concat_axis=2, tiled=True)
     head_grad = jnp.einsum(
         "mrwc,mrvw->cv", latent_layer_three, cotangent, preferred_element_type=jnp.float32
     )
@@ -191,19 +198,23 @@
             )
         rows_of.append(jnp.stack(cols_of))
     conv_grad = jnp.stack(rows_of)
-    conv_grad, head_grad_t, bias_grad = all_reduce_sum((conv_grad, head_grad.T, bias_grad), ("member", "tile"))
+    conv_grad, head_grad_t, bias_grad = all_reduce_sum((conv_grad, head_grad.T, bias_grad))
     head_grad = head_grad_t.T
     return (crps_map, conv_grad, head_grad, bias_grad)
 
 
 def solution(mesh):
+    members = mesh.shape["member"]
+    split = Mesh(
+        mesh.devices.reshape(members // 2, 2, mesh.shape["tile"]), ("group", "core", "tile")
+    )
     return jax.shard_map(
         on_device,
-        mesh=mesh,
+        mesh=split,
         in_specs=(
             P("tile", None, None),
             P("tile", None, None),
-            P("member"),
+            P(MEMBER),
             P(),
             P(),
             P(),
@@ -213,6 +224,6 @@
             P(),
             P(),
         ),
-        out_specs=(P("tile", "member", None), P(), P(), P()),
+        out_specs=(P("tile", MEMBER, None), P(), P(), P()),
         check_vma=False,
     )

time: 130 us -> 122 us (0.938)
  blocking collectives: 46.2 us -> 27 us
  starting transfers between devices: 22 us -> 30.7 us
  waiting for transfers between devices: 30.3 us -> 32.6 us
    all_to_all x2 -> x1, blocking collectives: 46.2 us -> 27 us  [all_reduce_sum(): lax.all_to_all(half.reshape(devices, width), peers, 0, 0, tiled=True)]
    ppermute x0 -> x2, starting transfers between devices: none -> 4.85 us  [the longest x1 3.46 us: all_reduce_sum(): other = lax.ppermute(summed, 'core', swap)]
    all_to_all x2 -> x3, starting transfers between devices: 16.4 us -> 20.2 us  [the longest x1 9.65 us: on_device(): lax.all_to_all(sample_prediction, MEMBER, split_axis=2, concat_axis=0, ti...]
    ppermute x0 -> x2, waiting for transfers between devices: none -> 1.79 us  [the longest x1 1.26 us: all_reduce_sum(): half = keep + lax.ppermute(jnp.where(first, flat[1], flat[0]), 'core', swap)]
    all_to_all x2 -> x3, waiting for transfers between devices: 28.8 us -> 29.4 us  [the longest x1 13.9 us: all_reduce_sum(): lax.all_to_all(jnp.broadcast_to(own, (devices, width)), peers, 0, 0, tile...]
  transfers between devices with their start and end apart: 4 -> 7, of which waited for: 3 -> 6; matrix products, arithmetic and copies ran while one was open for 3% -> 3% of each run, Pallas kernels for 0% -> 0%
where the time goes in v5:
time: 122 us
  waiting for transfers between devices  32.6 us (27%)
  starting transfers between devices  30.7 us (25%)
  blocking collectives  27 us (22%)
  matrix products  16.9 us (14%)
  other arithmetic  7.39 us (6%)
  local copies, waits for them, and re-layouts  5.48 us (4%)
  between operations  1.71 us (1%)
    all_to_all x1, blocking collectives, all_reduce_sum(): lax.all_to_all(half.reshape(devices, width), peers, 0, 0, tiled=True)  27 us
    all_to_all x1, waiting for transfers between devices, all_reduce_sum(): lax.all_to_all(jnp.broadcast_to(own, (devices, width)), peers, 0, 0, tile...  13.9 us
    all_to_all x1, starting transfers between devices, on_device(): lax.all_to_all(sample_prediction, MEMBER, split_axis=2, concat_axis=0, ti...  9.65 us
    all_to_all x1, waiting for transfers between devices, on_device(): lax.all_to_all(cot_share, MEMBER, split_axis=0, concat_axis=2, tiled=True)  8.61 us
    dot_general x18, matrix products, feature_conv(): jnp.einsum('mrwc,cd->mrwd', wide[:, i:i + out_rows, j:j + col_count], ker...  7.01 us
    all_to_all x1, waiting for transfers between devices, on_device(): lax.all_to_all(sample_prediction, MEMBER, split_axis=2, concat_axis=0, ti...  6.9 us
    all_to_all x1, starting transfers between devices, all_reduce_sum(): lax.all_to_all(jnp.broadcast_to(own, (devices, width)), peers, 0, 0, tile...  6.18 us
    dot_general x9, matrix products, input_conv(): jnp.einsum('rkw,kc->rwc', wide[i:i + out_rows, :, j:j + col_count], kerne...  4.4 us
  transfers between devices with their start and end apart: 7, of which 6 were waited for; matrix products, arithmetic and copies ran while one was open for 3% of the time, Pallas kernels for 0%

profile of v5, /device:TPU:1, one launch (start us, length us, event | category | flops | bytes accessed | tf_op | source)
XLA Modules:
  0.0 121.7 jit_solution(15254249115889039564)
XLA Ops:
  0.7 0.9 fusion.178
  1.5 4.3 %collective-permute-start = (bf16[3,32,256]{2,1,0:T(8,128)(2,1)S(1)}, bf16[3,32,256]{2,1,0:T(8,128)(2,1)S(1)}, u32[]{:S(2)}, u32[]{:S(2)}) collective-permute-start(bf16[3,32,256]{2,1,0:T(8,128)(2,1)S(1)} %get-tuple-element.21), channel_id=1, source_target_pairs={{0,1},{1,2},{2,3},{3,4},{4,5},{5,6},{6,7},{7,8},{8,9},{9,10},{10,1... | collective-permute-start | bytes 147464 | tf_op jit(solution)/shard_map/ppermute | solution.py:19
  5.9 1.3 %collective-permute-start.1 = (bf16[3,32,256]{2,1,0:T(8,128)(2,1)S(1)}, bf16[3,32,256]{2,1,0:T(8,128)(2,1)S(1)}, u32[]{:S(2)}, u32[]{:S(2)}) collective-permute-start(bf16[3,32,256]{2,1,0:T(8,128)(2,1)S(1)} %get-tuple-element.20), channel_id=1, source_target_pairs={{1,0},{2,1},{3,2},{4,3},{5,4},{6,5},{7,6},{8,7},{9,8},{10,9},{11,1... | collective-permute-start | bytes 147464 | tf_op jit(solution)/shard_map/ppermute | solution.py:20
  7.2 0.9 fusion.149
  8.4 0.9 fusion.177
  9.3 1.4 %collective-permute-done.1 = bf16[3,32,256]{2,1,0:T(8,128)(2,1)S(1)} collective-permute-done((bf16[3,32,256]{2,1,0:T(8,128)(2,1)S(1)}, bf16[3,32,256]{2,1,0:T(8,128)(2,1)S(1)}, u32[]{:S(2)}, u32[]{:S(2)}) %collective-permute-start.1) | collective-permute-done | bytes 49184 | tf_op jit(solution)/shard_map/ppermute | solution.py:20
  10.7 1.0 fusion.127
  14.4 0.8 fusion.179
  15.8 0.9 fusion.34
  19.7 1.1 fusion.33
  23.2 0.6 add_convert_fusion
  24.2 0.8 copy.84
  25.0 9.7 %all-to-all-start = ((bf16[2,4,32,256]{3,1,0,2:T(4,128)(2,1)}), bf16[2,4,32,256]{3,1,0,2:T(4,128)(2,1)S(1)}, u32[]{:S(2)}, u32[]{:S(2)}) async-start(bf16[2,4,32,256]{3,1,0,2:T(4,128)(2,1)} %copy.84), calls=%async_computation | async-start | bytes 262144 | tf_op jit(solution)/shard_map/all_to_all | solution.py:159
  35.3 0.7 dynamic-slice_convert_fusion
  36.1 6.9 %all-to-all-done = bf16[2,4,32,256]{3,1,0,2:T(4,128)(2,1)S(1)} async-done(((bf16[2,4,32,256]{3,1,0,2:T(4,128)(2,1)}), bf16[2,4,32,256]{3,1,0,2:T(4,128)(2,1)S(1)}, u32[]{:S(2)}, u32[]{:S(2)}) %all-to-all-start) | async-done | bytes 131104 | tf_op jit(solution)/shard_map/all_to_all | solution.py:159
  43.2 2.3 %fusion.1 = (f32[16,4,4,256]{3,2,1,0:T(4,128)S(1)}, f32[4,4,256]{2,1,0:T(4,128)S(1)}) fusion(f32[16,4,4,256]{3,0,2,1:T(8,128)S(1)} %copy.87, f32[16,4,4,256]{3,2,1,0:T(4,128)S(1)} %bitcast.309), kind=kLoop, calls=%fused_computation.3 | loop fusion | flops 5173248 | bytes 802816 | tf_op jit(solution)/shard_map/reduce_sum | solution.py:167
  45.5 0.9 multiply_convert_fusion
  46.4 4.3 %all-to-all-start.1 = ((bf16[16,4,4,256]{3,2,1,0:T(4,128)(2,1)}), bf16[16,4,4,256]{3,2,1,0:T(4,128)(2,1)S(1)}, u32[]{:S(2)}, u32[]{:S(2)}) async-start(bf16[16,4,4,256]{3,2,1,0:T(4,128)(2,1)} %multiply_convert_fusion), calls=%async_computation.1 | async-start | bytes 262144 | tf_op jit(solution)/shard_map/all_to_all | solution.py:178
  50.8 8.6 %all-to-all-done.1 = bf16[16,4,4,256]{3,2,1,0:T(4,128)(2,1)S(1)} async-done(((bf16[16,4,4,256]{3,2,1,0:T(4,128)(2,1)}), bf16[16,4,4,256]{3,2,1,0:T(4,128)(2,1)S(1)}, u32[]{:S(2)}, u32[]{:S(2)}) %all-to-all-start.1) | async-done | bytes 131104 | tf_op jit(solution)/shard_map/all_to_all | solution.py:178
  59.7 0.9 fusion.41
  64.1 1.4 %collective-permute-start.2 = (f32[81920]{0:T(1024)S(1)}, f32[81920]{0:T(1024)S(1)}, u32[]{:S(2)}, u32[]{:S(2)}) collective-permute-start(f32[81920]{0:T(1024)S(1)} %slice_select_fusion), channel_id=1, source_target_pairs={{0,32},{32,0},{1,33},{33,1},{2,34},{34,2},{3,35},{35,3},{4,36},{36... | collective-permute-start | bytes 983048 | tf_op jit(solution)/shard_map/ppermute | solution.py:93
  65.5 1.3 %collective-permute-done.2 = f32[81920]{0:T(1024)S(1)} collective-permute-done((f32[81920]{0:T(1024)S(1)}, f32[81920]{0:T(1024)S(1)}, u32[]{:S(2)}, u32[]{:S(2)}) %collective-permute-start.2) | collective-permute-done | bytes 327712 | tf_op jit(solution)/shard_map/ppermute | solution.py:93
  66.8 27.0 %all_to_all.42 = f32[128,1,640]{2,1,0:T(1,128)S(1)} all-to-all(f32[128,1,640]{2,1,0:T(1,128)S(1)} %bitcast.314), channel_id=1, replica_groups=mesh['group'=4,'core'=2,'tile'=32] {'group','tile'}, dimensions={0} | all-to-all | bytes 655360 | tf_op jit(solution)/shard_map/all_to_all | solution.py:94
  94.0 0.9 broadcast_in_dim.29
  94.9 6.2 %all-to-all-start.3 = ((f32[128,1,640]{2,1,0:T(1,128)}), f32[128,1,640]{2,1,0:T(1,128)S(1)}, u32[]{:S(2)}, u32[]{:S(2)}) async-start(f32[128,1,640]{2,1,0:T(1,128)} %broadcast_in_dim.29), calls=%async_computation.3 | async-start | bytes 655360 | tf_op jit(solution)/shard_map/all_to_all | solution.py:96
  101.1 13.9 %all-to-all-done.3 = f32[128,1,640]{2,1,0:T(1,128)S(1)} async-done(((f32[128,1,640]{2,1,0:T(1,128)}), f32[128,1,640]{2,1,0:T(1,128)S(1)}, u32[]{:S(2)}, u32[]{:S(2)}) %all-to-all-start.3) | async-done | bytes 327712 | tf_op jit(solution)/shard_map/all_to_all | solution.py:96
  115.0 3.5 %collective-permute-start.3 = (f32[81920]{0:T(1024)S(1)}, f32[81920]{0:T(1024)S(1)}, u32[]{:S(2)}, u32[]{:S(2)}) collective-permute-start(f32[81920]{0:T(1024)S(1)} %bitcast.310), channel_id=1, source_target_pairs={{0,32},{32,0},{1,33},{33,1},{2,34},{34,2},{3,35},{35,3},{4,36},{36... | collective-permute-start | bytes 983048 | tf_op jit(solution)/shard_map/ppermute | solution.py:98
  118.5 0.6 copy.100
  119.2 0.5 collective-permute-done.3
  119.7 0.9 slice.289
  120.6 0.5 slice.290
  121.1 0.6 fusion.124
  (77 shorter events, 13.5 us)
Async XLA Ops:
  0.6 7.5 %copy-start = (f32[16,256]{1,0:T(8,128)S(1)}, f32[16,256]{1,0:T(8,128)}, u32[]{:S(2)}) copy-start(f32[16,256]{1,0:T(8,128)} %param.16) | copy-start | bytes 49156
  0.6 11.1 %copy-start.3 = (bf16[3,3,32,128]{3,2,1,0:T(8,128)(2,1)S(1)}, bf16[3,3,32,128]{3,2,1,0:T(8,128)(2,1)}, u32[]{:S(2)}) copy-start(bf16[3,3,32,128]{3,2,1,0:T(8,128)(2,1)} %param.17) | copy-start | bytes 221188
  1.5 6.8 %collective-permute-start = (bf16[3,32,256]{2,1,0:T(8,128)(2,1)S(1)}, bf16[3,32,256]{2,1,0:T(8,128)(2,1)S(1)}, u32[]{:S(2)}, u32[]{:S(2)}) collective-permute-start(bf16[3,32,256]{2,1,0:T(8,128)(2,1)S(1)} %get-tuple-element.21), channel_id=1, source_target_pairs={{0,1},{1,2},{2,3},{3,4},{4,5},{5,6},{6,7},{7,8},{8,9},{9,10},{10,1... | collective-permute-start | bytes 147464 | tf_op jit(solution)/shard_map/ppermute | solution.py:19
  5.9 4.8 %collective-permute-start.1 = (bf16[3,32,256]{2,1,0:T(8,128)(2,1)S(1)}, bf16[3,32,256]{2,1,0:T(8,128)(2,1)S(1)}, u32[]{:S(2)}, u32[]{:S(2)}) collective-permute-start(bf16[3,32,256]{2,1,0:T(8,128)(2,1)S(1)} %get-tuple-element.20), channel_id=1, source_target_pairs={{1,0},{2,1},{3,2},{4,3},{5,4},{6,5},{7,6},{8,7},{9,8},{10,9},{11,1... | collective-permute-start | bytes 147464 | tf_op jit(solution)/shard_map/ppermute | solution.py:20
  15.8 1.0 copy-start.2
  19.7 1.1 copy-start.1
  23.2 0.7 copy-start.4
  23.2 0.7 copy-start.5
  25.0 18.0 %all-to-all-start = ((bf16[2,4,32,256]{3,1,0,2:T(4,128)(2,1)}), bf16[2,4,32,256]{3,1,0,2:T(4,128)(2,1)S(1)}, u32[]{:S(2)}, u32[]{:S(2)}) async-start(bf16[2,4,32,256]{3,1,0,2:T(4,128)(2,1)} %copy.84), calls=%async_computation | async-start | bytes 262144 | tf_op jit(solution)/shard_map/all_to_all | solution.py:159
  46.4 12.9 %all-to-all-start.1 = ((bf16[16,4,4,256]{3,2,1,0:T(4,128)(2,1)}), bf16[16,4,4,256]{3,2,1,0:T(4,128)(2,1)S(1)}, u32[]{:S(2)}, u32[]{:S(2)}) async-start(bf16[16,4,4,256]{3,2,1,0:T(4,128)(2,1)} %multiply_convert_fusion), calls=%async_computation.1 | async-start | bytes 262144 | tf_op jit(solution)/shard_map/all_to_all | solution.py:178
  64.1 2.7 %collective-permute-start.2 = (f32[81920]{0:T(1024)S(1)}, f32[81920]{0:T(1024)S(1)}, u32[]{:S(2)}, u32[]{:S(2)}) collective-permute-start(f32[81920]{0:T(1024)S(1)} %slice_select_fusion), channel_id=1, source_target_pairs={{0,32},{32,0},{1,33},{33,1},{2,34},{34,2},{3,35},{35,3},{4,36},{36... | collective-permute-start | bytes 983048 | tf_op jit(solution)/shard_map/ppermute | solution.py:93
  94.9 20.1 %all-to-all-start.3 = ((f32[128,1,640]{2,1,0:T(1,128)}), f32[128,1,640]{2,1,0:T(1,128)S(1)}, u32[]{:S(2)}, u32[]{:S(2)}) async-start(f32[128,1,640]{2,1,0:T(1,128)} %broadcast_in_dim.29), calls=%async_computation.3 | async-start | bytes 655360 | tf_op jit(solution)/shard_map/all_to_all | solution.py:96
  115.0 4.7 %collective-permute-start.3 = (f32[81920]{0:T(1024)S(1)}, f32[81920]{0:T(1024)S(1)}, u32[]{:S(2)}, u32[]{:S(2)}) collective-permute-start(f32[81920]{0:T(1024)S(1)} %bitcast.310), channel_id=1, source_target_pairs={{0,32},{32,0},{1,33},{33,1},{2,34},{34,2},{3,35},{35,3},{4,36},{36... | collective-permute-start | bytes 983048 | tf_op jit(solution)/shard_map/ppermute | solution.py:98

commit v6 on v5

--- a/solution.py
+++ b/solution.py
@@ -104,6 +104,29 @@
     return tuple(out)
 
 
+def member_scatter(x, var_share):
+    devices = lax.axis_size("group") * lax.axis_size("core")
+    rolled = jnp.roll(x, -lax.axis_index(MEMBER) * var_share, axis=2)
+    blocks = []
+    for k in range(devices):
+        block = rolled[:, :, k * var_share : (k + 1) * var_share]
+        if k:
+            block = lax.ppermute(block, MEMBER, [(s, (s + k) % devices) for s in range(devices)])
+        blocks.append(block)
+    return jnp.concatenate(blocks, axis=0)
+
+
+def member_gather(c, var_share, members):
+    devices = lax.axis_size("group") * lax.axis_size("core")
+    blocks = []
+    for k in range(devices):
+        block = c[k * members : (k + 1) * members]
+        if k:
+            block = lax.ppermute(block, MEMBER, [(d, (d - k) % devices) for d in range(devices)])
+        blocks.append(block)
+    return jnp.roll(jnp.concatenate(blocks, axis=2), lax.axis_index(MEMBER) * var_share, axis=2)
+
+
 def on_device(
     upsampled_coarse,
     target,
@@ -156,9 +179,7 @@
     row_factor = (jnp.cos(latitude) / (band_rows * col_count))[None, :, None, None]
     var_share = var_count // (lax.axis_size("group") * lax.axis_size("core"))
     var_start = lax.axis_index(MEMBER) * var_share
-    collected_members = lax.all_to_all(
-        sample_prediction, MEMBER, split_axis=2, concat_axis=0, tiled=True
-    )
+    collected_members = member_scatter(sample_prediction, var_share)
     sample_group_predictions = collected_members.astype(jnp.float32)
     member_count = sample_group_predictions.shape[0]
     truth = lax.dynamic_slice_in_dim(target, var_start, var_share, 1).astype(jnp.float32)
@@ -175,7 +196,7 @@
             - sign_sums / (member_count * (member_count - 1))
         )
     ).astype(jnp.bfloat16)
-    cotangent = lax.all_to_all(cot_share, MEMBER, split_axis=0, concat_axis=2, tiled=True)
+    cotangent = member_gather(cot_share, var_share, sample_prediction.shape[0])
     head_grad = jnp.einsum(
         "mrwc,mrvw->cv", latent_layer_three, cotangent, preferred_element_type=jnp.float32
     )

time: 122 us -> 130 us (1.066)
  blocking collectives: 27 us -> 51.3 us
  waiting for transfers between devices: 32.6 us -> 8.63 us
  starting transfers between devices: 30.7 us -> 39.7 us
  local copies, waits for them, and re-layouts: 5.48 us -> 3.32 us
    ppermute x0 -> x14, starting transfers between devices: none -> 30.8 us  [the longest x7 18.3 us: member_scatter(): lax.ppermute(block, MEMBER, [(s, (s + k) % devices) for s in range(device...]
    all_to_all x3 -> x0, waiting for transfers between devices: 29.4 us -> none  [the longest x1 13.9 us: all_reduce_sum(): lax.all_to_all(jnp.broadcast_to(own, (devices, width)), peers, 0, 0, tile...]
    all_to_all x3 -> x0, starting transfers between devices: 20.2 us -> none  [the longest x1 9.65 us: on_device(): lax.all_to_all(sample_prediction, MEMBER, split_axis=2, concat_axis=0, ti...]
    all_to_all x0 -> x1, blocking collectives: none -> 19.8 us  [all_reduce_sum(): lax.all_to_all(jnp.broadcast_to(own, (devices, width)), peers, 0, 0, tile...]
    ppermute x0 -> x14, waiting for transfers between devices: none -> 6.34 us  [the longest x7 4.52 us: member_gather(): lax.ppermute(block, MEMBER, [(d, (d - k) % devices) for d in range(device...]
    all_to_all x1, blocking collectives: 27 us -> 31.5 us  [all_reduce_sum(): lax.all_to_all(half.reshape(devices, width), peers, 0, 0, tiled=True)]
    ppermute x1, waiting for transfers between devices: 1.43 us -> 0.03 us  [extended(): after = lax.ppermute(first, axis, down)]
    ppermute x1, starting transfers between devices: 1.4 us -> 0.09 us  [all_reduce_sum(): half = keep + lax.ppermute(jnp.where(first, flat[1], flat[0]), 'core', swap)]
  transfers between devices with their start and end apart: 7 -> 18, of which waited for: 6 -> 5; matrix products, arithmetic and copies ran while one was open for 3% -> 3% of each run, Pallas kernels for 0% -> 0%
where the time goes in v6:
time: 130 us; the launch traced here: 129 us
  blocking collectives  51.3 us (39%)
  starting transfers between devices  39.7 us (31%)
  matrix products  16.9 us (13%)
  waiting for transfers between devices  8.63 us (7%)
  other arithmetic  7.49 us (6%)
  local copies, waits for them, and re-layouts  3.32 us (3%)
  between operations  1.81 us (1%)
    all_to_all x1, blocking collectives, all_reduce_sum(): lax.all_to_all(half.reshape(devices, width), peers, 0, 0, tiled=True)  31.5 us
    all_to_all x1, blocking collectives, all_reduce_sum(): lax.all_to_all(jnp.broadcast_to(own, (devices, width)), peers, 0, 0, tile...  19.8 us
    ppermute x7, starting transfers between devices, member_scatter(): lax.ppermute(block, MEMBER, [(s, (s + k) % devices) for s in range(device...  18.3 us
    ppermute x7, starting transfers between devices, member_gather(): lax.ppermute(block, MEMBER, [(d, (d - k) % devices) for d in range(device...  12.4 us
    dot_general x18, matrix products, feature_conv(): jnp.einsum('mrwc,cd->mrwd', wide[:, i:i + out_rows, j:j + col_count], ker...  7.03 us
    ppermute x7, waiting for transfers between devices, member_gather(): lax.ppermute(block, MEMBER, [(d, (d - k) % devices) for d in range(device...  4.52 us
    dot_general x9, matrix products, input_conv(): jnp.einsum('rkw,kc->rwc', wide[i:i + out_rows, :, j:j + col_count], kerne...  4.4 us
    ppermute x1, starting transfers between devices, extended(): before = lax.ppermute(last, axis, up)  4.35 us
  transfers between devices with their start and end apart: 18, of which 5 were waited for; matrix products, arithmetic and copies ran while one was open for 3% of the time, Pallas kernels for 0%

profile of v6, /device:TPU:1, one launch (start us, length us, event | category | flops | bytes accessed | tf_op | source)
XLA Modules:
  0.0 129.2 jit_solution(16850214226982991345)
XLA Ops:
  0.7 0.9 fusion.182
  1.5 4.3 %collective-permute-start = (bf16[3,32,256]{2,1,0:T(8,128)(2,1)S(1)}, bf16[3,32,256]{2,1,0:T(8,128)(2,1)S(1)}, u32[]{:S(2)}, u32[]{:S(2)}) collective-permute-start(bf16[3,32,256]{2,1,0:T(8,128)(2,1)S(1)} %get-tuple-element.30), channel_id=1, source_target_pairs={{0,1},{1,2},{2,3},{3,4},{4,5},{5,6},{6,7},{7,8},{8,9},{9,10},{10,1... | collective-permute-start | bytes 147464 | tf_op jit(solution)/shard_map/ppermute | solution.py:19
  5.9 1.3 %collective-permute-start.1 = (bf16[3,32,256]{2,1,0:T(8,128)(2,1)S(1)}, bf16[3,32,256]{2,1,0:T(8,128)(2,1)S(1)}, u32[]{:S(2)}, u32[]{:S(2)}) collective-permute-start(bf16[3,32,256]{2,1,0:T(8,128)(2,1)S(1)} %get-tuple-element.29), channel_id=1, source_target_pairs={{1,0},{2,1},{3,2},{4,3},{5,4},{6,5},{7,6},{8,7},{9,8},{10,9},{11,1... | collective-permute-start | bytes 147464 | tf_op jit(solution)/shard_map/ppermute | solution.py:20
  7.2 0.9 fusion.150
  8.3 0.7 dynamic-slice_convert_fusion
  9.8 0.9 fusion.181
  10.7 1.0 fusion.128
  14.4 0.8 fusion.183
  15.8 0.9 fusion.34
  19.7 1.1 fusion.33
  24.4 5.0 %collective-permute-start.2 = (bf16[2,4,4,256]{3,2,1,0:T(4,128)(2,1)S(1)}, bf16[2,4,4,256]{3,2,1,0:T(4,128)(2,1)S(1)}, u32[]{:S(2)}, u32[]{:S(2)}) collective-permute-start(bf16[2,4,4,256]{3,2,1,0:T(4,128)(2,1)S(1)} %get-tuple-element.25), channel_id=1, source_target_pairs={{0,32},{32,64},{64,96},{96,128},{128,160},{160,192},{192,224},{224... | collective-permute-start | bytes 49160 | tf_op jit(solution)/shard_map/ppermute | solution.py:114
  29.5 3.6 %collective-permute-start.3 = (bf16[2,4,4,256]{3,2,1,0:T(4,128)(2,1)S(1)}, bf16[2,4,4,256]{3,2,1,0:T(4,128)(2,1)S(1)}, u32[]{:S(2)}, u32[]{:S(2)}) collective-permute-start(bf16[2,4,4,256]{3,2,1,0:T(4,128)(2,1)S(1)} %get-tuple-element.24), channel_id=1, source_target_pairs={{0,64},{32,96},{64,128},{96,160},{128,192},{160,224},{192,0},{224,... | collective-permute-start | bytes 49160 | tf_op jit(solution)/shard_map/ppermute | solution.py:114
  33.1 1.2 collective-permute-start.4
  34.3 1.1 collective-permute-start.5
  35.4 2.8 %collective-permute-start.6 = (bf16[2,4,4,256]{3,2,1,0:T(4,128)(2,1)S(1)}, bf16[2,4,4,256]{3,2,1,0:T(4,128)(2,1)S(1)}, u32[]{:S(2)}, u32[]{:S(2)}) collective-permute-start(bf16[2,4,4,256]{3,2,1,0:T(4,128)(2,1)S(1)} %get-tuple-element.21), channel_id=1, source_target_pairs={{0,160},{32,192},{64,224},{96,0},{128,32},{160,64},{192,96},{224,1... | collective-permute-start | bytes 49160 | tf_op jit(solution)/shard_map/ppermute | solution.py:114
  38.2 2.3 %collective-permute-start.7 = (bf16[2,4,4,256]{3,2,1,0:T(4,128)(2,1)S(1)}, bf16[2,4,4,256]{3,2,1,0:T(4,128)(2,1)S(1)}, u32[]{:S(2)}, u32[]{:S(2)}) collective-permute-start(bf16[2,4,4,256]{3,2,1,0:T(4,128)(2,1)S(1)} %get-tuple-element.20), channel_id=1, source_target_pairs={{0,192},{32,224},{64,0},{96,32},{128,64},{160,96},{192,128},{224,1... | collective-permute-start | bytes 49160 | tf_op jit(solution)/shard_map/ppermute | solution.py:114
  40.5 2.3 %collective-permute-start.8 = (bf16[2,4,4,256]{3,2,1,0:T(4,128)(2,1)S(1)}, bf16[2,4,4,256]{3,2,1,0:T(4,128)(2,1)S(1)}, u32[]{:S(2)}, u32[]{:S(2)}) collective-permute-start(bf16[2,4,4,256]{3,2,1,0:T(4,128)(2,1)S(1)} %get-tuple-element.19), channel_id=1, source_target_pairs={{0,224},{32,0},{64,32},{96,64},{128,96},{160,128},{192,160},{224,1... | collective-permute-start | bytes 49160 | tf_op jit(solution)/shard_map/ppermute | solution.py:114
  42.9 1.8 %collective-permute-done.8 = bf16[2,4,4,256]{3,2,1,0:T(4,128)(2,1)S(1)} collective-permute-done((bf16[2,4,4,256]{3,2,1,0:T(4,128)(2,1)S(1)}, bf16[2,4,4,256]{3,2,1,0:T(4,128)(2,1)S(1)}, u32[]{:S(2)}, u32[]{:S(2)}) %collective-permute-start.8) | collective-permute-done | bytes 16416 | tf_op jit(solution)/shard_map/ppermute | solution.py:114
  44.8 2.3 %fusion.1 = (f32[16,4,4,256]{3,2,1,0:T(4,128)S(1)}, f32[4,4,256]{2,1,0:T(4,128)S(1)}) fusion(f32[16,4,4,256]{3,0,2,1:T(8,128)S(1)} %copy.47, f32[16,4,4,256]{3,2,1,0:T(4,128)S(1)} %convert_element_type.64), kind=kLoop, calls=%fused_computation.3 | loop fusion | flops 5173248 | bytes 802816 | tf_op jit(solution)/shard_map/reduce_sum | solution.py:188
  47.5 3.6 %collective-permute-start.10 = (bf16[2,4,4,256]{3,2,1,0:T(4,128)(2,1)S(1)}, bf16[2,4,4,256]{3,2,1,0:T(4,128)(2,1)S(1)}, u32[]{:S(2)}, u32[]{:S(2)}) collective-permute-start(bf16[2,4,4,256]{3,2,1,0:T(4,128)(2,1)S(1)} %get-tuple-element.16), channel_id=1, source_target_pairs={{0,192},{32,224},{64,0},{96,32},{128,64},{160,96},{192,128},{224,1... | collective-permute-start | bytes 49160 | tf_op jit(solution)/shard_map/ppermute | solution.py:125
  51.1 2.5 %collective-permute-start.12 = (bf16[2,4,4,256]{3,2,1,0:T(4,128)(2,1)S(1)}, bf16[2,4,4,256]{3,2,1,0:T(4,128)(2,1)S(1)}, u32[]{:S(2)}, u32[]{:S(2)}) collective-permute-start(bf16[2,4,4,256]{3,2,1,0:T(4,128)(2,1)S(1)} %get-tuple-element.14), channel_id=1, source_target_pairs={{0,128},{32,160},{64,192},{96,224},{128,0},{160,32},{192,64},{224,... | collective-permute-start | bytes 49160 | tf_op jit(solution)/shard_map/ppermute | solution.py:125
  53.7 4.3 %collective-permute-start.13 = (bf16[2,4,4,256]{3,2,1,0:T(4,128)(2,1)S(1)}, bf16[2,4,4,256]{3,2,1,0:T(4,128)(2,1)S(1)}, u32[]{:S(2)}, u32[]{:S(2)}) collective-permute-start(bf16[2,4,4,256]{3,2,1,0:T(4,128)(2,1)S(1)} %get-tuple-element.13), channel_id=1, source_target_pairs={{0,96},{32,128},{64,160},{96,192},{128,224},{160,0},{192,32},{224,... | collective-permute-start | bytes 49160 | tf_op jit(solution)/shard_map/ppermute | solution.py:125
  58.0 1.2 collective-permute-start.14
  59.1 0.8 collective-permute-start.15
  59.9 3.0 %collective-permute-done.14 = bf16[2,4,4,256]{3,2,1,0:T(4,128)(2,1)S(1)} collective-permute-done((bf16[2,4,4,256]{3,2,1,0:T(4,128)(2,1)S(1)}, bf16[2,4,4,256]{3,2,1,0:T(4,128)(2,1)S(1)}, u32[]{:S(2)}, u32[]{:S(2)}) %collective-permute-start.14) | collective-permute-done | bytes 16416 | tf_op jit(solution)/shard_map/ppermute | solution.py:125
  63.0 1.5 %collective-permute-done.9 = bf16[2,4,4,256]{3,2,1,0:T(4,128)(2,1)S(1)} collective-permute-done((bf16[2,4,4,256]{3,2,1,0:T(4,128)(2,1)S(1)}, bf16[2,4,4,256]{3,2,1,0:T(4,128)(2,1)S(1)}, u32[]{:S(2)}, u32[]{:S(2)}) %collective-permute-start.9) | collective-permute-done | bytes 16416 | tf_op jit(solution)/shard_map/ppermute | solution.py:125
  65.0 0.9 fusion.41
  69.3 1.6 %collective-permute-done.16 = f32[81920]{0:T(1024)S(1)} collective-permute-done((f32[81920]{0:T(1024)S(1)}, f32[81920]{0:T(1024)S(1)}, u32[]{:S(2)}, u32[]{:S(2)}) %collective-permute-start.16) | collective-permute-done | bytes 327712 | tf_op jit(solution)/shard_map/ppermute | solution.py:93
  71.0 31.5 %all_to_all.15 = f32[128,1,640]{2,1,0:T(1,128)S(1)} all-to-all(f32[128,1,640]{2,1,0:T(1,128)S(1)} %bitcast.302), channel_id=1, replica_groups=mesh['group'=4,'core'=2,'tile'=32] {'group','tile'}, dimensions={0} | all-to-all | bytes 655360 | tf_op jit(solution)/shard_map/all_to_all | solution.py:94
  102.9 19.8 %all_to_all.16 = f32[128,1,640]{2,1,0:T(1,128)S(1)} all-to-all(f32[128,1,640]{2,1,0:T(1,128)S(1)} %broadcast_in_dim.29), channel_id=1, replica_groups=mesh['group'=4,'core'=2,'tile'=32] {'group','tile'}, dimensions={0} | all-to-all | bytes 655360 | tf_op jit(solution)/shard_map/all_to_all | solution.py:96
  122.7 3.2 %collective-permute-start.17 = (f32[81920]{0:T(1024)S(1)}, f32[81920]{0:T(1024)S(1)}, u32[]{:S(2)}, u32[]{:S(2)}) collective-permute-start(f32[81920]{0:T(1024)S(1)} %bitcast.298), channel_id=1, source_target_pairs={{0,32},{32,0},{1,33},{33,1},{2,34},{34,2},{3,35},{35,3},{4,36},{36... | collective-permute-start | bytes 983048 | tf_op jit(solution)/shard_map/ppermute | solution.py:98
  127.2 0.9 slice.369
  (103 shorter events, 17.3 us)
Async XLA Ops:
  0.6 7.5 %copy-start = (f32[16,256]{1,0:T(8,128)S(1)}, f32[16,256]{1,0:T(8,128)}, u32[]{:S(2)}) copy-start(f32[16,256]{1,0:T(8,128)} %param.18) | copy-start | bytes 49156
  0.6 11.1 %copy-start.3 = (bf16[3,3,32,128]{3,2,1,0:T(8,128)(2,1)S(1)}, bf16[3,3,32,128]{3,2,1,0:T(8,128)(2,1)}, u32[]{:S(2)}) copy-start(bf16[3,3,32,128]{3,2,1,0:T(8,128)(2,1)} %param.19) | copy-start | bytes 221188
  1.5 8.2 %collective-permute-start = (bf16[3,32,256]{2,1,0:T(8,128)(2,1)S(1)}, bf16[3,32,256]{2,1,0:T(8,128)(2,1)S(1)}, u32[]{:S(2)}, u32[]{:S(2)}) collective-permute-start(bf16[3,32,256]{2,1,0:T(8,128)(2,1)S(1)} %get-tuple-element.30), channel_id=1, source_target_pairs={{0,1},{1,2},{2,3},{3,4},{4,5},{5,6},{6,7},{7,8},{8,9},{9,10},{10,1... | collective-permute-start | bytes 147464 | tf_op jit(solution)/shard_map/ppermute | solution.py:19
  5.9 4.8 %collective-permute-start.1 = (bf16[3,32,256]{2,1,0:T(8,128)(2,1)S(1)}, bf16[3,32,256]{2,1,0:T(8,128)(2,1)S(1)}, u32[]{:S(2)}, u32[]{:S(2)}) collective-permute-start(bf16[3,32,256]{2,1,0:T(8,128)(2,1)S(1)} %get-tuple-element.29), channel_id=1, source_target_pairs={{1,0},{2,1},{3,2},{4,3},{5,4},{6,5},{7,6},{8,7},{9,8},{10,9},{11,1... | collective-permute-start | bytes 147464 | tf_op jit(solution)/shard_map/ppermute | solution.py:20
  15.8 1.0 copy-start.2
  19.7 1.1 copy-start.1
  23.2 0.7 copy-start.4
  23.2 0.7 copy-start.5
  24.4 13.8 %collective-permute-start.2 = (bf16[2,4,4,256]{3,2,1,0:T(4,128)(2,1)S(1)}, bf16[2,4,4,256]{3,2,1,0:T(4,128)(2,1)S(1)}, u32[]{:S(2)}, u32[]{:S(2)}) collective-permute-start(bf16[2,4,4,256]{3,2,1,0:T(4,128)(2,1)S(1)} %get-tuple-element.25), channel_id=1, source_target_pairs={{0,32},{32,64},{64,96},{96,128},{128,160},{160,192},{192,224},{224... | collective-permute-start | bytes 49160 | tf_op jit(solution)/shard_map/ppermute | solution.py:114
  29.5 11.0 %collective-permute-start.3 = (bf16[2,4,4,256]{3,2,1,0:T(4,128)(2,1)S(1)}, bf16[2,4,4,256]{3,2,1,0:T(4,128)(2,1)S(1)}, u32[]{:S(2)}, u32[]{:S(2)}) collective-permute-start(bf16[2,4,4,256]{3,2,1,0:T(4,128)(2,1)S(1)} %get-tuple-element.24), channel_id=1, source_target_pairs={{0,64},{32,96},{64,128},{96,160},{128,192},{160,224},{192,0},{224,... | collective-permute-start | bytes 49160 | tf_op jit(solution)/shard_map/ppermute | solution.py:114
  33.1 9.8 %collective-permute-start.4 = (bf16[2,4,4,256]{3,2,1,0:T(4,128)(2,1)S(1)}, bf16[2,4,4,256]{3,2,1,0:T(4,128)(2,1)S(1)}, u32[]{:S(2)}, u32[]{:S(2)}) collective-permute-start(bf16[2,4,4,256]{3,2,1,0:T(4,128)(2,1)S(1)} %get-tuple-element.23), channel_id=1, source_target_pairs={{0,96},{32,128},{64,160},{96,192},{128,224},{160,0},{192,32},{224,... | collective-permute-start | bytes 49160 | tf_op jit(solution)/shard_map/ppermute | solution.py:114
  34.3 8.6 %collective-permute-start.5 = (bf16[2,4,4,256]{3,2,1,0:T(4,128)(2,1)S(1)}, bf16[2,4,4,256]{3,2,1,0:T(4,128)(2,1)S(1)}, u32[]{:S(2)}, u32[]{:S(2)}) collective-permute-start(bf16[2,4,4,256]{3,2,1,0:T(4,128)(2,1)S(1)} %get-tuple-element.22), channel_id=1, source_target_pairs={{0,128},{32,160},{64,192},{96,224},{128,0},{160,32},{192,64},{224,... | collective-permute-start | bytes 49160 | tf_op jit(solution)/shard_map/ppermute | solution.py:114
  35.4 7.5 %collective-permute-start.6 = (bf16[2,4,4,256]{3,2,1,0:T(4,128)(2,1)S(1)}, bf16[2,4,4,256]{3,2,1,0:T(4,128)(2,1)S(1)}, u32[]{:S(2)}, u32[]{:S(2)}) collective-permute-start(bf16[2,4,4,256]{3,2,1,0:T(4,128)(2,1)S(1)} %get-tuple-element.21), channel_id=1, source_target_pairs={{0,160},{32,192},{64,224},{96,0},{128,32},{160,64},{192,96},{224,1... | collective-permute-start | bytes 49160 | tf_op jit(solution)/shard_map/ppermute | solution.py:114
  38.2 4.7 %collective-permute-start.7 = (bf16[2,4,4,256]{3,2,1,0:T(4,128)(2,1)S(1)}, bf16[2,4,4,256]{3,2,1,0:T(4,128)(2,1)S(1)}, u32[]{:S(2)}, u32[]{:S(2)}) collective-permute-start(bf16[2,4,4,256]{3,2,1,0:T(4,128)(2,1)S(1)} %get-tuple-element.20), channel_id=1, source_target_pairs={{0,192},{32,224},{64,0},{96,32},{128,64},{160,96},{192,128},{224,1... | collective-permute-start | bytes 49160 | tf_op jit(solution)/shard_map/ppermute | solution.py:114
  40.5 4.2 %collective-permute-start.8 = (bf16[2,4,4,256]{3,2,1,0:T(4,128)(2,1)S(1)}, bf16[2,4,4,256]{3,2,1,0:T(4,128)(2,1)S(1)}, u32[]{:S(2)}, u32[]{:S(2)}) collective-permute-start(bf16[2,4,4,256]{3,2,1,0:T(4,128)(2,1)S(1)} %get-tuple-element.19), channel_id=1, source_target_pairs={{0,224},{32,0},{64,32},{96,64},{128,96},{160,128},{192,160},{224,1... | collective-permute-start | bytes 49160 | tf_op jit(solution)/shard_map/ppermute | solution.py:114
  47.5 11.7 %collective-permute-start.10 = (bf16[2,4,4,256]{3,2,1,0:T(4,128)(2,1)S(1)}, bf16[2,4,4,256]{3,2,1,0:T(4,128)(2,1)S(1)}, u32[]{:S(2)}, u32[]{:S(2)}) collective-permute-start(bf16[2,4,4,256]{3,2,1,0:T(4,128)(2,1)S(1)} %get-tuple-element.16), channel_id=1, source_target_pairs={{0,192},{32,224},{64,0},{96,32},{128,64},{160,96},{192,128},{224,1... | collective-permute-start | bytes 49160 | tf_op jit(solution)/shard_map/ppermute | solution.py:125
  51.0 8.9 %collective-permute-start.11 = (bf16[2,4,4,256]{3,2,1,0:T(4,128)(2,1)S(1)}, bf16[2,4,4,256]{3,2,1,0:T(4,128)(2,1)S(1)}, u32[]{:S(2)}, u32[]{:S(2)}) collective-permute-start(bf16[2,4,4,256]{3,2,1,0:T(4,128)(2,1)S(1)} %get-tuple-element.15), channel_id=1, source_target_pairs={{0,160},{32,192},{64,224},{96,0},{128,32},{160,64},{192,96},{224,1... | collective-permute-start | bytes 49160 | tf_op jit(solution)/shard_map/ppermute | solution.py:125
  51.1 8.8 %collective-permute-start.12 = (bf16[2,4,4,256]{3,2,1,0:T(4,128)(2,1)S(1)}, bf16[2,4,4,256]{3,2,1,0:T(4,128)(2,1)S(1)}, u32[]{:S(2)}, u32[]{:S(2)}) collective-permute-start(bf16[2,4,4,256]{3,2,1,0:T(4,128)(2,1)S(1)} %get-tuple-element.14), channel_id=1, source_target_pairs={{0,128},{32,160},{64,192},{96,224},{128,0},{160,32},{192,64},{224,... | collective-permute-start | bytes 49160 | tf_op jit(solution)/shard_map/ppermute | solution.py:125
  53.7 6.3 %collective-permute-start.13 = (bf16[2,4,4,256]{3,2,1,0:T(4,128)(2,1)S(1)}, bf16[2,4,4,256]{3,2,1,0:T(4,128)(2,1)S(1)}, u32[]{:S(2)}, u32[]{:S(2)}) collective-permute-start(bf16[2,4,4,256]{3,2,1,0:T(4,128)(2,1)S(1)} %get-tuple-element.13), channel_id=1, source_target_pairs={{0,96},{32,128},{64,160},{96,192},{128,224},{160,0},{192,32},{224,... | collective-permute-start | bytes 49160 | tf_op jit(solution)/shard_map/ppermute | solution.py:125
  58.0 5.0 %collective-permute-start.14 = (bf16[2,4,4,256]{3,2,1,0:T(4,128)(2,1)S(1)}, bf16[2,4,4,256]{3,2,1,0:T(4,128)(2,1)S(1)}, u32[]{:S(2)}, u32[]{:S(2)}) collective-permute-start(bf16[2,4,4,256]{3,2,1,0:T(4,128)(2,1)S(1)} %get-tuple-element.12), channel_id=1, source_target_pairs={{0,64},{32,96},{64,128},{96,160},{128,192},{160,224},{192,0},{224,... | collective-permute-start | bytes 49160 | tf_op jit(solution)/shard_map/ppermute | solution.py:125
  59.1 3.8 %collective-permute-start.15 = (bf16[2,4,4,256]{3,2,1,0:T(4,128)(2,1)S(1)}, bf16[2,4,4,256]{3,2,1,0:T(4,128)(2,1)S(1)}, u32[]{:S(2)}, u32[]{:S(2)}) collective-permute-start(bf16[2,4,4,256]{3,2,1,0:T(4,128)(2,1)S(1)} %get-tuple-element.11), channel_id=1, source_target_pairs={{0,32},{32,64},{64,96},{96,128},{128,160},{160,192},{192,224},{224... | collective-permute-start | bytes 49160 | tf_op jit(solution)/shard_map/ppermute | solution.py:125
  59.9 4.5 %collective-permute-start.9 = (bf16[2,4,4,256]{3,2,1,0:T(4,128)(2,1)S(1)}, bf16[2,4,4,256]{3,2,1,0:T(4,128)(2,1)S(1)}, u32[]{:S(2)}, u32[]{:S(2)}) collective-permute-start(bf16[2,4,4,256]{3,2,1,0:T(4,128)(2,1)S(1)} %get-tuple-element.17), channel_id=1, source_target_pairs={{0,224},{32,0},{64,32},{96,64},{128,96},{160,128},{192,160},{224,1... | collective-permute-start | bytes 49160 | tf_op jit(solution)/shard_map/ppermute | solution.py:125
  69.2 1.7 %collective-permute-start.16 = (f32[81920]{0:T(1024)S(1)}, f32[81920]{0:T(1024)S(1)}, u32[]{:S(2)}, u32[]{:S(2)}) collective-permute-start(f32[81920]{0:T(1024)S(1)} %slice_select_fusion), channel_id=1, source_target_pairs={{0,32},{32,0},{1,33},{33,1},{2,34},{34,2},{3,35},{35,3},{4,36},{36... | collective-permute-start | bytes 983048 | tf_op jit(solution)/shard_map/ppermute | solution.py:93
  122.7 4.5 %collective-permute-start.17 = (f32[81920]{0:T(1024)S(1)}, f32[81920]{0:T(1024)S(1)}, u32[]{:S(2)}, u32[]{:S(2)}) collective-permute-start(f32[81920]{0:T(1024)S(1)} %bitcast.298), channel_id=1, source_target_pairs={{0,32},{32,0},{1,33},{33,1},{2,34},{34,2},{3,35},{35,3},{4,36},{36... | collective-permute-start | bytes 983048 | tf_op jit(solution)/shard_map/ppermute | solution.py:98

commit v7 on v5

--- a/solution.py
+++ b/solution.py
@@ -23,35 +23,37 @@
 
 
 def input_conv(padded, kernel):
-    out_rows = padded.shape[0] - 2
-    col_count = padded.shape[2]
-    wide = jnp.pad(padded, ((0, 0), (0, 0), (1, 1)))
-    summed = jnp.zeros((out_rows, col_count, kernel.shape[3]), jnp.float32)
-    for i in range(3):
-        for j in range(3):
-            summed = summed + jnp.einsum(
-                "rkw,kc->rwc",
-                wide[i : i + out_rows, :, j : j + col_count],
-                kernel[i, j],
-                preferred_element_type=jnp.float32,
-            )
-    return summed
+    return lax.conv_general_dilated(
+        padded[None],
+        kernel,
+        window_strides=(1, 1),
+        padding=((0, 0), (1, 1)),
+        dimension_numbers=("NHCW", "HWIO", "NHWC"),
+        preferred_element_type=jnp.float32,
+    )[0]
 
 
 def feature_conv(padded, kernel):
-    out_rows = padded.shape[1] - 2
-    col_count = padded.shape[2]
-    wide = jnp.pad(padded, ((0, 0), (0, 0), (1, 1), (0, 0)))
-    summed = jnp.zeros((padded.shape[0], out_rows, col_count, kernel.shape[3]), jnp.float32)
-    for i in range(3):
-        for j in range(3):
-            summed = summed + jnp.einsum(
-                "mrwc,cd->mrwd",
-                wide[:, i : i + out_rows, j : j + col_count],
-                kernel[i, j],
-                preferred_element_type=jnp.float32,
-            )
-    return summed
+    return lax.conv_general_dilated(
+        padded,
+        kernel,
+        window_strides=(1, 1),
+        padding=((0, 0), (1, 1)),
+        dimension_numbers=("NHWC", "HWIO", "NHWC"),
+        preferred_element_type=jnp.float32,
+    )
+
+
+def kernel_grad(padded, d_out):
+    grad = lax.conv_general_dilated(
+        padded,
+        d_out,
+        window_strides=(1, 1),
+        padding=((0, 0), (1, 1)),
+        dimension_numbers=("CHWN", "IHWO", "NHWC"),
+        preferred_element_type=jnp.float32,
+    )
+    return jnp.transpose(grad, (1, 2, 0, 3))
 
 
 def condition(base, cond_scale, cond_shift):
@@ -183,21 +185,7 @@
     back = jnp.einsum("mrvw,cv->mrwc", cotangent, head_weight, preferred_element_type=jnp.float32)
     unused_out, pullback = jax.vjp(jax.nn.gelu, final_linear_response)
     d_pre = pullback(back)[0].astype(jnp.bfloat16)
-    second_wide = jnp.pad(second_padded, ((0, 0), (0, 0), (1, 1), (0, 0)))
-    rows_of = []
-    for i in range(3):
-        cols_of = []
-        for j in range(3):
-            cols_of.append(
-                jnp.einsum(
-                    "mrwc,mrwd->cd",
-                    second_wide[:, i : i + row_count, j : j + col_count],
-                    d_pre,
-                    preferred_element_type=jnp.float32,
-                )
-            )
-        rows_of.append(jnp.stack(cols_of))
-    conv_grad = jnp.stack(rows_of)
+    conv_grad = kernel_grad(second_padded, d_pre)
     conv_grad, head_grad_t, bias_grad = all_reduce_sum((conv_grad, head_grad.T, bias_grad))
     head_grad = head_grad_t.T
     return (crps_map, conv_grad, head_grad, bias_grad)

time: 122 us -> 138 us (1.13)
  local copies, waits for them, and re-layouts: 5.48 us -> 21.1 us
  waiting for transfers between devices: 32.6 us -> 23.9 us
  other arithmetic: 7.39 us -> 12.7 us
  blocking collectives: 27 us -> 30.5 us
  matrix products: 16.9 us -> 15.1 us
    dot_general x36 -> x0, matrix products: 14.5 us -> none  [the longest x18 7.01 us: feature_conv(): jnp.einsum('mrwc,cd->mrwd', wide[:, i:i + out_rows, j:j + col_count], ker...]
    all_to_all x1, waiting for transfers between devices: 8.61 us -> 0.52 us  [on_device(): lax.all_to_all(cot_share, MEMBER, split_axis=0, concat_axis=2, tiled=True)]
    conv_general_dilated x0 -> x3, matrix products: none -> 6.96 us  [the longest x2 5.93 us: feature_conv(): lax.conv_general_dilated(padded, kernel, window_strides=(1, 1), padding=(...]
    unnamed x14 -> x41, local copies, waits for them, and re-layouts: 0.74 us -> 6.54 us
    mul x1 -> x9, local copies, waits for them, and re-layouts: 0.32 us -> 4.13 us  [the longest x4 2.95 us: on_device(): unused_out, pullback = jax.vjp(jax.nn.gelu, final_linear_response)]
    all_to_all x1, blocking collectives: 27 us -> 30.5 us  [all_reduce_sum(): lax.all_to_all(half.reshape(devices, width), peers, 0, 0, tiled=True)]
    all_to_all x2, local copies, waits for them, and re-layouts: 0.08 us -> 3.2 us  [on_device(): lax.all_to_all(cot_share, MEMBER, split_axis=0, concat_axis=2, tiled=True)]
    transpose x0 -> x1, matrix products: none -> 2.67 us  [kernel_grad(): return jnp.transpose(grad, (1, 2, 0, 3))]
  transfers between devices with their start and end apart: 7 -> 7, of which waited for: 6 -> 6; matrix products, arithmetic and copies ran while one was open for 3% -> 7% of each run, Pallas kernels for 0% -> 0%
where the time goes in v7:
time: 138 us; the launch traced here: 136 us
  starting transfers between devices  31.5 us (23%)
  blocking collectives  30.5 us (22%)
  waiting for transfers between devices  23.9 us (17%)
  local copies, waits for them, and re-layouts  21.1 us (15%)
  matrix products  15.1 us (11%)
  other arithmetic  12.7 us (9%)
  between operations  1.8 us (1%)
    all_to_all x1, blocking collectives, all_reduce_sum(): lax.all_to_all(half.reshape(devices, width), peers, 0, 0, tiled=True)  30.5 us
    all_to_all x1, waiting for transfers between devices, all_reduce_sum(): lax.all_to_all(jnp.broadcast_to(own, (devices, width)), peers, 0, 0, tile...  13.9 us
    all_to_all x1, starting transfers between devices, on_device(): lax.all_to_all(sample_prediction, MEMBER, split_axis=2, concat_axis=0, ti...  9.67 us
    all_to_all x1, waiting for transfers between devices, on_device(): lax.all_to_all(sample_prediction, MEMBER, split_axis=2, concat_axis=0, ti...  6.9 us
    unnamed x41, local copies, waits for them, and re-layouts  6.54 us
    all_to_all x1, starting transfers between devices, all_reduce_sum(): lax.all_to_all(jnp.broadcast_to(own, (devices, width)), peers, 0, 0, tile...  6.4 us
    conv_general_dilated x2, matrix products, feature_conv(): lax.conv_general_dilated(padded, kernel, window_strides=(1, 1), padding=(...  5.93 us
    all_to_all x1, starting transfers between devices, on_device(): lax.all_to_all(cot_share, MEMBER, split_axis=0, concat_axis=2, tiled=True)  4.95 us
  transfers between devices with their start and end apart: 7, of which 6 were waited for; matrix products, arithmetic and copies ran while one was open for 7% of the time, Pallas kernels for 0%

profile of v7, /device:TPU:1, one launch (start us, length us, event | category | flops | bytes accessed | tf_op | source)
XLA Modules:
  0.0 136.5 jit_solution(11648044042158223032)
XLA Ops:
  1.5 4.3 %collective-permute-start = (bf16[3,32,256]{2,1,0:T(8,128)(2,1)S(1)}, bf16[3,32,256]{2,1,0:T(8,128)(2,1)S(1)}, u32[]{:S(2)}, u32[]{:S(2)}) collective-permute-start(bf16[3,32,256]{2,1,0:T(8,128)(2,1)S(1)} %get-tuple-element.30), channel_id=1, source_target_pairs={{0,1},{1,2},{2,3},{3,4},{4,5},{5,6},{6,7},{7,8},{8,9},{9,10},{10,1... | collective-permute-start | bytes 147464 | tf_op jit(solution)/shard_map/ppermute | solution.py:19
  5.9 1.3 collective-permute-start.1
  7.2 0.9 fusion.75
  13.1 1.0 convolution_select_fusion
  16.2 0.9 fusion.97
  17.1 0.9 fusion.38
  19.8 2.5 %fusion.35 = bf16[6,16,33,128]{3,1,2,0:T(8,128)(2,1)S(1)} fusion(bf16[3,3,128,128]{3,2,1,0:T(8,128)(2,1)S(1)} %copy-done.15, bf16[8,2,8,35,128]{4,0,3,2,1:T(8,128)(2,1)S(1)} %fusion.25, pred[6]{0:T(512)(128)(4,1)S(1)} %slice_bitcast_fusion, pred[16,33]{0,1:T(8,128)(4,1)S(1)} %copy-done.17), kind=kOutput, calls=%fused_computation.46 | convolution fusion | flops 939147264 | bytes 2253334 | tf_op jit(solution)/shard_map/conv_general_dilated | solution.py:37
  22.4 3.4 %add_multiply_fusion = (f32[4,16,33,128]{3,1,2,0:T(8,128)}, f32[4,16,33,128]{3,1,2,0:T(8,128)}, f32[4,16,33,128]{3,1,2,0:T(8,128)S(1)}, f32[4,16,33,128]{3,1,2,0:T(8,128)}, f32[4,16,33,128]{3,1,2,0:T(8,128)S(1)}) fusion(bf16[3,3,128,128]{3,2,1,0:T(8,128)(2,1)S(1)} %copy-done, bf16[6,2,8,1,128]{4,2,1,3,0:T(8,128)(2,1)S(1)} %pad.10, ...), kind=kOutput, calls=%fused_computation.70 | convolution fusion | flops 626688000 | bytes 6561792 | tf_op jit(solution)/shard_map/conv_general_dilated | solution.py:37
  27.2 0.9 copy.142
  28.2 9.7 %all-to-all-start = ((bf16[2,4,32,256]{3,1,0,2:T(4,128)(2,1)}), bf16[2,4,32,256]{3,1,0,2:T(4,128)(2,1)S(1)}, u32[]{:S(2)}, u32[]{:S(2)}) async-start(bf16[2,4,32,256]{3,1,0,2:T(4,128)(2,1)} %copy.142), calls=%async_computation | async-start | bytes 262144 | tf_op jit(solution)/shard_map/all_to_all | solution.py:161
  39.3 6.9 %all-to-all-done = bf16[2,4,32,256]{3,1,0,2:T(4,128)(2,1)S(1)} async-done(((bf16[2,4,32,256]{3,1,0,2:T(4,128)(2,1)}), bf16[2,4,32,256]{3,1,0,2:T(4,128)(2,1)S(1)}, u32[]{:S(2)}, u32[]{:S(2)}) %all-to-all-start) | async-done | bytes 131104 | tf_op jit(solution)/shard_map/all_to_all | solution.py:161
  46.5 2.3 %fusion.1 = (f32[16,4,4,256]{3,2,1,0:T(4,128)S(1)}, f32[4,4,256]{2,1,0:T(4,128)S(1)}) fusion(f32[16,4,4,256]{3,0,2,1:T(8,128)S(1)} %copy.145, f32[16,4,4,256]{3,2,1,0:T(4,128)S(1)} %bitcast.165), kind=kLoop, calls=%fused_computation.3 | loop fusion | flops 5173248 | bytes 802816 | tf_op jit(solution)/shard_map/reduce_sum | solution.py:169
  48.7 0.9 multiply_convert_fusion
  49.6 4.9 %all-to-all-start.1 = ((bf16[16,4,4,256]{3,2,1,0:T(4,128)(2,1)}), bf16[16,4,4,256]{3,2,1,0:T(4,128)(2,1)}, u32[]{:S(2)}, u32[]{:S(2)}) async-start(bf16[16,4,4,256]{3,2,1,0:T(4,128)(2,1)} %multiply_convert_fusion), calls=%async_computation.1 | async-start | bytes 262144 | tf_op jit(solution)/shard_map/all_to_all | solution.py:180
  54.9 1.0 copy-done.10
  56.8 1.1 copy-done.9
  58.4 1.1 slice.78
  60.5 1.0 slice.79
  61.5 1.3 maximum_bitcast_fusion.2
  63.3 1.6 %copy.147 = bf16[2,4,8,4,256]{4,3,2,1,0:T(4,128)(2,1)} copy(bf16[2,4,8,4,256]{4,3,1,0,2:T(4,128)(2,1)} %bitcast.27) | data formatting | bytes 262144 | tf_op jit(solution)/shard_map/all_to_all | solution.py:180
  65.0 1.0 convert_reduce_fusion
  66.0 1.6 %all_to_all.34 = bf16[2,4,32,256]{3,2,1,0:T(8,128)(2,1)} reshape(bf16[2,4,8,4,256]{4,3,2,1,0:T(4,128)(2,1)} %copy.147) | data formatting | bytes 262144 | tf_op jit(solution)/shard_map/all_to_all | solution.py:180
  67.6 1.4 %convolution_bitcast_fusion.1 = f32[4096]{0:T(1024)S(1)} fusion(bf16[2,4,32,256]{3,2,1,0:T(8,128)(2,1)} %all_to_all.34, f32[4,2,256,128]{3,0,2,1:T(4,128)S(1)} %slice.73, bf16[2,8,256,128]{3,2,1,0:T(8,128)(2,1)} %copy-done.2), kind=kOutput, calls=%fused_computation.39 | convolution fusion | flops 17563648 | bytes 1720320 | tf_op jit(solution)/shard_map/mrwc,mrvw->cv/dot_general | solution.py:181
  69.0 2.0 %fusion.53 = bf16[4,2,256,128]{3,2,0,1:T(8,128)(2,1)S(1)} fusion(f32[4,2,256,128]{3,0,2,1:T(4,128)} %slice.79, f32[4,2,256,128]{3,0,2,1:T(4,128)S(1)} %copy-done.1, f32[4,2,256,128]{3,0,2,1:T(4,128)S(1)} %slice.77, f32[4,2,256,128]{3,0,2,1:T(4,128)S(1)} %slice.76, bf16[2,4,32,256]{3,2,1,0:T(8,128)(2,1)S(1)} %copy-done.7, bf16[128,32]{0,1:T(8,128)(2,1)S(1)} %copy-done.13), kind=kOutput, calls=%fused_computation.69 | convolution fusion | flops 19398656 | bytes 4857856 | tf_op jit(solution)/shard_map/mrvw,cv->mrwc/dot_general | solution.py:185
  72.4 2.7 %fusion.2 = f32[3,3,128,128,1]{3,2,1,4,0:T(8,128)S(1)} fusion(bf16[4,16,33,128,1]{3,0,2,1,4:T(4,128)(2,1)S(1)} %bitcast.177, bf16[6,16,33,128,1]{3,1,2,0,4:T(8,128)(2,1)} %get-tuple-element.36, bf16[6,16,33,128,1]{3,1,2,0,4:T(8,128)(2,1)S(1)} %bitcast.169, bf16[6,16,33,128,1]{3,1,2,0,4:T(8,128)(2,1)S(1)} %copy-done.11), kind=kOutput, calls=%fused_computation.6 | convolution fusion | flops 625287168 | bytes 3563520 | tf_op jit(solution)/shard_map/transpose | solution.py:56
  75.1 1.4 %collective-permute-start.2 = (f32[81920]{0:T(1024)S(1)}, f32[81920]{0:T(1024)S(1)}, u32[]{:S(2)}, u32[]{:S(2)}) collective-permute-start(f32[81920]{0:T(1024)S(1)} %slice_select_fusion), channel_id=1, source_target_pairs={{0,32},{32,0},{1,33},{33,1},{2,34},{34,2},{3,35},{35,3},{4,36},{36... | collective-permute-start | bytes 983048 | tf_op jit(solution)/shard_map/ppermute | solution.py:95
  76.5 1.3 collective-permute-done.2
  77.8 30.5 %all_to_all.42 = f32[128,1,640]{2,1,0:T(1,128)S(1)} all-to-all(f32[128,1,640]{2,1,0:T(1,128)S(1)} %bitcast.174), channel_id=1, replica_groups=mesh['group'=4,'core'=2,'tile'=32] {'group','tile'}, dimensions={0} | all-to-all | bytes 655360 | tf_op jit(solution)/shard_map/all_to_all | solution.py:96
  108.5 0.9 broadcast_in_dim.32
  109.4 6.4 %all-to-all-start.3 = ((f32[128,1,640]{2,1,0:T(1,128)}), f32[128,1,640]{2,1,0:T(1,128)S(1)}, u32[]{:S(2)}, u32[]{:S(2)}) async-start(f32[128,1,640]{2,1,0:T(1,128)} %broadcast_in_dim.32), calls=%async_computation.3 | async-start | bytes 655360 | tf_op jit(solution)/shard_map/all_to_all | solution.py:98
  115.9 13.9 %all-to-all-done.3 = f32[128,1,640]{2,1,0:T(1,128)S(1)} async-done(((f32[128,1,640]{2,1,0:T(1,128)}), f32[128,1,640]{2,1,0:T(1,128)S(1)}, u32[]{:S(2)}, u32[]{:S(2)}) %all-to-all-start.3) | async-done | bytes 327712 | tf_op jit(solution)/shard_map/all_to_all | solution.py:98
  129.7 3.5 %collective-permute-start.3 = (f32[81920]{0:T(1024)S(1)}, f32[81920]{0:T(1024)S(1)}, u32[]{:S(2)}, u32[]{:S(2)}) collective-permute-start(f32[81920]{0:T(1024)S(1)} %bitcast.170), channel_id=1, source_target_pairs={{0,32},{32,0},{1,33},{33,1},{2,34},{34,2},{3,35},{35,3},{4,36},{36... | collective-permute-start | bytes 983048 | tf_op jit(solution)/shard_map/ppermute | solution.py:100
  (95 shorter events, 20.2 us)
Async XLA Ops:
  0.6 21.8 %copy-start = (bf16[3,3,128,128]{3,2,1,0:T(8,128)(2,1)S(1)}, bf16[3,3,128,128]{3,2,1,0:T(8,128)(2,1)}, u32[]{:S(2)}) copy-start(bf16[3,3,128,128]{3,2,1,0:T(8,128)(2,1)} %param.19) | copy-start | bytes 884740
  1.5 8.4 %collective-permute-start = (bf16[3,32,256]{2,1,0:T(8,128)(2,1)S(1)}, bf16[3,32,256]{2,1,0:T(8,128)(2,1)S(1)}, u32[]{:S(2)}, u32[]{:S(2)}) collective-permute-start(bf16[3,32,256]{2,1,0:T(8,128)(2,1)S(1)} %get-tuple-element.30), channel_id=1, source_target_pairs={{0,1},{1,2},{2,3},{3,4},{4,5},{5,6},{6,7},{7,8},{8,9},{9,10},{10,1... | collective-permute-start | bytes 147464 | tf_op jit(solution)/shard_map/ppermute | solution.py:19
  5.9 4.8 %collective-permute-start.1 = (bf16[3,32,256]{2,1,0:T(8,128)(2,1)S(1)}, bf16[3,32,256]{2,1,0:T(8,128)(2,1)S(1)}, u32[]{:S(2)}, u32[]{:S(2)}) collective-permute-start(bf16[3,32,256]{2,1,0:T(8,128)(2,1)S(1)} %get-tuple-element.31), channel_id=1, source_target_pairs={{1,0},{2,1},{3,2},{4,3},{5,4},{6,5},{7,6},{8,7},{9,8},{10,9},{11,1... | collective-permute-start | bytes 147464 | tf_op jit(solution)/shard_map/ppermute | solution.py:20
  11.7 1.4 copy-start.16
  11.8 1.4 copy-start.18
  18.0 8.3 %copy-start.2 = (bf16[2,8,256,128]{3,2,1,0:T(8,128)(2,1)}, bf16[2,8,256,128]{3,2,1,0:T(8,128)(2,1)S(1)}, u32[]{:S(2)}) copy-start(bf16[2,8,256,128]{3,2,1,0:T(8,128)(2,1)S(1)} %fusion.38) | copy-start | bytes 3145732
  18.8 1.0 copy-start.15
  18.8 1.0 copy-start.17
  22.3 32.2 %copy-start.3 = (bf16[6,16,33,128]{3,1,2,0:T(8,128)(2,1)}, bf16[6,16,33,128]{3,1,2,0:T(8,128)(2,1)S(1)}, u32[]{:S(2)}) copy-start(bf16[6,16,33,128]{3,1,2,0:T(8,128)(2,1)S(1)} %fusion.35) | copy-start | bytes 2433028
  26.2 0.7 copy-start.12
  26.2 0.7 copy-start.14
  28.2 18.0 %all-to-all-start = ((bf16[2,4,32,256]{3,1,0,2:T(4,128)(2,1)}), bf16[2,4,32,256]{3,1,0,2:T(4,128)(2,1)S(1)}, u32[]{:S(2)}, u32[]{:S(2)}) async-start(bf16[2,4,32,256]{3,1,0,2:T(4,128)(2,1)} %copy.142), calls=%async_computation | async-start | bytes 262144 | tf_op jit(solution)/shard_map/all_to_all | solution.py:161
  46.2 3.5 %copy-start.5 = (bf16[2,4,32,256]{3,1,0,2:T(4,128)(2,1)}, bf16[2,4,32,256]{3,1,0,2:T(4,128)(2,1)S(1)}, u32[]{:S(2)}) copy-start(bf16[2,4,32,256]{3,1,0,2:T(4,128)(2,1)S(1)} %all-to-all-done) | copy-start | bytes 393220
  49.6 13.7 %all-to-all-start.1 = ((bf16[16,4,4,256]{3,2,1,0:T(4,128)(2,1)}), bf16[16,4,4,256]{3,2,1,0:T(4,128)(2,1)}, u32[]{:S(2)}, u32[]{:S(2)}) async-start(bf16[16,4,4,256]{3,2,1,0:T(4,128)(2,1)} %multiply_convert_fusion), calls=%async_computation.1 | async-start | bytes 262144 | tf_op jit(solution)/shard_map/all_to_all | solution.py:180
  54.6 1.2 copy-start.10
  56.8 1.2 copy-start.9
  58.4 1.6 %copy-start.8 = (f32[4,16,33,128]{3,1,2,0:T(8,128)S(1)}, f32[4,16,33,128]{3,1,2,0:T(8,128)}, u32[]{:S(2)}) copy-start(f32[4,16,33,128]{3,1,2,0:T(8,128)} %get-tuple-element.25) | copy-start | bytes 3244036
  63.3 5.7 %copy-start.13 = (bf16[128,32]{0,1:T(8,128)(2,1)S(1)}, bf16[128,32]{0,1:T(8,128)(2,1)}, u32[]{:S(2)}) copy-start(bf16[128,32]{0,1:T(8,128)(2,1)} %param.20) | copy-start | bytes 24580
  67.6 1.4 %copy-start.1 = (f32[4,2,256,128]{3,0,2,1:T(4,128)S(1)}, f32[4,2,256,128]{3,0,2,1:T(4,128)}, u32[]{:S(2)}) copy-start(f32[4,2,256,128]{3,0,2,1:T(4,128)} %slice.78) | copy-start | bytes 3145732
  67.6 1.4 %copy-start.7 = (bf16[2,4,32,256]{3,2,1,0:T(8,128)(2,1)S(1)}, bf16[2,4,32,256]{3,2,1,0:T(8,128)(2,1)}, u32[]{:S(2)}) copy-start(bf16[2,4,32,256]{3,2,1,0:T(8,128)(2,1)} %all_to_all.34) | copy-start | bytes 393220
  71.0 1.1 copy-start.4
  71.0 1.4 %copy-start.11 = (bf16[6,16,33,128,1]{3,1,2,0,4:T(8,128)(2,1)S(1)}, bf16[6,16,33,128,1]{3,1,2,0,4:T(8,128)(2,1)}, u32[]{:S(2)}) copy-start(bf16[6,16,33,128,1]{3,1,2,0,4:T(8,128)(2,1)} %get-tuple-element.35) | copy-start | bytes 2433028
  75.1 2.6 %collective-permute-start.2 = (f32[81920]{0:T(1024)S(1)}, f32[81920]{0:T(1024)S(1)}, u32[]{:S(2)}, u32[]{:S(2)}) collective-permute-start(f32[81920]{0:T(1024)S(1)} %slice_select_fusion), channel_id=1, source_target_pairs={{0,32},{32,0},{1,33},{33,1},{2,34},{34,2},{3,35},{35,3},{4,36},{36... | collective-permute-start | bytes 983048 | tf_op jit(solution)/shard_map/ppermute | solution.py:95
  77.8 55.4 %copy-start.6 = (bf16[2,4,32,256]{3,1,0,2:T(4,128)(2,1)S(1)}, bf16[2,4,32,256]{3,1,0,2:T(4,128)(2,1)}, u32[]{:S(2)}) copy-start(bf16[2,4,32,256]{3,1,0,2:T(4,128)(2,1)} %copy-done.5) | copy-start | bytes 393220
  109.4 20.3 %all-to-all-start.3 = ((f32[128,1,640]{2,1,0:T(1,128)}), f32[128,1,640]{2,1,0:T(1,128)S(1)}, u32[]{:S(2)}, u32[]{:S(2)}) async-start(f32[128,1,640]{2,1,0:T(1,128)} %broadcast_in_dim.32), calls=%async_computation.3 | async-start | bytes 655360 | tf_op jit(solution)/shard_map/all_to_all | solution.py:98
  129.7 4.7 %collective-permute-start.3 = (f32[81920]{0:T(1024)S(1)}, f32[81920]{0:T(1024)S(1)}, u32[]{:S(2)}, u32[]{:S(2)}) collective-permute-start(f32[81920]{0:T(1024)S(1)} %bitcast.170), channel_id=1, source_target_pairs={{0,32},{32,0},{1,33},{33,1},{2,34},{34,2},{3,35},{35,3},{4,36},{36... | collective-permute-start | bytes 983048 | tf_op jit(solution)/shard_map/ppermute | solution.py:100

commit v8 on v5

--- a/solution.py
+++ b/solution.py
@@ -26,15 +26,15 @@
     out_rows = padded.shape[0] - 2
     col_count = padded.shape[2]
     wide = jnp.pad(padded, ((0, 0), (0, 0), (1, 1)))
+    shifted = jnp.concatenate([wide[:, :, j : j + col_count] for j in range(3)], axis=1)
     summed = jnp.zeros((out_rows, col_count, kernel.shape[3]), jnp.float32)
     for i in range(3):
-        for j in range(3):
-            summed = summed + jnp.einsum(
-                "rkw,kc->rwc",
-                wide[i : i + out_rows, :, j : j + col_count],
-                kernel[i, j],
-                preferred_element_type=jnp.float32,
-            )
+        summed = summed + jnp.einsum(
+            "rkw,kc->rwc",
+            shifted[i : i + out_rows],
+            kernel[i].reshape(-1, kernel.shape[3]),
+            preferred_element_type=jnp.float32,
+        )
     return summed
 
 
@@ -42,15 +42,15 @@
     out_rows = padded.shape[1] - 2
     col_count = padded.shape[2]
     wide = jnp.pad(padded, ((0, 0), (0, 0), (1, 1), (0, 0)))
+    shifted = jnp.concatenate([wide[:, :, j : j + col_count] for j in range(3)], axis=3)
     summed = jnp.zeros((padded.shape[0], out_rows, col_count, kernel.shape[3]), jnp.float32)
     for i in range(3):
-        for j in range(3):
-            summed = summed + jnp.einsum(
-                "mrwc,cd->mrwd",
-                wide[:, i : i + out_rows, j : j + col_count],
-                kernel[i, j],
-                preferred_element_type=jnp.float32,
-            )
+        summed = summed + jnp.einsum(
+            "mrwc,cd->mrwd",
+            shifted[:, i : i + out_rows],
+            kernel[i].reshape(-1, kernel.shape[3]),
+            preferred_element_type=jnp.float32,
+        )
     return summed
 
 

time: 122 us -> 118 us (0.967)
  matrix products: 16.9 us -> 11.2 us
  local copies, waits for them, and re-layouts: 5.48 us -> 9.4 us
  waiting for transfers between devices: 32.6 us -> 31.3 us
    dot_general x27 -> x9, matrix products: 11.4 us -> 5.73 us  [the longest x6 4.7 us: feature_conv(): jnp.einsum('mrwc,cd->mrwd', shifted[:, i:i + out_rows], kernel[i].reshape...]
    slice x0 -> x6, local copies, waits for them, and re-layouts: none -> 4 us  [the longest x2 2.03 us: feature_conv(): kernel[i].reshape(-1, kernel.shape[3])]
    ppermute x1, waiting for transfers between devices: 1.43 us -> 0.01 us  [extended(): after = lax.ppermute(first, axis, down)]
  transfers between devices with their start and end apart: 7 -> 7, of which waited for: 6 -> 5; matrix products, arithmetic and copies ran while one was open for 3% -> 5% of each run, Pallas kernels for 0% -> 0%
where the time goes in v8:
time: 118 us; the launch traced here: 117 us
  waiting for transfers between devices  31.3 us (27%)
  starting transfers between devices  30.1 us (26%)
  blocking collectives  26.9 us (23%)
  matrix products  11.2 us (9%)
  local copies, waits for them, and re-layouts  9.4 us (8%)
  other arithmetic  6.47 us (5%)
  between operations  1.71 us (1%)
    all_to_all x1, blocking collectives, all_reduce_sum(): lax.all_to_all(half.reshape(devices, width), peers, 0, 0, tiled=True)  26.9 us
    all_to_all x1, waiting for transfers between devices, all_reduce_sum(): lax.all_to_all(jnp.broadcast_to(own, (devices, width)), peers, 0, 0, tile...  13.9 us
    all_to_all x1, starting transfers between devices, on_device(): lax.all_to_all(sample_prediction, MEMBER, split_axis=2, concat_axis=0, ti...  9.16 us
    all_to_all x1, waiting for transfers between devices, on_device(): lax.all_to_all(cot_share, MEMBER, split_axis=0, concat_axis=2, tiled=True)  8.71 us
    all_to_all x1, waiting for transfers between devices, on_device(): lax.all_to_all(sample_prediction, MEMBER, split_axis=2, concat_axis=0, ti...  6.9 us
    all_to_all x1, starting transfers between devices, all_reduce_sum(): lax.all_to_all(jnp.broadcast_to(own, (devices, width)), peers, 0, 0, tile...  6.18 us
    dot_general x6, matrix products, feature_conv(): jnp.einsum('mrwc,cd->mrwd', shifted[:, i:i + out_rows], kernel[i].reshape...  4.7 us
    ppermute x1, starting transfers between devices, extended(): before = lax.ppermute(last, axis, up)  4.35 us
  transfers between devices with their start and end apart: 7, of which 5 were waited for; matrix products, arithmetic and copies ran while one was open for 5% of the time, Pallas kernels for 0%

profile of v8, /device:TPU:1, one launch (start us, length us, event | category | flops | bytes accessed | tf_op | source)
XLA Modules:
  0.0 117.1 jit_solution(8264000674549051746)
XLA Ops:
  0.7 0.9 fusion.67
  1.6 4.3 %collective-permute-start = (bf16[3,32,256]{2,1,0:T(8,128)(2,1)S(1)}, bf16[3,32,256]{2,1,0:T(8,128)(2,1)S(1)}, u32[]{:S(2)}, u32[]{:S(2)}) collective-permute-start(bf16[3,32,256]{2,1,0:T(8,128)(2,1)S(1)} %get-tuple-element.36), channel_id=1, source_target_pairs={{0,1},{1,2},{2,3},{3,4},{4,5},{5,6},{6,7},{7,8},{8,9},{9,10},{10,1... | collective-permute-start | bytes 147464 | tf_op jit(solution)/shard_map/ppermute | solution.py:19
  5.9 1.3 %collective-permute-start.1 = (bf16[3,32,256]{2,1,0:T(8,128)(2,1)S(1)}, bf16[3,32,256]{2,1,0:T(8,128)(2,1)S(1)}, u32[]{:S(2)}, u32[]{:S(2)}) collective-permute-start(bf16[3,32,256]{2,1,0:T(8,128)(2,1)S(1)} %get-tuple-element.35), channel_id=1, source_target_pairs={{1,0},{2,1},{3,2},{4,3},{5,4},{6,5},{7,6},{8,7},{9,8},{10,9},{11,1... | collective-permute-start | bytes 147464 | tf_op jit(solution)/shard_map/ppermute | solution.py:20
  7.2 0.8 fusion.65
  8.0 0.9 fusion.49
  9.0 1.0 fusion.64
  10.2 1.0 fusion.63
  13.1 0.9 fusion.22
  14.0 0.6 pad_slice_fusion.1
  14.6 0.8 fusion.61
  15.4 0.8 fusion.62
  16.2 1.2 fusion.21
  19.0 0.8 add_convert_fusion
  20.1 0.8 copy.84
  20.9 9.2 %all-to-all-start = ((bf16[2,4,32,256]{3,1,0,2:T(4,128)(2,1)}), bf16[2,4,32,256]{3,1,0,2:T(4,128)(2,1)S(1)}, u32[]{:S(2)}, u32[]{:S(2)}) async-start(bf16[2,4,32,256]{3,1,0,2:T(4,128)(2,1)} %copy.84), calls=%async_computation | async-start | bytes 262144 | tf_op jit(solution)/shard_map/all_to_all | solution.py:159
  30.7 0.7 dynamic-slice_convert_fusion
  31.5 6.9 %all-to-all-done = bf16[2,4,32,256]{3,1,0,2:T(4,128)(2,1)S(1)} async-done(((bf16[2,4,32,256]{3,1,0,2:T(4,128)(2,1)}), bf16[2,4,32,256]{3,1,0,2:T(4,128)(2,1)S(1)}, u32[]{:S(2)}, u32[]{:S(2)}) %all-to-all-start) | async-done | bytes 131104 | tf_op jit(solution)/shard_map/all_to_all | solution.py:159
  38.7 2.3 %fusion.1 = (f32[16,4,4,256]{3,2,1,0:T(4,128)S(1)}, f32[4,4,256]{2,1,0:T(4,128)S(1)}) fusion(f32[16,4,4,256]{3,0,2,1:T(8,128)S(1)} %copy.87, f32[16,4,4,256]{3,2,1,0:T(4,128)S(1)} %bitcast.173), kind=kLoop, calls=%fused_computation.3 | loop fusion | flops 5173248 | bytes 802816 | tf_op jit(solution)/shard_map/reduce_sum | solution.py:167
  40.9 0.9 multiply_convert_fusion
  41.8 4.3 %all-to-all-start.1 = ((bf16[16,4,4,256]{3,2,1,0:T(4,128)(2,1)}), bf16[16,4,4,256]{3,2,1,0:T(4,128)(2,1)S(1)}, u32[]{:S(2)}, u32[]{:S(2)}) async-start(bf16[16,4,4,256]{3,2,1,0:T(4,128)(2,1)} %multiply_convert_fusion), calls=%async_computation.1 | async-start | bytes 262144 | tf_op jit(solution)/shard_map/all_to_all | solution.py:178
  46.2 8.7 %all-to-all-done.1 = bf16[16,4,4,256]{3,2,1,0:T(4,128)(2,1)S(1)} async-done(((bf16[16,4,4,256]{3,2,1,0:T(4,128)(2,1)}), bf16[16,4,4,256]{3,2,1,0:T(4,128)(2,1)S(1)}, u32[]{:S(2)}, u32[]{:S(2)}) %all-to-all-start.1) | async-done | bytes 131104 | tf_op jit(solution)/shard_map/all_to_all | solution.py:178
  55.2 0.9 fusion.29
  59.6 1.3 %collective-permute-start.2 = (f32[81920]{0:T(1024)S(1)}, f32[81920]{0:T(1024)S(1)}, u32[]{:S(2)}, u32[]{:S(2)}) collective-permute-start(f32[81920]{0:T(1024)S(1)} %slice_select_fusion), channel_id=1, source_target_pairs={{0,32},{32,0},{1,33},{33,1},{2,34},{34,2},{3,35},{35,3},{4,36},{36... | collective-permute-start | bytes 983048 | tf_op jit(solution)/shard_map/ppermute | solution.py:93
  60.9 1.3 %collective-permute-done.2 = f32[81920]{0:T(1024)S(1)} collective-permute-done((f32[81920]{0:T(1024)S(1)}, f32[81920]{0:T(1024)S(1)}, u32[]{:S(2)}, u32[]{:S(2)}) %collective-permute-start.2) | collective-permute-done | bytes 327712 | tf_op jit(solution)/shard_map/ppermute | solution.py:93
  62.2 26.9 %all_to_all.42 = f32[128,1,640]{2,1,0:T(1,128)S(1)} all-to-all(f32[128,1,640]{2,1,0:T(1,128)S(1)} %bitcast.178), channel_id=1, replica_groups=mesh['group'=4,'core'=2,'tile'=32] {'group','tile'}, dimensions={0} | all-to-all | bytes 655360 | tf_op jit(solution)/shard_map/all_to_all | solution.py:94
  89.4 0.9 broadcast_in_dim.29
  90.3 6.2 %all-to-all-start.3 = ((f32[128,1,640]{2,1,0:T(1,128)}), f32[128,1,640]{2,1,0:T(1,128)S(1)}, u32[]{:S(2)}, u32[]{:S(2)}) async-start(f32[128,1,640]{2,1,0:T(1,128)} %broadcast_in_dim.29), calls=%async_computation.3 | async-start | bytes 655360 | tf_op jit(solution)/shard_map/all_to_all | solution.py:96
  96.5 13.9 %all-to-all-done.3 = f32[128,1,640]{2,1,0:T(1,128)S(1)} async-done(((f32[128,1,640]{2,1,0:T(1,128)}), f32[128,1,640]{2,1,0:T(1,128)S(1)}, u32[]{:S(2)}, u32[]{:S(2)}) %all-to-all-start.3) | async-done | bytes 327712 | tf_op jit(solution)/shard_map/all_to_all | solution.py:96
  110.4 3.5 %collective-permute-start.3 = (f32[81920]{0:T(1024)S(1)}, f32[81920]{0:T(1024)S(1)}, u32[]{:S(2)}, u32[]{:S(2)}) collective-permute-start(f32[81920]{0:T(1024)S(1)} %bitcast.174), channel_id=1, source_target_pairs={{0,32},{32,0},{1,33},{33,1},{2,34},{34,2},{3,35},{35,3},{4,36},{36... | collective-permute-start | bytes 983048 | tf_op jit(solution)/shard_map/ppermute | solution.py:98
  113.9 0.6 copy.100
  115.1 0.9 slice.193
  116.5 0.6 fusion.45
  (61 shorter events, 9.5 us)
Async XLA Ops:
  0.6 8.3 %copy-start = (f32[16,256]{1,0:T(8,128)S(1)}, f32[16,256]{1,0:T(8,128)}, u32[]{:S(2)}) copy-start(f32[16,256]{1,0:T(8,128)} %param.16) | copy-start | bytes 49156
  0.6 10.6 %copy-start.1 = (bf16[4,32,256]{2,1,0:T(8,128)(2,1)S(1)}, bf16[4,32,256]{2,1,0:T(8,128)(2,1)}, u32[]{:S(2)}) copy-start(bf16[4,32,256]{2,1,0:T(8,128)(2,1)} %param.11) | copy-start | bytes 196612
  1.6 9.6 %collective-permute-start = (bf16[3,32,256]{2,1,0:T(8,128)(2,1)S(1)}, bf16[3,32,256]{2,1,0:T(8,128)(2,1)S(1)}, u32[]{:S(2)}, u32[]{:S(2)}) collective-permute-start(bf16[3,32,256]{2,1,0:T(8,128)(2,1)S(1)} %get-tuple-element.36), channel_id=1, source_target_pairs={{0,1},{1,2},{2,3},{3,4},{4,5},{5,6},{6,7},{7,8},{8,9},{9,10},{10,1... | collective-permute-start | bytes 147464 | tf_op jit(solution)/shard_map/ppermute | solution.py:19
  5.9 5.3 %collective-permute-start.1 = (bf16[3,32,256]{2,1,0:T(8,128)(2,1)S(1)}, bf16[3,32,256]{2,1,0:T(8,128)(2,1)S(1)}, u32[]{:S(2)}, u32[]{:S(2)}) collective-permute-start(bf16[3,32,256]{2,1,0:T(8,128)(2,1)S(1)} %get-tuple-element.35), channel_id=1, source_target_pairs={{1,0},{2,1},{3,2},{4,3},{5,4},{6,5},{7,6},{8,7},{9,8},{10,9},{11,1... | collective-permute-start | bytes 147464 | tf_op jit(solution)/shard_map/ppermute | solution.py:20
  18.9 0.9 copy-start.2
  19.0 0.9 copy-start.3
  20.9 17.5 %all-to-all-start = ((bf16[2,4,32,256]{3,1,0,2:T(4,128)(2,1)}), bf16[2,4,32,256]{3,1,0,2:T(4,128)(2,1)S(1)}, u32[]{:S(2)}, u32[]{:S(2)}) async-start(bf16[2,4,32,256]{3,1,0,2:T(4,128)(2,1)} %copy.84), calls=%async_computation | async-start | bytes 262144 | tf_op jit(solution)/shard_map/all_to_all | solution.py:159
  41.8 13.1 %all-to-all-start.1 = ((bf16[16,4,4,256]{3,2,1,0:T(4,128)(2,1)}), bf16[16,4,4,256]{3,2,1,0:T(4,128)(2,1)S(1)}, u32[]{:S(2)}, u32[]{:S(2)}) async-start(bf16[16,4,4,256]{3,2,1,0:T(4,128)(2,1)} %multiply_convert_fusion), calls=%async_computation.1 | async-start | bytes 262144 | tf_op jit(solution)/shard_map/all_to_all | solution.py:178
  59.6 2.6 %collective-permute-start.2 = (f32[81920]{0:T(1024)S(1)}, f32[81920]{0:T(1024)S(1)}, u32[]{:S(2)}, u32[]{:S(2)}) collective-permute-start(f32[81920]{0:T(1024)S(1)} %slice_select_fusion), channel_id=1, source_target_pairs={{0,32},{32,0},{1,33},{33,1},{2,34},{34,2},{3,35},{35,3},{4,36},{36... | collective-permute-start | bytes 983048 | tf_op jit(solution)/shard_map/ppermute | solution.py:93
  90.3 20.1 %all-to-all-start.3 = ((f32[128,1,640]{2,1,0:T(1,128)}), f32[128,1,640]{2,1,0:T(1,128)S(1)}, u32[]{:S(2)}, u32[]{:S(2)}) async-start(f32[128,1,640]{2,1,0:T(1,128)} %broadcast_in_dim.29), calls=%async_computation.3 | async-start | bytes 655360 | tf_op jit(solution)/shard_map/all_to_all | solution.py:96
  110.4 4.7 %collective-permute-start.3 = (f32[81920]{0:T(1024)S(1)}, f32[81920]{0:T(1024)S(1)}, u32[]{:S(2)}, u32[]{:S(2)}) collective-permute-start(f32[81920]{0:T(1024)S(1)} %bitcast.174), channel_id=1, source_target_pairs={{0,32},{32,0},{1,33},{33,1},{2,34},{34,2},{3,35},{35,3},{4,36},{36... | collective-permute-start | bytes 983048 | tf_op jit(solution)/shard_map/ppermute | solution.py:98

commit v9 on v8

--- a/solution.py
+++ b/solution.py
@@ -184,20 +184,18 @@
     unused_out, pullback = jax.vjp(jax.nn.gelu, final_linear_response)
     d_pre = pullback(back)[0].astype(jnp.bfloat16)
     second_wide = jnp.pad(second_padded, ((0, 0), (0, 0), (1, 1), (0, 0)))
-    rows_of = []
-    for i in range(3):
-        cols_of = []
-        for j in range(3):
-            cols_of.append(
-                jnp.einsum(
-                    "mrwc,mrwd->cd",
-                    second_wide[:, i : i + row_count, j : j + col_count],
-                    d_pre,
-                    preferred_element_type=jnp.float32,
-                )
-            )
-        rows_of.append(jnp.stack(cols_of))
-    conv_grad = jnp.stack(rows_of)
+    second_shifted = jnp.concatenate([second_wide[:, :, j : j + col_count] for j in range(3)], axis=3)
+    conv_grad = jnp.stack(
+        [
+            jnp.einsum(
+                "mrwk,mrwd->kd",
+                second_shifted[:, i : i + row_count],
+                d_pre,
+                preferred_element_type=jnp.float32,
+            ).reshape(conv_out.shape[1:])
+            for i in range(3)
+        ]
+    )
     conv_grad, head_grad_t, bias_grad = all_reduce_sum((conv_grad, head_grad.T, bias_grad))
     head_grad = head_grad_t.T
     return (crps_map, conv_grad, head_grad, bias_grad)

time: 118 us -> 119 us (level)
    dot_general x9 -> x3, matrix products: 3.11 us -> 1.82 us  [on_device(): jnp.einsum('mrwk,mrwd->kd', second_shifted[:, i:i + row_count], d_pre, pr...]
    dot_general x1, matrix products: 0.89 us -> 2.11 us  [on_device(): jnp.einsum('mrvw,cv->mrwc', cotangent, head_weight, preferred_element_typ...]
where the time goes in v9:
time: 119 us
  waiting for transfers between devices  31.3 us (26%)
  starting transfers between devices  29.5 us (25%)
  blocking collectives  27.1 us (23%)
  matrix products  12.1 us (10%)
  local copies, waits for them, and re-layouts  10.5 us (9%)
  other arithmetic  6.43 us (5%)
  between operations  1.64 us (1%)
    all_to_all x1, blocking collectives, all_reduce_sum(): lax.all_to_all(half.reshape(devices, width), peers, 0, 0, tiled=True)  27.1 us
    all_to_all x1, waiting for transfers between devices, all_reduce_sum(): lax.all_to_all(jnp.broadcast_to(own, (devices, width)), peers, 0, 0, tile...  13.9 us
    all_to_all x1, waiting for transfers between devices, on_device(): lax.all_to_all(cot_share, MEMBER, split_axis=0, concat_axis=2, tiled=True)  8.71 us
    all_to_all x1, starting transfers between devices, on_device(): lax.all_to_all(sample_prediction, MEMBER, split_axis=2, concat_axis=0, ti...  8.53 us
    all_to_all x1, waiting for transfers between devices, on_device(): lax.all_to_all(sample_prediction, MEMBER, split_axis=2, concat_axis=0, ti...  6.9 us
    all_to_all x1, starting transfers between devices, all_reduce_sum(): lax.all_to_all(jnp.broadcast_to(own, (devices, width)), peers, 0, 0, tile...  6.18 us
    dot_general x6, matrix products, feature_conv(): jnp.einsum('mrwc,cd->mrwd', shifted[:, i:i + out_rows], kernel[i].reshape...  5.64 us
    ppermute x1, starting transfers between devices, extended(): before = lax.ppermute(last, axis, up)  4.35 us
  transfers between devices with their start and end apart: 7, of which 5 were waited for; matrix products, arithmetic and copies ran while one was open for 5% of the time, Pallas kernels for 0%

profile of v9, /device:TPU:1, one launch (start us, length us, event | category | flops | bytes accessed | tf_op | source)
XLA Modules:
  0.0 118.5 jit_solution(14653790734756906824)
XLA Ops:
  0.7 0.9 fusion.52
  1.6 4.3 %collective-permute-start = (bf16[3,32,256]{2,1,0:T(8,128)(2,1)S(1)}, bf16[3,32,256]{2,1,0:T(8,128)(2,1)S(1)}, u32[]{:S(2)}, u32[]{:S(2)}) collective-permute-start(bf16[3,32,256]{2,1,0:T(8,128)(2,1)S(1)} %get-tuple-element.36), channel_id=1, source_target_pairs={{0,1},{1,2},{2,3},{3,4},{4,5},{5,6},{6,7},{7,8},{8,9},{9,10},{10,1... | collective-permute-start | bytes 147464 | tf_op jit(solution)/shard_map/ppermute | solution.py:19
  5.9 1.3 %collective-permute-start.1 = (bf16[3,32,256]{2,1,0:T(8,128)(2,1)S(1)}, bf16[3,32,256]{2,1,0:T(8,128)(2,1)S(1)}, u32[]{:S(2)}, u32[]{:S(2)}) collective-permute-start(bf16[3,32,256]{2,1,0:T(8,128)(2,1)S(1)} %get-tuple-element.35), channel_id=1, source_target_pairs={{1,0},{2,1},{3,2},{4,3},{5,4},{6,5},{7,6},{8,7},{9,8},{10,9},{11,1... | collective-permute-start | bytes 147464 | tf_op jit(solution)/shard_map/ppermute | solution.py:20
  7.2 0.8 fusion.50
  8.0 0.9 fusion.37
  9.0 1.0 fusion.49
  10.2 1.6 %fusion.48 = (bf16[1,3,128,128]{3,2,1,0:T(8,128)(2,1)S(1)}, bf16[1,3,128,128]{3,2,1,0:T(8,128)(2,1)}, bf16[1,3,128,128]{3,2,1,0:T(8,128)(2,1)S(1)}) fusion(bf16[3,3,128,128]{3,2,1,0:T(8,128)(2,1)} %param.19), kind=kLoop, calls=%fused_computation.98 | loop fusion | bytes 589824 | tf_op jit(solution)/shard_map/slice | solution.py:51
  13.7 0.9 fusion.22
  15.2 0.8 fusion.42
  16.0 0.8 fusion.43
  16.8 1.2 fusion.21
  20.1 1.8 %add_convert_fusion = (bf16[2,4,256,128]{3,2,1,0:T(8,128)(2,1)S(1)}, f32[2,4,256,128]{3,2,1,0:T(8,128)}) fusion(bf16[2,8,256,128]{3,2,1,0:T(8,128)(2,1)S(1)} %fusion.22, f32[2,4,256,128]{3,2,1,0:T(8,128)S(1)} %convolution_add_fusion.1, bf16[384,128,1,1]{1,0,3,2:T(8,128)(2,1)S(1)} %bitcast.134, bf16[2,6,256,128]{3,2,1,0:T(8,128)(2,1)S(1)} %get-tuple-element.21, ...), kind=kOutput, calls=%fused_computation.44 | convolution fusion | flops 211550208 | bytes 5603328 | tf_op jit(solution)/shard_map/mrwc,cd->mrwd/dot_general | solution.py:48
  22.1 0.8 copy.54
  22.9 8.5 %all-to-all-start = ((bf16[2,4,32,256]{3,1,0,2:T(4,128)(2,1)}), bf16[2,4,32,256]{3,1,0,2:T(4,128)(2,1)S(1)}, u32[]{:S(2)}, u32[]{:S(2)}) async-start(bf16[2,4,32,256]{3,1,0,2:T(4,128)(2,1)} %copy.54), calls=%async_computation | async-start | bytes 262144 | tf_op jit(solution)/shard_map/all_to_all | solution.py:159
  32.1 0.7 dynamic-slice_convert_fusion
  32.9 6.9 %all-to-all-done = bf16[2,4,32,256]{3,1,0,2:T(4,128)(2,1)S(1)} async-done(((bf16[2,4,32,256]{3,1,0,2:T(4,128)(2,1)}), bf16[2,4,32,256]{3,1,0,2:T(4,128)(2,1)S(1)}, u32[]{:S(2)}, u32[]{:S(2)}) %all-to-all-start) | async-done | bytes 131104 | tf_op jit(solution)/shard_map/all_to_all | solution.py:159
  40.1 2.3 %fusion.1 = (f32[16,4,4,256]{3,2,1,0:T(4,128)S(1)}, f32[4,4,256]{2,1,0:T(4,128)S(1)}) fusion(f32[16,4,4,256]{3,0,2,1:T(8,128)S(1)} %copy.57, f32[16,4,4,256]{3,2,1,0:T(4,128)S(1)} %bitcast.119), kind=kLoop, calls=%fused_computation.3 | loop fusion | flops 5173248 | bytes 802816 | tf_op jit(solution)/shard_map/reduce_sum | solution.py:167
  42.3 0.9 multiply_convert_fusion
  43.2 4.3 %all-to-all-start.1 = ((bf16[16,4,4,256]{3,2,1,0:T(4,128)(2,1)}), bf16[16,4,4,256]{3,2,1,0:T(4,128)(2,1)S(1)}, u32[]{:S(2)}, u32[]{:S(2)}) async-start(bf16[16,4,4,256]{3,2,1,0:T(4,128)(2,1)} %multiply_convert_fusion), calls=%async_computation.1 | async-start | bytes 262144 | tf_op jit(solution)/shard_map/all_to_all | solution.py:178
  47.6 8.7 %all-to-all-done.1 = bf16[16,4,4,256]{3,2,1,0:T(4,128)(2,1)S(1)} async-done(((bf16[16,4,4,256]{3,2,1,0:T(4,128)(2,1)}), bf16[16,4,4,256]{3,2,1,0:T(4,128)(2,1)S(1)}, u32[]{:S(2)}, u32[]{:S(2)}) %all-to-all-start.1) | async-done | bytes 131104 | tf_op jit(solution)/shard_map/all_to_all | solution.py:178
  56.6 2.1 %fusion.29 = bf16[2,4,256,128]{3,2,1,0:T(8,128)(2,1)S(1)} fusion(f32[2,4,256,128]{3,2,1,0:T(8,128)} %get-tuple-element.42, bf16[2,4,32,256]{3,2,1,0:T(8,128)(2,1)S(1)} %all_to_all.34, bf16[128,32]{0,1:T(8,128)(2,1)S(1)} %copy-done.3), kind=kOutput, calls=%fused_computation.43 | convolution fusion | flops 22020096 | bytes 1712128 | tf_op jit(solution)/shard_map/mrvw,cv->mrwc/dot_general | solution.py:183
  59.3 0.6 fusion.46
  60.9 1.3 %collective-permute-start.2 = (f32[81920]{0:T(1024)S(1)}, f32[81920]{0:T(1024)S(1)}, u32[]{:S(2)}, u32[]{:S(2)}) collective-permute-start(f32[81920]{0:T(1024)S(1)} %slice_select_fusion), channel_id=1, source_target_pairs={{0,32},{32,0},{1,33},{33,1},{2,34},{34,2},{3,35},{35,3},{4,36},{36... | collective-permute-start | bytes 983048 | tf_op jit(solution)/shard_map/ppermute | solution.py:93
  62.2 1.3 %collective-permute-done.2 = f32[81920]{0:T(1024)S(1)} collective-permute-done((f32[81920]{0:T(1024)S(1)}, f32[81920]{0:T(1024)S(1)}, u32[]{:S(2)}, u32[]{:S(2)}) %collective-permute-start.2) | collective-permute-done | bytes 327712 | tf_op jit(solution)/shard_map/ppermute | solution.py:93
  63.5 27.1 %all_to_all.42 = f32[128,1,640]{2,1,0:T(1,128)S(1)} all-to-all(f32[128,1,640]{2,1,0:T(1,128)S(1)} %bitcast.124), channel_id=1, replica_groups=mesh['group'=4,'core'=2,'tile'=32] {'group','tile'}, dimensions={0} | all-to-all | bytes 655360 | tf_op jit(solution)/shard_map/all_to_all | solution.py:94
  90.8 0.9 broadcast_in_dim.29
  91.7 6.2 %all-to-all-start.3 = ((f32[128,1,640]{2,1,0:T(1,128)}), f32[128,1,640]{2,1,0:T(1,128)S(1)}, u32[]{:S(2)}, u32[]{:S(2)}) async-start(f32[128,1,640]{2,1,0:T(1,128)} %broadcast_in_dim.29), calls=%async_computation.3 | async-start | bytes 655360 | tf_op jit(solution)/shard_map/all_to_all | solution.py:96
  97.9 13.9 %all-to-all-done.3 = f32[128,1,640]{2,1,0:T(1,128)S(1)} async-done(((f32[128,1,640]{2,1,0:T(1,128)}), f32[128,1,640]{2,1,0:T(1,128)S(1)}, u32[]{:S(2)}, u32[]{:S(2)}) %all-to-all-start.3) | async-done | bytes 327712 | tf_op jit(solution)/shard_map/all_to_all | solution.py:96
  111.8 3.5 %collective-permute-start.3 = (f32[81920]{0:T(1024)S(1)}, f32[81920]{0:T(1024)S(1)}, u32[]{:S(2)}, u32[]{:S(2)}) collective-permute-start(f32[81920]{0:T(1024)S(1)} %bitcast.120), channel_id=1, source_target_pairs={{0,32},{32,0},{1,33},{33,1},{2,34},{34,2},{3,35},{35,3},{4,36},{36... | collective-permute-start | bytes 983048 | tf_op jit(solution)/shard_map/ppermute | solution.py:98
  115.3 0.6 copy.64
  116.5 0.9 slice.160
  117.9 0.6 fusion.33
  (55 shorter events, 8.6 us)
Async XLA Ops:
  0.6 8.3 %copy-start = (f32[16,256]{1,0:T(8,128)S(1)}, f32[16,256]{1,0:T(8,128)}, u32[]{:S(2)}) copy-start(f32[16,256]{1,0:T(8,128)} %param.16) | copy-start | bytes 49156
  0.6 11.2 %copy-start.1 = (bf16[4,32,256]{2,1,0:T(8,128)(2,1)S(1)}, bf16[4,32,256]{2,1,0:T(8,128)(2,1)}, u32[]{:S(2)}) copy-start(bf16[4,32,256]{2,1,0:T(8,128)(2,1)} %param.11) | copy-start | bytes 196612
  1.6 10.3 %collective-permute-start = (bf16[3,32,256]{2,1,0:T(8,128)(2,1)S(1)}, bf16[3,32,256]{2,1,0:T(8,128)(2,1)S(1)}, u32[]{:S(2)}, u32[]{:S(2)}) collective-permute-start(bf16[3,32,256]{2,1,0:T(8,128)(2,1)S(1)} %get-tuple-element.36), channel_id=1, source_target_pairs={{0,1},{1,2},{2,3},{3,4},{4,5},{5,6},{6,7},{7,8},{8,9},{9,10},{10,1... | collective-permute-start | bytes 147464 | tf_op jit(solution)/shard_map/ppermute | solution.py:19
  5.9 6.0 %collective-permute-start.1 = (bf16[3,32,256]{2,1,0:T(8,128)(2,1)S(1)}, bf16[3,32,256]{2,1,0:T(8,128)(2,1)S(1)}, u32[]{:S(2)}, u32[]{:S(2)}) collective-permute-start(bf16[3,32,256]{2,1,0:T(8,128)(2,1)S(1)} %get-tuple-element.35), channel_id=1, source_target_pairs={{1,0},{2,1},{3,2},{4,3},{5,4},{6,5},{7,6},{8,7},{9,8},{10,9},{11,1... | collective-permute-start | bytes 147464 | tf_op jit(solution)/shard_map/ppermute | solution.py:20
  18.0 0.9 copy-start.2
  20.0 1.8 %copy-start.3 = (bf16[128,32]{0,1:T(8,128)(2,1)S(1)}, bf16[128,32]{0,1:T(8,128)(2,1)}, u32[]{:S(2)}) copy-start(bf16[128,32]{0,1:T(8,128)(2,1)} %param.20) | copy-start | bytes 24580
  20.0 1.8 %copy-start.4 = (f32[32]{0:T(128)S(1)}, f32[32]{0:T(128)}, u32[]{:S(2)}) copy-start(f32[32]{0:T(128)} %param.21) | copy-start | bytes 388
  22.9 16.9 %all-to-all-start = ((bf16[2,4,32,256]{3,1,0,2:T(4,128)(2,1)}), bf16[2,4,32,256]{3,1,0,2:T(4,128)(2,1)S(1)}, u32[]{:S(2)}, u32[]{:S(2)}) async-start(bf16[2,4,32,256]{3,1,0,2:T(4,128)(2,1)} %copy.54), calls=%async_computation | async-start | bytes 262144 | tf_op jit(solution)/shard_map/all_to_all | solution.py:159
  43.2 13.1 %all-to-all-start.1 = ((bf16[16,4,4,256]{3,2,1,0:T(4,128)(2,1)}), bf16[16,4,4,256]{3,2,1,0:T(4,128)(2,1)S(1)}, u32[]{:S(2)}, u32[]{:S(2)}) async-start(bf16[16,4,4,256]{3,2,1,0:T(4,128)(2,1)} %multiply_convert_fusion), calls=%async_computation.1 | async-start | bytes 262144 | tf_op jit(solution)/shard_map/all_to_all | solution.py:178
  60.9 2.6 %collective-permute-start.2 = (f32[81920]{0:T(1024)S(1)}, f32[81920]{0:T(1024)S(1)}, u32[]{:S(2)}, u32[]{:S(2)}) collective-permute-start(f32[81920]{0:T(1024)S(1)} %slice_select_fusion), channel_id=1, source_target_pairs={{0,32},{32,0},{1,33},{33,1},{2,34},{34,2},{3,35},{35,3},{4,36},{36... | collective-permute-start | bytes 983048 | tf_op jit(solution)/shard_map/ppermute | solution.py:93
  91.7 20.1 %all-to-all-start.3 = ((f32[128,1,640]{2,1,0:T(1,128)}), f32[128,1,640]{2,1,0:T(1,128)S(1)}, u32[]{:S(2)}, u32[]{:S(2)}) async-start(f32[128,1,640]{2,1,0:T(1,128)} %broadcast_in_dim.29), calls=%async_computation.3 | async-start | bytes 655360 | tf_op jit(solution)/shard_map/all_to_all | solution.py:96
  111.8 4.7 %collective-permute-start.3 = (f32[81920]{0:T(1024)S(1)}, f32[81920]{0:T(1024)S(1)}, u32[]{:S(2)}, u32[]{:S(2)}) collective-permute-start(f32[81920]{0:T(1024)S(1)} %bitcast.120), channel_id=1, source_target_pairs={{0,32},{32,0},{1,33},{33,1},{2,34},{34,2},{3,35},{35,3},{4,36},{36... | collective-permute-start | bytes 983048 | tf_op jit(solution)/shard_map/ppermute | solution.py:98

commit v10 on v8

--- a/solution.py
+++ b/solution.py
@@ -144,43 +144,46 @@
         first_hidden.astype(jnp.float32) + jax.nn.gelu(final_linear_response)
     ).astype(jnp.bfloat16)
     final_layer_result = jnp.einsum(
-        "mrwc,cv->mrvw", latent_layer_three, head_weight, preferred_element_type=jnp.float32
+        "mrwc,cv->vmrw", latent_layer_three, head_weight, preferred_element_type=jnp.float32
     )
     sample_prediction = (
         final_layer_result
-        + upsampled_coarse.astype(jnp.float32)[None]
-        + per_quantity_offset[None, None, :, None]
+        + jnp.transpose(upsampled_coarse, (1, 0, 2)).astype(jnp.float32)[:, None]
+        + per_quantity_offset[:, None, None, None]
     ).astype(jnp.bfloat16)
     row_global = band_row[0] + tile_at * row_count + jnp.arange(row_count, dtype=jnp.int32)
     latitude = math.pi * (row_global.astype(jnp.float32) + 0.5) / GRID_ROWS - math.pi / 2
-    row_factor = (jnp.cos(latitude) / (band_rows * col_count))[None, :, None, None]
+    row_factor = (jnp.cos(latitude) / (band_rows * col_count))[None, None, :, None]
     var_share = var_count // (lax.axis_size("group") * lax.axis_size("core"))
     var_start = lax.axis_index(MEMBER) * var_share
     collected_members = lax.all_to_all(
-        sample_prediction, MEMBER, split_axis=2, concat_axis=0, tiled=True
+        sample_prediction, MEMBER, split_axis=0, concat_axis=1, tiled=True
     )
     sample_group_predictions = collected_members.astype(jnp.float32)
-    member_count = sample_group_predictions.shape[0]
-    truth = lax.dynamic_slice_in_dim(target, var_start, var_share, 1).astype(jnp.float32)
-    pair_differ = sample_group_predictions[:, None] - sample_group_predictions[None, :]
-    abs_sums = jnp.sum(jnp.abs(pair_differ), axis=1)
-    sign_sums = jnp.sum(jnp.sign(pair_differ), axis=1)
-    crps_map = jnp.mean(jnp.abs(sample_group_predictions - truth[None]), axis=0) - jnp.sum(
-        abs_sums, axis=0
+    member_count = sample_group_predictions.shape[1]
+    truth = jnp.transpose(
+        lax.dynamic_slice_in_dim(target, var_start, var_share, 1), (1, 0, 2)
+    ).astype(jnp.float32)[:, None]
+    pair_differ = sample_group_predictions[:, :, None] - sample_group_predictions[:, None, :]
+    abs_sums = jnp.sum(jnp.abs(pair_differ), axis=2)
+    sign_sums = jnp.sum(jnp.sign(pair_differ), axis=2)
+    crps_share = jnp.mean(jnp.abs(sample_group_predictions - truth), axis=1) - jnp.sum(
+        abs_sums, axis=1
     ) / (2 * member_count * (member_count - 1))
+    crps_map = jnp.transpose(crps_share, (1, 0, 2))
     cot_share = (
         row_factor
         * (
-            jnp.sign(sample_group_predictions - truth[None]) / member_count
+            jnp.sign(sample_group_predictions - truth) / member_count
             - sign_sums / (member_count * (member_count - 1))
         )
     ).astype(jnp.bfloat16)
-    cotangent = lax.all_to_all(cot_share, MEMBER, split_axis=0, concat_axis=2, tiled=True)
+    cotangent = lax.all_to_all(cot_share, MEMBER, split_axis=1, concat_axis=0, tiled=True)
     head_grad = jnp.einsum(
-        "mrwc,mrvw->cv", latent_layer_three, cotangent, preferred_element_type=jnp.float32
-    )
-    bias_grad = jnp.sum(cotangent.astype(jnp.float32), axis=(0, 1, 3))
-    back = jnp.einsum("mrvw,cv->mrwc", cotangent, head_weight, preferred_element_type=jnp.float32)
+        "mrwc,vmrw->cv", latent_layer_three, cotangent, preferred_element_type=jnp.float32
+    )
+    bias_grad = jnp.sum(cotangent.astype(jnp.float32), axis=(1, 2, 3))
+    back = jnp.einsum("vmrw,cv->mrwc", cotangent, head_weight, preferred_element_type=jnp.float32)
     unused_out, pullback = jax.vjp(jax.nn.gelu, final_linear_response)
     d_pre = pullback(back)[0].astype(jnp.bfloat16)
     second_wide = jnp.pad(second_padded, ((0, 0), (0, 0), (1, 1), (0, 0)))

time: 118 us -> 117 us (level)
  blocking collectives: 26.9 us -> 46.7 us
  waiting for transfers between devices: 31.3 us -> 17.4 us
  starting transfers between devices: 30.1 us -> 23.8 us
    all_to_all x0 -> x1, blocking collectives: none -> 19.7 us  [all_reduce_sum(): lax.all_to_all(jnp.broadcast_to(own, (devices, width)), peers, 0, 0, tile...]
    all_to_all x3 -> x2, waiting for transfers between devices: 29.5 us -> 15.6 us  [the longest x1 8.71 us: on_device(): lax.all_to_all(cot_share, MEMBER, split_axis=1, concat_axis=0, tiled=True)]
    all_to_all x3 -> x2, starting transfers between devices: 19.7 us -> 13.5 us  [the longest x1 9.16 us: on_device(): lax.all_to_all(sample_prediction, MEMBER, split_axis=0, concat_axis=1, ti...]
  transfers between devices with their start and end apart: 7 -> 6, of which waited for: 5 -> 4; matrix products, arithmetic and copies ran while one was open for 5% -> 5% of each run, Pallas kernels for 0% -> 0%
where the time goes in v10:
time: 117 us; the launch traced here: 116 us
  blocking collectives  46.7 us (40%)
  starting transfers between devices  23.8 us (20%)
  waiting for transfers between devices  17.4 us (15%)
  matrix products  11.2 us (10%)
  local copies, waits for them, and re-layouts  9.33 us (8%)
  other arithmetic  5.84 us (5%)
  between operations  1.71 us (1%)
    all_to_all x1, blocking collectives, all_reduce_sum(): lax.all_to_all(half.reshape(devices, width), peers, 0, 0, tiled=True)  27 us
    all_to_all x1, blocking collectives, all_reduce_sum(): lax.all_to_all(jnp.broadcast_to(own, (devices, width)), peers, 0, 0, tile...  19.7 us
    all_to_all x1, starting transfers between devices, on_device(): lax.all_to_all(sample_prediction, MEMBER, split_axis=0, concat_axis=1, ti...  9.16 us
    all_to_all x1, waiting for transfers between devices, on_device(): lax.all_to_all(cot_share, MEMBER, split_axis=1, concat_axis=0, tiled=True)  8.71 us
    all_to_all x1, waiting for transfers between devices, on_device(): lax.all_to_all(sample_prediction, MEMBER, split_axis=0, concat_axis=1, ti...  6.9 us
    dot_general x6, matrix products, feature_conv(): jnp.einsum('mrwc,cd->mrwd', shifted[:, i:i + out_rows], kernel[i].reshape...  4.7 us
    ppermute x1, starting transfers between devices, extended(): before = lax.ppermute(last, axis, up)  4.35 us
    all_to_all x1, starting transfers between devices, on_device(): lax.all_to_all(cot_share, MEMBER, split_axis=1, concat_axis=0, tiled=True)  4.34 us
  transfers between devices with their start and end apart: 6, of which 4 were waited for; matrix products, arithmetic and copies ran while one was open for 5% of the time, Pallas kernels for 0%

profile of v10, /device:TPU:1, one launch (start us, length us, event | category | flops | bytes accessed | tf_op | source)
XLA Modules:
  0.0 116.0 jit_solution(6540962450538911732)
XLA Ops:
  0.7 0.9 fusion.65
  1.6 4.3 %collective-permute-start = (bf16[3,32,256]{2,1,0:T(8,128)(2,1)S(1)}, bf16[3,32,256]{2,1,0:T(8,128)(2,1)S(1)}, u32[]{:S(2)}, u32[]{:S(2)}) collective-permute-start(bf16[3,32,256]{2,1,0:T(8,128)(2,1)S(1)} %get-tuple-element.36), channel_id=1, source_target_pairs={{0,1},{1,2},{2,3},{3,4},{4,5},{5,6},{6,7},{7,8},{8,9},{9,10},{10,1... | collective-permute-start | bytes 147464 | tf_op jit(solution)/shard_map/ppermute | solution.py:19
  5.9 1.3 %collective-permute-start.1 = (bf16[3,32,256]{2,1,0:T(8,128)(2,1)S(1)}, bf16[3,32,256]{2,1,0:T(8,128)(2,1)S(1)}, u32[]{:S(2)}, u32[]{:S(2)}) collective-permute-start(bf16[3,32,256]{2,1,0:T(8,128)(2,1)S(1)} %get-tuple-element.35), channel_id=1, source_target_pairs={{1,0},{2,1},{3,2},{4,3},{5,4},{6,5},{7,6},{8,7},{9,8},{10,9},{11,1... | collective-permute-start | bytes 147464 | tf_op jit(solution)/shard_map/ppermute | solution.py:20
  7.2 0.8 fusion.64
  8.0 0.9 fusion.48
  9.0 1.0 fusion.63
  10.2 1.0 fusion.62
  13.1 0.9 fusion.22
  14.0 0.6 pad_slice_fusion.1
  14.6 0.8 fusion.60
  15.4 0.8 fusion.61
  16.2 1.2 fusion.21
  17.8 0.6 fusion.59
  18.3 0.6 convolution_add_fusion.1
  19.0 0.8 add_convert_fusion
  20.1 0.8 copy.97
  20.9 9.2 %all-to-all-start = ((bf16[32,2,4,256]{3,2,1,0:T(4,128)(2,1)}), bf16[32,2,4,256]{3,2,1,0:T(4,128)(2,1)S(1)}, u32[]{:S(2)}, u32[]{:S(2)}) async-start(bf16[32,2,4,256]{3,2,1,0:T(4,128)(2,1)} %copy.97), calls=%async_computation | async-start | bytes 262144 | tf_op jit(solution)/shard_map/all_to_all | solution.py:159
  30.0 0.7 convert_bitcast_fusion.1
  31.5 6.9 %all-to-all-done = bf16[32,2,4,256]{3,2,1,0:T(4,128)(2,1)S(1)} async-done(((bf16[32,2,4,256]{3,2,1,0:T(4,128)(2,1)}), bf16[32,2,4,256]{3,2,1,0:T(4,128)(2,1)S(1)}, u32[]{:S(2)}, u32[]{:S(2)}) %all-to-all-start) | async-done | bytes 131104 | tf_op jit(solution)/shard_map/all_to_all | solution.py:159
  38.5 2.3 %fusion.1 = (f32[4,16,4,256]{3,2,1,0:T(4,128)S(1)}, f32[4,4,256]{2,1,0:T(4,128)S(1)}) fusion(f32[4,16,4,256]{3,1,2,0:T(8,128)S(1)} %copy.100, f32[4,16,4,256]{3,2,1,0:T(4,128)S(1)} %bitcast.181), kind=kLoop, calls=%fused_computation.3 | loop fusion | flops 5173248 | bytes 802816 | tf_op jit(solution)/shard_map/reduce_sum | solution.py:169
  41.0 0.7 copy.102
  41.7 4.3 %all-to-all-start.1 = ((bf16[4,16,4,256]{3,2,0,1:T(4,128)(2,1)}), bf16[4,16,4,256]{3,2,0,1:T(4,128)(2,1)S(1)}, u32[]{:S(2)}, u32[]{:S(2)}) async-start(bf16[4,16,4,256]{3,2,0,1:T(4,128)(2,1)} %copy.102), calls=%async_computation.1 | async-start | bytes 262144 | tf_op jit(solution)/shard_map/all_to_all | solution.py:181
  46.0 8.7 %all-to-all-done.1 = bf16[4,16,4,256]{3,2,0,1:T(4,128)(2,1)S(1)} async-done(((bf16[4,16,4,256]{3,2,0,1:T(4,128)(2,1)}), bf16[4,16,4,256]{3,2,0,1:T(4,128)(2,1)S(1)}, u32[]{:S(2)}, u32[]{:S(2)}) %all-to-all-start.1) | async-done | bytes 131104 | tf_op jit(solution)/shard_map/all_to_all | solution.py:181
  55.0 0.9 fusion.29
  59.6 1.3 %collective-permute-start.2 = (f32[81920]{0:T(1024)S(1)}, f32[81920]{0:T(1024)S(1)}, u32[]{:S(2)}, u32[]{:S(2)}) collective-permute-start(f32[81920]{0:T(1024)S(1)} %slice_select_fusion), channel_id=1, source_target_pairs={{0,32},{32,0},{1,33},{33,1},{2,34},{34,2},{3,35},{35,3},{4,36},{36... | collective-permute-start | bytes 983048 | tf_op jit(solution)/shard_map/ppermute | solution.py:93
  60.9 1.3 %collective-permute-done.2 = f32[81920]{0:T(1024)S(1)} collective-permute-done((f32[81920]{0:T(1024)S(1)}, f32[81920]{0:T(1024)S(1)}, u32[]{:S(2)}, u32[]{:S(2)}) %collective-permute-start.2) | collective-permute-done | bytes 327712 | tf_op jit(solution)/shard_map/ppermute | solution.py:93
  62.2 27.0 %all_to_all.42 = f32[128,1,640]{2,1,0:T(1,128)S(1)} all-to-all(f32[128,1,640]{2,1,0:T(1,128)S(1)} %bitcast.187), channel_id=1, replica_groups=mesh['group'=4,'core'=2,'tile'=32] {'group','tile'}, dimensions={0} | all-to-all | bytes 655360 | tf_op jit(solution)/shard_map/all_to_all | solution.py:94
  89.6 19.7 %all_to_all.43 = f32[128,1,640]{2,1,0:T(1,128)S(1)} all-to-all(f32[128,1,640]{2,1,0:T(1,128)S(1)} %broadcast_in_dim.29), channel_id=1, replica_groups=mesh['group'=4,'core'=2,'tile'=32] {'group','tile'}, dimensions={0} | all-to-all | bytes 655360 | tf_op jit(solution)/shard_map/all_to_all | solution.py:96
  109.4 3.4 %collective-permute-start.3 = (f32[81920]{0:T(1024)S(1)}, f32[81920]{0:T(1024)S(1)}, u32[]{:S(2)}, u32[]{:S(2)}) collective-permute-start(f32[81920]{0:T(1024)S(1)} %bitcast.183), channel_id=1, source_target_pairs={{0,32},{32,0},{1,33},{33,1},{2,34},{34,2},{3,35},{35,3},{4,36},{36... | collective-permute-start | bytes 983048 | tf_op jit(solution)/shard_map/ppermute | solution.py:98
  112.9 0.6 copy.116
  114.0 0.9 slice.193
  115.4 0.6 fusion.45
  (63 shorter events, 8.7 us)
Async XLA Ops:
  0.6 8.3 %copy-start = (f32[16,256]{1,0:T(8,128)S(1)}, f32[16,256]{1,0:T(8,128)}, u32[]{:S(2)}) copy-start(f32[16,256]{1,0:T(8,128)} %param.16) | copy-start | bytes 49156
  0.6 10.6 %copy-start.1 = (bf16[4,32,256]{2,1,0:T(8,128)(2,1)S(1)}, bf16[4,32,256]{2,1,0:T(8,128)(2,1)}, u32[]{:S(2)}) copy-start(bf16[4,32,256]{2,1,0:T(8,128)(2,1)} %param.11) | copy-start | bytes 196612
  1.6 9.6 %collective-permute-start = (bf16[3,32,256]{2,1,0:T(8,128)(2,1)S(1)}, bf16[3,32,256]{2,1,0:T(8,128)(2,1)S(1)}, u32[]{:S(2)}, u32[]{:S(2)}) collective-permute-start(bf16[3,32,256]{2,1,0:T(8,128)(2,1)S(1)} %get-tuple-element.36), channel_id=1, source_target_pairs={{0,1},{1,2},{2,3},{3,4},{4,5},{5,6},{6,7},{7,8},{8,9},{9,10},{10,1... | collective-permute-start | bytes 147464 | tf_op jit(solution)/shard_map/ppermute | solution.py:19
  5.9 5.3 %collective-permute-start.1 = (bf16[3,32,256]{2,1,0:T(8,128)(2,1)S(1)}, bf16[3,32,256]{2,1,0:T(8,128)(2,1)S(1)}, u32[]{:S(2)}, u32[]{:S(2)}) collective-permute-start(bf16[3,32,256]{2,1,0:T(8,128)(2,1)S(1)} %get-tuple-element.35), channel_id=1, source_target_pairs={{1,0},{2,1},{3,2},{4,3},{5,4},{6,5},{7,6},{8,7},{9,8},{10,9},{11,1... | collective-permute-start | bytes 147464 | tf_op jit(solution)/shard_map/ppermute | solution.py:20
  18.9 0.9 copy-start.2
  19.0 0.9 copy-start.3
  20.9 17.5 %all-to-all-start = ((bf16[32,2,4,256]{3,2,1,0:T(4,128)(2,1)}), bf16[32,2,4,256]{3,2,1,0:T(4,128)(2,1)S(1)}, u32[]{:S(2)}, u32[]{:S(2)}) async-start(bf16[32,2,4,256]{3,2,1,0:T(4,128)(2,1)} %copy.97), calls=%async_computation | async-start | bytes 262144 | tf_op jit(solution)/shard_map/all_to_all | solution.py:159
  41.7 13.1 %all-to-all-start.1 = ((bf16[4,16,4,256]{3,2,0,1:T(4,128)(2,1)}), bf16[4,16,4,256]{3,2,0,1:T(4,128)(2,1)S(1)}, u32[]{:S(2)}, u32[]{:S(2)}) async-start(bf16[4,16,4,256]{3,2,0,1:T(4,128)(2,1)} %copy.102), calls=%async_computation.1 | async-start | bytes 262144 | tf_op jit(solution)/shard_map/all_to_all | solution.py:181
  59.6 2.6 %collective-permute-start.2 = (f32[81920]{0:T(1024)S(1)}, f32[81920]{0:T(1024)S(1)}, u32[]{:S(2)}, u32[]{:S(2)}) collective-permute-start(f32[81920]{0:T(1024)S(1)} %slice_select_fusion), channel_id=1, source_target_pairs={{0,32},{32,0},{1,33},{33,1},{2,34},{34,2},{3,35},{35,3},{4,36},{36... | collective-permute-start | bytes 983048 | tf_op jit(solution)/shard_map/ppermute | solution.py:93
  109.4 4.6 %collective-permute-start.3 = (f32[81920]{0:T(1024)S(1)}, f32[81920]{0:T(1024)S(1)}, u32[]{:S(2)}, u32[]{:S(2)}) collective-permute-start(f32[81920]{0:T(1024)S(1)} %bitcast.183), channel_id=1, source_target_pairs={{0,32},{32,0},{1,33},{33,1},{2,34},{34,2},{3,35},{35,3},{4,36},{36... | collective-permute-start | bytes 983048 | tf_op jit(solution)/shard_map/ppermute | solution.py:98

commit v11 on v10

--- a/solution.py
+++ b/solution.py
@@ -85,18 +85,20 @@
     flat = jnp.concatenate([p.reshape(-1) for p in parts])
     total = flat.shape[0]
     width = -(-total // (2 * devices * 128)) * 128
-    flat = jnp.pad(flat, (0, 2 * width * devices - total)).reshape(2, devices * width)
+    flat = jnp.pad(flat, (0, 2 * width * devices - total))
     core = lax.axis_index("core")
     swap = [(0, 1), (1, 0)]
-    first = core == 0
-    keep = jnp.where(first, flat[0], flat[1])
-    half = keep + lax.ppermute(jnp.where(first, flat[1], flat[0]), "core", swap)
+    size = width * devices
+    keep = lax.dynamic_slice_in_dim(flat, core * size, size)
+    send = lax.dynamic_slice_in_dim(flat, (1 - core) * size, size)
+    half = keep + lax.ppermute(send, "core", swap)
     pieces = lax.all_to_all(half.reshape(devices, width), peers, 0, 0, tiled=True)
     own = jnp.sum(pieces, axis=0, keepdims=True)
     summed = lax.all_to_all(jnp.broadcast_to(own, (devices, width)), peers, 0, 0, tiled=True)
     summed = summed.reshape(-1)
     other = lax.ppermute(summed, "core", swap)
-    spread = jnp.where(first, jnp.concatenate([summed, other]), jnp.concatenate([other, summed]))
+    spread = lax.dynamic_update_slice_in_dim(jnp.zeros_like(flat), summed, core * size, 0)
+    spread = lax.dynamic_update_slice_in_dim(spread, other, (1 - core) * size, 0)
     out, at = [], 0
     for p in parts:
         out.append(spread[at : at + p.size].reshape(p.shape))

time: 117 us -> 121 us (1.034)
  local copies, waits for them, and re-layouts: 9.33 us -> 14.8 us
    dynamic_update_slice x0 -> x2, local copies, waits for them, and re-layouts: none -> 4.77 us  [the longest x1 2.48 us: all_reduce_sum(): lax.dynamic_update_slice_in_dim(spread, other, (1 - core) * size, 0)]
  transfers between devices with their start and end apart: 6 -> 6, of which waited for: 4 -> 3; matrix products, arithmetic and copies ran while one was open for 5% -> 6% of each run, Pallas kernels for 0% -> 0%
where the time goes in v11:
time: 121 us; the launch traced here: 120 us
  blocking collectives  46.7 us (39%)
  starting transfers between devices  23.8 us (20%)
  waiting for transfers between devices  16.9 us (14%)
  local copies, waits for them, and re-layouts  14.8 us (12%)
  matrix products  11.2 us (9%)
  other arithmetic  5.18 us (4%)
  between operations  1.74 us (1%)
    all_to_all x1, blocking collectives, all_reduce_sum(): lax.all_to_all(half.reshape(devices, width), peers, 0, 0, tiled=True)  27 us
    all_to_all x1, blocking collectives, all_reduce_sum(): lax.all_to_all(jnp.broadcast_to(own, (devices, width)), peers, 0, 0, tile...  19.7 us
    all_to_all x1, starting transfers between devices, on_device(): lax.all_to_all(sample_prediction, MEMBER, split_axis=0, concat_axis=1, ti...  9.16 us
    all_to_all x1, waiting for transfers between devices, on_device(): lax.all_to_all(cot_share, MEMBER, split_axis=1, concat_axis=0, tiled=True)  8.71 us
    all_to_all x1, waiting for transfers between devices, on_device(): lax.all_to_all(sample_prediction, MEMBER, split_axis=0, concat_axis=1, ti...  6.9 us
    dot_general x6, matrix products, feature_conv(): jnp.einsum('mrwc,cd->mrwd', shifted[:, i:i + out_rows], kernel[i].reshape...  4.7 us
    ppermute x1, starting transfers between devices, extended(): before = lax.ppermute(last, axis, up)  4.35 us
    all_to_all x1, starting transfers between devices, on_device(): lax.all_to_all(cot_share, MEMBER, split_axis=1, concat_axis=0, tiled=True)  4.34 us
  transfers between devices with their start and end apart: 6, of which 3 were waited for; matrix products, arithmetic and copies ran while one was open for 6% of the time, Pallas kernels for 0%

profile of v11, /device:TPU:1, one launch (start us, length us, event | category | flops | bytes accessed | tf_op | source)
XLA Modules:
  0.0 120.3 jit_solution(18208385662169431917)
XLA Ops:
  0.7 0.9 fusion.61
  1.6 4.3 %collective-permute-start = (bf16[3,32,256]{2,1,0:T(8,128)(2,1)S(1)}, bf16[3,32,256]{2,1,0:T(8,128)(2,1)S(1)}, u32[]{:S(2)}, u32[]{:S(2)}) collective-permute-start(bf16[3,32,256]{2,1,0:T(8,128)(2,1)S(1)} %get-tuple-element.36), channel_id=1, source_target_pairs={{0,1},{1,2},{2,3},{3,4},{4,5},{5,6},{6,7},{7,8},{8,9},{9,10},{10,1... | collective-permute-start | bytes 147464 | tf_op jit(solution)/shard_map/ppermute | solution.py:19
  5.9 1.3 %collective-permute-start.1 = (bf16[3,32,256]{2,1,0:T(8,128)(2,1)S(1)}, bf16[3,32,256]{2,1,0:T(8,128)(2,1)S(1)}, u32[]{:S(2)}, u32[]{:S(2)}) collective-permute-start(bf16[3,32,256]{2,1,0:T(8,128)(2,1)S(1)} %get-tuple-element.35), channel_id=1, source_target_pairs={{1,0},{2,1},{3,2},{4,3},{5,4},{6,5},{7,6},{8,7},{9,8},{10,9},{11,1... | collective-permute-start | bytes 147464 | tf_op jit(solution)/shard_map/ppermute | solution.py:20
  7.2 0.8 fusion.60
  8.0 0.9 fusion.44
  9.0 1.0 fusion.59
  10.2 1.0 fusion.58
  13.1 0.9 fusion.22
  14.0 0.6 pad_slice_fusion.1
  14.6 0.8 fusion.56
  15.4 0.8 fusion.57
  16.2 1.2 fusion.21
  19.0 0.8 add_convert_fusion
  20.1 0.8 copy.97
  20.9 9.2 %all-to-all-start = ((bf16[32,2,4,256]{3,2,1,0:T(4,128)(2,1)}), bf16[32,2,4,256]{3,2,1,0:T(4,128)(2,1)S(1)}, u32[]{:S(2)}, u32[]{:S(2)}) async-start(bf16[32,2,4,256]{3,2,1,0:T(4,128)(2,1)} %copy.97), calls=%async_computation | async-start | bytes 262144 | tf_op jit(solution)/shard_map/all_to_all | solution.py:161
  30.0 0.7 convert_bitcast_fusion.1
  31.5 6.9 %all-to-all-done = bf16[32,2,4,256]{3,2,1,0:T(4,128)(2,1)S(1)} async-done(((bf16[32,2,4,256]{3,2,1,0:T(4,128)(2,1)}), bf16[32,2,4,256]{3,2,1,0:T(4,128)(2,1)S(1)}, u32[]{:S(2)}, u32[]{:S(2)}) %all-to-all-start) | async-done | bytes 131104 | tf_op jit(solution)/shard_map/all_to_all | solution.py:161
  38.5 2.3 %fusion.1 = (f32[4,16,4,256]{3,2,1,0:T(4,128)S(1)}, f32[4,4,256]{2,1,0:T(4,128)S(1)}) fusion(f32[4,16,4,256]{3,1,2,0:T(8,128)S(1)} %copy.100, f32[4,16,4,256]{3,2,1,0:T(4,128)S(1)} %bitcast.179), kind=kLoop, calls=%fused_computation.3 | loop fusion | flops 5173248 | bytes 802816 | tf_op jit(solution)/shard_map/reduce_sum | solution.py:171
  41.0 0.7 copy.102
  41.7 4.3 %all-to-all-start.1 = ((bf16[4,16,4,256]{3,2,0,1:T(4,128)(2,1)}), bf16[4,16,4,256]{3,2,0,1:T(4,128)(2,1)S(1)}, u32[]{:S(2)}, u32[]{:S(2)}) async-start(bf16[4,16,4,256]{3,2,0,1:T(4,128)(2,1)} %copy.102), calls=%async_computation.1 | async-start | bytes 262144 | tf_op jit(solution)/shard_map/all_to_all | solution.py:183
  46.0 8.7 %all-to-all-done.1 = bf16[4,16,4,256]{3,2,0,1:T(4,128)(2,1)S(1)} async-done(((bf16[4,16,4,256]{3,2,0,1:T(4,128)(2,1)}), bf16[4,16,4,256]{3,2,0,1:T(4,128)(2,1)S(1)}, u32[]{:S(2)}, u32[]{:S(2)}) %all-to-all-start.1) | async-done | bytes 131104 | tf_op jit(solution)/shard_map/all_to_all | solution.py:183
  54.8 0.9 fusion.29
  59.7 1.3 %collective-permute-start.2 = (f32[81920]{0:T(1024)S(1)}, f32[81920]{0:T(1024)S(1)}, u32[]{:S(2)}, u32[]{:S(2)}) collective-permute-start(f32[81920]{0:T(1024)S(1)} %dynamic_slice.11), channel_id=1, source_target_pairs={{0,32},{32,0},{1,33},{33,1},{2,34},{34,2},{3,35},{35,3},{4,36},{36... | collective-permute-start | bytes 983048 | tf_op jit(solution)/shard_map/ppermute | solution.py:94
  61.0 1.3 %collective-permute-done.2 = f32[81920]{0:T(1024)S(1)} collective-permute-done((f32[81920]{0:T(1024)S(1)}, f32[81920]{0:T(1024)S(1)}, u32[]{:S(2)}, u32[]{:S(2)}) %collective-permute-start.2) | collective-permute-done | bytes 327712 | tf_op jit(solution)/shard_map/ppermute | solution.py:94
  62.3 27.0 %all_to_all.42 = f32[128,1,640]{2,1,0:T(1,128)S(1)} all-to-all(f32[128,1,640]{2,1,0:T(1,128)S(1)} %bitcast.182), channel_id=1, replica_groups=mesh['group'=4,'core'=2,'tile'=32] {'group','tile'}, dimensions={0} | all-to-all | bytes 655360 | tf_op jit(solution)/shard_map/all_to_all | solution.py:95
  89.7 19.7 %all_to_all.43 = f32[128,1,640]{2,1,0:T(1,128)S(1)} all-to-all(f32[128,1,640]{2,1,0:T(1,128)S(1)} %broadcast_in_dim.32), channel_id=1, replica_groups=mesh['group'=4,'core'=2,'tile'=32] {'group','tile'}, dimensions={0} | all-to-all | bytes 655360 | tf_op jit(solution)/shard_map/all_to_all | solution.py:97
  109.4 3.4 %collective-permute-start.3 = (f32[81920]{0:T(1024)S(1)}, f32[81920]{0:T(1024)S(1)}, u32[]{:S(2)}, u32[]{:S(2)}) collective-permute-start(f32[81920]{0:T(1024)S(1)} %bitcast.183), channel_id=1, source_target_pairs={{0,32},{32,0},{1,33},{33,1},{2,34},{34,2},{3,35},{35,3},{4,36},{36... | collective-permute-start | bytes 983048 | tf_op jit(solution)/shard_map/ppermute | solution.py:99
  112.9 0.6 copy.116
  113.5 2.3 %dynamic_update_slice.6 = f32[163840]{0:T(1024)S(1)} dynamic-update-slice(f32[163840]{0:T(1024)S(1)} %broadcast_in_dim.31, f32[81920]{0:T(1024)S(1)} %bitcast.184, s32[]{:T(128)S(6)} %select_n.22) | dynamic-update-slice | bytes 655364 | tf_op jit(solution)/shard_map/dynamic_update_slice | solution.py:100
  115.8 2.5 %dynamic_update_slice.7 = f32[163840]{0:T(1024)S(1)} dynamic-update-slice(f32[163840]{0:T(1024)S(1)} %dynamic_update_slice.6, f32[81920]{0:T(1024)S(1)} %collective-permute-done.3, s32[]{:T(128)S(6)} %select_n.23) | dynamic-update-slice | bytes 655364 | tf_op jit(solution)/shard_map/dynamic_update_slice | solution.py:101
  118.3 0.9 slice.188
  119.2 0.6 slice_bitcast_fusion
  (66 shorter events, 9.4 us)
Async XLA Ops:
  0.6 8.3 %copy-start = (f32[16,256]{1,0:T(8,128)S(1)}, f32[16,256]{1,0:T(8,128)}, u32[]{:S(2)}) copy-start(f32[16,256]{1,0:T(8,128)} %param.16) | copy-start | bytes 49156
  0.6 10.6 %copy-start.1 = (bf16[4,32,256]{2,1,0:T(8,128)(2,1)S(1)}, bf16[4,32,256]{2,1,0:T(8,128)(2,1)}, u32[]{:S(2)}) copy-start(bf16[4,32,256]{2,1,0:T(8,128)(2,1)} %param.11) | copy-start | bytes 196612
  1.6 9.6 %collective-permute-start = (bf16[3,32,256]{2,1,0:T(8,128)(2,1)S(1)}, bf16[3,32,256]{2,1,0:T(8,128)(2,1)S(1)}, u32[]{:S(2)}, u32[]{:S(2)}) collective-permute-start(bf16[3,32,256]{2,1,0:T(8,128)(2,1)S(1)} %get-tuple-element.36), channel_id=1, source_target_pairs={{0,1},{1,2},{2,3},{3,4},{4,5},{5,6},{6,7},{7,8},{8,9},{9,10},{10,1... | collective-permute-start | bytes 147464 | tf_op jit(solution)/shard_map/ppermute | solution.py:19
  5.9 5.3 %collective-permute-start.1 = (bf16[3,32,256]{2,1,0:T(8,128)(2,1)S(1)}, bf16[3,32,256]{2,1,0:T(8,128)(2,1)S(1)}, u32[]{:S(2)}, u32[]{:S(2)}) collective-permute-start(bf16[3,32,256]{2,1,0:T(8,128)(2,1)S(1)} %get-tuple-element.35), channel_id=1, source_target_pairs={{1,0},{2,1},{3,2},{4,3},{5,4},{6,5},{7,6},{8,7},{9,8},{10,9},{11,1... | collective-permute-start | bytes 147464 | tf_op jit(solution)/shard_map/ppermute | solution.py:20
  18.9 0.9 copy-start.2
  19.0 0.9 copy-start.3
  20.9 17.5 %all-to-all-start = ((bf16[32,2,4,256]{3,2,1,0:T(4,128)(2,1)}), bf16[32,2,4,256]{3,2,1,0:T(4,128)(2,1)S(1)}, u32[]{:S(2)}, u32[]{:S(2)}) async-start(bf16[32,2,4,256]{3,2,1,0:T(4,128)(2,1)} %copy.97), calls=%async_computation | async-start | bytes 262144 | tf_op jit(solution)/shard_map/all_to_all | solution.py:161
  41.7 13.1 %all-to-all-start.1 = ((bf16[4,16,4,256]{3,2,0,1:T(4,128)(2,1)}), bf16[4,16,4,256]{3,2,0,1:T(4,128)(2,1)S(1)}, u32[]{:S(2)}, u32[]{:S(2)}) async-start(bf16[4,16,4,256]{3,2,0,1:T(4,128)(2,1)} %copy.102), calls=%async_computation.1 | async-start | bytes 262144 | tf_op jit(solution)/shard_map/all_to_all | solution.py:183
  59.7 2.6 %collective-permute-start.2 = (f32[81920]{0:T(1024)S(1)}, f32[81920]{0:T(1024)S(1)}, u32[]{:S(2)}, u32[]{:S(2)}) collective-permute-start(f32[81920]{0:T(1024)S(1)} %dynamic_slice.11), channel_id=1, source_target_pairs={{0,32},{32,0},{1,33},{33,1},{2,34},{34,2},{3,35},{35,3},{4,36},{36... | collective-permute-start | bytes 983048 | tf_op jit(solution)/shard_map/ppermute | solution.py:94
  109.4 6.5 %collective-permute-start.3 = (f32[81920]{0:T(1024)S(1)}, f32[81920]{0:T(1024)S(1)}, u32[]{:S(2)}, u32[]{:S(2)}) collective-permute-start(f32[81920]{0:T(1024)S(1)} %bitcast.183), channel_id=1, source_target_pairs={{0,32},{32,0},{1,33},{33,1},{2,34},{34,2},{3,35},{35,3},{4,36},{36... | collective-permute-start | bytes 983048 | tf_op jit(solution)/shard_map/ppermute | solution.py:99

commit v12 on v10

--- a/solution.py
+++ b/solution.py
@@ -26,16 +26,15 @@
     out_rows = padded.shape[0] - 2
     col_count = padded.shape[2]
     wide = jnp.pad(padded, ((0, 0), (0, 0), (1, 1)))
-    shifted = jnp.concatenate([wide[:, :, j : j + col_count] for j in range(3)], axis=1)
-    summed = jnp.zeros((out_rows, col_count, kernel.shape[3]), jnp.float32)
-    for i in range(3):
-        summed = summed + jnp.einsum(
-            "rkw,kc->rwc",
-            shifted[i : i + out_rows],
-            kernel[i].reshape(-1, kernel.shape[3]),
-            preferred_element_type=jnp.float32,
-        )
-    return summed
+    shifted = jnp.concatenate(
+        [wide[i : i + out_rows, :, j : j + col_count] for i in range(3) for j in range(3)], axis=1
+    )
+    return jnp.einsum(
+        "rkw,kc->rwc",
+        shifted,
+        kernel.reshape(-1, kernel.shape[3]),
+        preferred_element_type=jnp.float32,
+    )
 
 
 def feature_conv(padded, kernel):

time: 117 us -> 117 us (level)
  no operation moved by 1% of the time
where the time goes in v12:
time: 117 us; the launch traced here: 116 us
  blocking collectives  46.7 us (40%)
  starting transfers between devices  23.9 us (20%)
  waiting for transfers between devices  17.4 us (15%)
  matrix products  11.4 us (10%)
  local copies, waits for them, and re-layouts  9.03 us (8%)
  other arithmetic  5.84 us (5%)
  between operations  1.76 us (2%)
    all_to_all x1, blocking collectives, all_reduce_sum(): lax.all_to_all(half.reshape(devices, width), peers, 0, 0, tiled=True)  26.9 us
    all_to_all x1, blocking collectives, all_reduce_sum(): lax.all_to_all(jnp.broadcast_to(own, (devices, width)), peers, 0, 0, tile...  19.7 us
    all_to_all x1, starting transfers between devices, on_device(): lax.all_to_all(sample_prediction, MEMBER, split_axis=0, concat_axis=1, ti...  9.22 us
    all_to_all x1, waiting for transfers between devices, on_device(): lax.all_to_all(cot_share, MEMBER, split_axis=1, concat_axis=0, tiled=True)  8.71 us
    all_to_all x1, waiting for transfers between devices, on_device(): lax.all_to_all(sample_prediction, MEMBER, split_axis=0, concat_axis=1, ti...  6.9 us
    dot_general x6, matrix products, feature_conv(): jnp.einsum('mrwc,cd->mrwd', shifted[:, i:i + out_rows], kernel[i].reshape...  4.68 us
    ppermute x1, starting transfers between devices, extended(): before = lax.ppermute(last, axis, up)  4.35 us
    all_to_all x1, starting transfers between devices, on_device(): lax.all_to_all(cot_share, MEMBER, split_axis=1, concat_axis=0, tiled=True)  4.34 us
  transfers between devices with their start and end apart: 6, of which 4 were waited for; matrix products, arithmetic and copies ran while one was open for 5% of the time, Pallas kernels for 0%

profile of v12, /device:TPU:1, one launch (start us, length us, event | category | flops | bytes accessed | tf_op | source)
XLA Modules:
  0.0 116.0 jit_solution(17245010402485827581)
XLA Ops:
  0.7 0.9 fusion.69
  1.6 4.3 %collective-permute-start = (bf16[3,32,256]{2,1,0:T(8,128)(2,1)S(1)}, bf16[3,32,256]{2,1,0:T(8,128)(2,1)S(1)}, u32[]{:S(2)}, u32[]{:S(2)}) collective-permute-start(bf16[3,32,256]{2,1,0:T(8,128)(2,1)S(1)} %get-tuple-element.31), channel_id=1, source_target_pairs={{0,1},{1,2},{2,3},{3,4},{4,5},{5,6},{6,7},{7,8},{8,9},{9,10},{10,1... | collective-permute-start | bytes 147464 | tf_op jit(solution)/shard_map/ppermute | solution.py:19
  5.9 1.3 %collective-permute-start.1 = (bf16[3,32,256]{2,1,0:T(8,128)(2,1)S(1)}, bf16[3,32,256]{2,1,0:T(8,128)(2,1)S(1)}, u32[]{:S(2)}, u32[]{:S(2)}) collective-permute-start(bf16[3,32,256]{2,1,0:T(8,128)(2,1)S(1)} %get-tuple-element.30), channel_id=1, source_target_pairs={{1,0},{2,1},{3,2},{4,3},{5,4},{6,5},{7,6},{8,7},{9,8},{10,9},{11,1... | collective-permute-start | bytes 147464 | tf_op jit(solution)/shard_map/ppermute | solution.py:20
  7.2 0.9 fusion.54
  8.1 0.8 fusion.71
  9.0 1.0 fusion.68
  10.1 1.0 fusion.67
  13.0 0.9 fusion.22
  13.9 0.6 pad_slice_fusion.1
  14.5 0.8 fusion.65
  15.3 0.8 fusion.66
  16.1 1.1 fusion.21
  17.7 0.6 fusion.64
  18.3 0.6 convolution_add_fusion.1
  18.9 0.8 add_convert_fusion
  20.0 0.8 copy.97
  20.8 9.2 %all-to-all-start = ((bf16[32,2,4,256]{3,2,1,0:T(4,128)(2,1)}), bf16[32,2,4,256]{3,2,1,0:T(4,128)(2,1)S(1)}, u32[]{:S(2)}, u32[]{:S(2)}) async-start(bf16[32,2,4,256]{3,2,1,0:T(4,128)(2,1)} %copy.97), calls=%async_computation | async-start | bytes 262144 | tf_op jit(solution)/shard_map/all_to_all | solution.py:158
  30.0 0.7 convert_bitcast_fusion.1
  31.4 6.9 %all-to-all-done = bf16[32,2,4,256]{3,2,1,0:T(4,128)(2,1)S(1)} async-done(((bf16[32,2,4,256]{3,2,1,0:T(4,128)(2,1)}), bf16[32,2,4,256]{3,2,1,0:T(4,128)(2,1)S(1)}, u32[]{:S(2)}, u32[]{:S(2)}) %all-to-all-start) | async-done | bytes 131104 | tf_op jit(solution)/shard_map/all_to_all | solution.py:158
  38.4 2.3 %fusion.1 = (f32[4,16,4,256]{3,2,1,0:T(4,128)S(1)}, f32[4,4,256]{2,1,0:T(4,128)S(1)}) fusion(f32[4,16,4,256]{3,1,2,0:T(8,128)S(1)} %copy.100, f32[4,16,4,256]{3,2,1,0:T(4,128)S(1)} %bitcast.175), kind=kLoop, calls=%fused_computation.3 | loop fusion | flops 5173248 | bytes 802816 | tf_op jit(solution)/shard_map/reduce_sum | solution.py:168
  41.0 0.7 copy.102
  41.7 4.3 %all-to-all-start.1 = ((bf16[4,16,4,256]{3,2,0,1:T(4,128)(2,1)}), bf16[4,16,4,256]{3,2,0,1:T(4,128)(2,1)S(1)}, u32[]{:S(2)}, u32[]{:S(2)}) async-start(bf16[4,16,4,256]{3,2,0,1:T(4,128)(2,1)} %copy.102), calls=%async_computation.1 | async-start | bytes 262144 | tf_op jit(solution)/shard_map/all_to_all | solution.py:180
  46.0 8.7 %all-to-all-done.1 = bf16[4,16,4,256]{3,2,0,1:T(4,128)(2,1)S(1)} async-done(((bf16[4,16,4,256]{3,2,0,1:T(4,128)(2,1)}), bf16[4,16,4,256]{3,2,0,1:T(4,128)(2,1)S(1)}, u32[]{:S(2)}, u32[]{:S(2)}) %all-to-all-start.1) | async-done | bytes 131104 | tf_op jit(solution)/shard_map/all_to_all | solution.py:180
  55.0 0.9 fusion.29
  59.6 1.3 %collective-permute-start.2 = (f32[81920]{0:T(1024)S(1)}, f32[81920]{0:T(1024)S(1)}, u32[]{:S(2)}, u32[]{:S(2)}) collective-permute-start(f32[81920]{0:T(1024)S(1)} %slice_select_fusion), channel_id=1, source_target_pairs={{0,32},{32,0},{1,33},{33,1},{2,34},{34,2},{3,35},{35,3},{4,36},{36... | collective-permute-start | bytes 983048 | tf_op jit(solution)/shard_map/ppermute | solution.py:92
  60.9 1.3 %collective-permute-done.2 = f32[81920]{0:T(1024)S(1)} collective-permute-done((f32[81920]{0:T(1024)S(1)}, f32[81920]{0:T(1024)S(1)}, u32[]{:S(2)}, u32[]{:S(2)}) %collective-permute-start.2) | collective-permute-done | bytes 327712 | tf_op jit(solution)/shard_map/ppermute | solution.py:92
  62.2 26.9 %all_to_all.42 = f32[128,1,640]{2,1,0:T(1,128)S(1)} all-to-all(f32[128,1,640]{2,1,0:T(1,128)S(1)} %bitcast.181), channel_id=1, replica_groups=mesh['group'=4,'core'=2,'tile'=32] {'group','tile'}, dimensions={0} | all-to-all | bytes 655360 | tf_op jit(solution)/shard_map/all_to_all | solution.py:93
  89.6 19.7 %all_to_all.43 = f32[128,1,640]{2,1,0:T(1,128)S(1)} all-to-all(f32[128,1,640]{2,1,0:T(1,128)S(1)} %broadcast_in_dim.29), channel_id=1, replica_groups=mesh['group'=4,'core'=2,'tile'=32] {'group','tile'}, dimensions={0} | all-to-all | bytes 655360 | tf_op jit(solution)/shard_map/all_to_all | solution.py:95
  109.3 3.4 %collective-permute-start.3 = (f32[81920]{0:T(1024)S(1)}, f32[81920]{0:T(1024)S(1)}, u32[]{:S(2)}, u32[]{:S(2)}) collective-permute-start(f32[81920]{0:T(1024)S(1)} %bitcast.177), channel_id=1, source_target_pairs={{0,32},{32,0},{1,33},{33,1},{2,34},{34,2},{3,35},{35,3},{4,36},{36... | collective-permute-start | bytes 983048 | tf_op jit(solution)/shard_map/ppermute | solution.py:97
  112.8 0.6 copy.116
  114.0 0.9 slice.202
  115.4 0.6 fusion.51
  (68 shorter events, 8.5 us)
Async XLA Ops:
  0.6 11.3 %copy-start = (bf16[3,3,32,128]{3,2,1,0:T(8,128)(2,1)S(1)}, bf16[3,3,32,128]{3,2,1,0:T(8,128)(2,1)}, u32[]{:S(2)}) copy-start(bf16[3,3,32,128]{3,2,1,0:T(8,128)(2,1)} %param.17) | copy-start | bytes 221188
  0.6 10.5 %copy-start.1 = (bf16[4,32,256]{2,1,0:T(8,128)(2,1)S(1)}, bf16[4,32,256]{2,1,0:T(8,128)(2,1)}, u32[]{:S(2)}) copy-start(bf16[4,32,256]{2,1,0:T(8,128)(2,1)} %param.11) | copy-start | bytes 196612
  1.6 9.6 %collective-permute-start = (bf16[3,32,256]{2,1,0:T(8,128)(2,1)S(1)}, bf16[3,32,256]{2,1,0:T(8,128)(2,1)S(1)}, u32[]{:S(2)}, u32[]{:S(2)}) collective-permute-start(bf16[3,32,256]{2,1,0:T(8,128)(2,1)S(1)} %get-tuple-element.31), channel_id=1, source_target_pairs={{0,1},{1,2},{2,3},{3,4},{4,5},{5,6},{6,7},{7,8},{8,9},{9,10},{10,1... | collective-permute-start | bytes 147464 | tf_op jit(solution)/shard_map/ppermute | solution.py:19
  5.9 5.3 %collective-permute-start.1 = (bf16[3,32,256]{2,1,0:T(8,128)(2,1)S(1)}, bf16[3,32,256]{2,1,0:T(8,128)(2,1)S(1)}, u32[]{:S(2)}, u32[]{:S(2)}) collective-permute-start(bf16[3,32,256]{2,1,0:T(8,128)(2,1)S(1)} %get-tuple-element.30), channel_id=1, source_target_pairs={{1,0},{2,1},{3,2},{4,3},{5,4},{6,5},{7,6},{8,7},{9,8},{10,9},{11,1... | collective-permute-start | bytes 147464 | tf_op jit(solution)/shard_map/ppermute | solution.py:20
  18.9 0.9 copy-start.2
  18.9 0.9 copy-start.3
  20.8 17.6 %all-to-all-start = ((bf16[32,2,4,256]{3,2,1,0:T(4,128)(2,1)}), bf16[32,2,4,256]{3,2,1,0:T(4,128)(2,1)S(1)}, u32[]{:S(2)}, u32[]{:S(2)}) async-start(bf16[32,2,4,256]{3,2,1,0:T(4,128)(2,1)} %copy.97), calls=%async_computation | async-start | bytes 262144 | tf_op jit(solution)/shard_map/all_to_all | solution.py:158
  41.7 13.1 %all-to-all-start.1 = ((bf16[4,16,4,256]{3,2,0,1:T(4,128)(2,1)}), bf16[4,16,4,256]{3,2,0,1:T(4,128)(2,1)S(1)}, u32[]{:S(2)}, u32[]{:S(2)}) async-start(bf16[4,16,4,256]{3,2,0,1:T(4,128)(2,1)} %copy.102), calls=%async_computation.1 | async-start | bytes 262144 | tf_op jit(solution)/shard_map/all_to_all | solution.py:180
  59.6 2.6 %collective-permute-start.2 = (f32[81920]{0:T(1024)S(1)}, f32[81920]{0:T(1024)S(1)}, u32[]{:S(2)}, u32[]{:S(2)}) collective-permute-start(f32[81920]{0:T(1024)S(1)} %slice_select_fusion), channel_id=1, source_target_pairs={{0,32},{32,0},{1,33},{33,1},{2,34},{34,2},{3,35},{35,3},{4,36},{36... | collective-permute-start | bytes 983048 | tf_op jit(solution)/shard_map/ppermute | solution.py:92
  109.3 4.6 %collective-permute-start.3 = (f32[81920]{0:T(1024)S(1)}, f32[81920]{0:T(1024)S(1)}, u32[]{:S(2)}, u32[]{:S(2)}) collective-permute-start(f32[81920]{0:T(1024)S(1)} %bitcast.177), channel_id=1, source_target_pairs={{0,32},{32,0},{1,33},{33,1},{2,34},{34,2},{3,35},{35,3},{4,36},{36... | collective-permute-start | bytes 983048 | tf_op jit(solution)/shard_map/ppermute | solution.py:97

commit v13 on v12

--- a/solution.py
+++ b/solution.py
@@ -164,9 +164,10 @@
         lax.dynamic_slice_in_dim(target, var_start, var_share, 1), (1, 0, 2)
     ).astype(jnp.float32)[:, None]
     pair_differ = sample_group_predictions[:, :, None] - sample_group_predictions[:, None, :]
-    abs_sums = jnp.sum(jnp.abs(pair_differ), axis=2)
     sign_sums = jnp.sum(jnp.sign(pair_differ), axis=2)
-    crps_share = jnp.mean(jnp.abs(sample_group_predictions - truth), axis=1) - jnp.sum(
+    scored, scored_truth = lax.optimization_barrier((sample_group_predictions, truth))
+    abs_sums = jnp.sum(jnp.abs(scored[:, :, None] - scored[:, None, :]), axis=2)
+    crps_share = jnp.mean(jnp.abs(scored - scored_truth), axis=1) - jnp.sum(
         abs_sums, axis=1
     ) / (2 * member_count * (member_count - 1))
     crps_map = jnp.transpose(crps_share, (1, 0, 2))

time: 117 us -> 118 us (level)
  blocking collectives: 46.7 us -> 27 us
  waiting for transfers between devices: 17.4 us -> 30.8 us
  starting transfers between devices: 23.9 us -> 30.1 us
    all_to_all x1 -> x0, blocking collectives: 19.7 us -> none  [all_reduce_sum(): lax.all_to_all(jnp.broadcast_to(own, (devices, width)), peers, 0, 0, tile...]
    all_to_all x0 -> x1, waiting for transfers between devices: none -> 13.4 us  [all_reduce_sum(): lax.all_to_all(jnp.broadcast_to(own, (devices, width)), peers, 0, 0, tile...]
    all_to_all x0 -> x1, starting transfers between devices: none -> 6.18 us  [all_reduce_sum(): lax.all_to_all(jnp.broadcast_to(own, (devices, width)), peers, 0, 0, tile...]
  transfers between devices with their start and end apart: 6 -> 7, of which waited for: 4 -> 5; matrix products, arithmetic and copies ran while one was open for 5% -> 5% of each run, Pallas kernels for 0% -> 0%
where the time goes in v13:
time: 118 us; the launch traced here: 117 us
  waiting for transfers between devices  30.8 us (26%)
  starting transfers between devices  30.1 us (26%)
  blocking collectives  27 us (23%)
  matrix products  11.4 us (10%)
  local copies, waits for them, and re-layouts  9.81 us (8%)
  other arithmetic  6.01 us (5%)
  between operations  1.77 us (2%)
    all_to_all x1, blocking collectives, all_reduce_sum(): lax.all_to_all(half.reshape(devices, width), peers, 0, 0, tiled=True)  27 us
    all_to_all x1, waiting for transfers between devices, all_reduce_sum(): lax.all_to_all(jnp.broadcast_to(own, (devices, width)), peers, 0, 0, tile...  13.4 us
    all_to_all x1, starting transfers between devices, on_device(): lax.all_to_all(sample_prediction, MEMBER, split_axis=0, concat_axis=1, ti...  9.22 us
    all_to_all x1, waiting for transfers between devices, on_device(): lax.all_to_all(cot_share, MEMBER, split_axis=1, concat_axis=0, tiled=True)  8.71 us
    all_to_all x1, waiting for transfers between devices, on_device(): lax.all_to_all(sample_prediction, MEMBER, split_axis=0, concat_axis=1, ti...  6.9 us
    all_to_all x1, starting transfers between devices, all_reduce_sum(): lax.all_to_all(jnp.broadcast_to(own, (devices, width)), peers, 0, 0, tile...  6.18 us
    dot_general x6, matrix products, feature_conv(): jnp.einsum('mrwc,cd->mrwd', shifted[:, i:i + out_rows], kernel[i].reshape...  4.68 us
    ppermute x1, starting transfers between devices, extended(): before = lax.ppermute(last, axis, up)  4.35 us
  transfers between devices with their start and end apart: 7, of which 5 were waited for; matrix products, arithmetic and copies ran while one was open for 5% of the time, Pallas kernels for 0%

profile of v13, /device:TPU:1, one launch (start us, length us, event | category | flops | bytes accessed | tf_op | source)
XLA Modules:
  0.0 116.8 jit_solution(11261077396860868069)
XLA Ops:
  0.7 0.9 fusion.67
  1.6 4.3 %collective-permute-start = (bf16[3,32,256]{2,1,0:T(8,128)(2,1)S(1)}, bf16[3,32,256]{2,1,0:T(8,128)(2,1)S(1)}, u32[]{:S(2)}, u32[]{:S(2)}) collective-permute-start(bf16[3,32,256]{2,1,0:T(8,128)(2,1)S(1)} %get-tuple-element.35), channel_id=1, source_target_pairs={{0,1},{1,2},{2,3},{3,4},{4,5},{5,6},{6,7},{7,8},{8,9},{9,10},{10,1... | collective-permute-start | bytes 147464 | tf_op jit(solution)/shard_map/ppermute | solution.py:19
  5.9 1.3 %collective-permute-start.1 = (bf16[3,32,256]{2,1,0:T(8,128)(2,1)S(1)}, bf16[3,32,256]{2,1,0:T(8,128)(2,1)S(1)}, u32[]{:S(2)}, u32[]{:S(2)}) collective-permute-start(bf16[3,32,256]{2,1,0:T(8,128)(2,1)S(1)} %get-tuple-element.34), channel_id=1, source_target_pairs={{1,0},{2,1},{3,2},{4,3},{5,4},{6,5},{7,6},{8,7},{9,8},{10,9},{11,1... | collective-permute-start | bytes 147464 | tf_op jit(solution)/shard_map/ppermute | solution.py:20
  7.2 0.9 fusion.52
  8.1 0.8 fusion.69
  9.0 1.0 fusion.66
  10.1 1.0 fusion.65
  13.0 0.9 fusion.20
  13.9 0.6 pad_slice_fusion.1
  14.5 0.8 fusion.63
  15.3 0.8 fusion.64
  16.1 1.1 fusion.19
  18.9 0.8 add_convert_fusion
  20.0 0.8 copy.82
  20.8 9.2 %all-to-all-start = ((bf16[32,2,4,256]{3,2,1,0:T(4,128)(2,1)}), bf16[32,2,4,256]{3,2,1,0:T(4,128)(2,1)S(1)}, u32[]{:S(2)}, u32[]{:S(2)}) async-start(bf16[32,2,4,256]{3,2,1,0:T(4,128)(2,1)} %copy.82), calls=%async_computation | async-start | bytes 262144 | tf_op jit(solution)/shard_map/all_to_all | solution.py:158
  30.0 0.7 convert_bitcast_fusion.2
  31.4 6.9 %all-to-all-done = bf16[32,2,4,256]{3,2,1,0:T(4,128)(2,1)S(1)} async-done(((bf16[32,2,4,256]{3,2,1,0:T(4,128)(2,1)}), bf16[32,2,4,256]{3,2,1,0:T(4,128)(2,1)S(1)}, u32[]{:S(2)}, u32[]{:S(2)}) %all-to-all-start) | async-done | bytes 131104 | tf_op jit(solution)/shard_map/all_to_all | solution.py:158
  38.4 2.0 %sign_reduce_fusion = f32[4,16,4,256]{3,2,1,0:T(4,128)S(1)} fusion(f32[4,16,4,256]{3,1,2,0:T(8,128)S(1)} %copy.87, f32[4,16,4,256]{3,2,1,0:T(4,128)S(1)} %bitcast.176), kind=kLoop, calls=%fused_computation | loop fusion | flops 3080192 | bytes 786432 | tf_op jit(solution)/shard_map/reduce_sum | solution.py:167
  40.7 0.7 copy.88
  41.4 4.3 %all-to-all-start.1 = ((bf16[4,16,4,256]{3,2,0,1:T(4,128)(2,1)}), bf16[4,16,4,256]{3,2,0,1:T(4,128)(2,1)S(1)}, u32[]{:S(2)}, u32[]{:S(2)}) async-start(bf16[4,16,4,256]{3,2,0,1:T(4,128)(2,1)} %copy.88), calls=%async_computation.1 | async-start | bytes 262144 | tf_op jit(solution)/shard_map/all_to_all | solution.py:181
  45.7 8.7 %all-to-all-done.1 = bf16[4,16,4,256]{3,2,0,1:T(4,128)(2,1)S(1)} async-done(((bf16[4,16,4,256]{3,2,0,1:T(4,128)(2,1)}), bf16[4,16,4,256]{3,2,0,1:T(4,128)(2,1)S(1)}, u32[]{:S(2)}, u32[]{:S(2)}) %all-to-all-start.1) | async-done | bytes 131104 | tf_op jit(solution)/shard_map/all_to_all | solution.py:181
  54.7 0.9 fusion.27
  59.3 1.3 %collective-permute-start.2 = (f32[81920]{0:T(1024)S(1)}, f32[81920]{0:T(1024)S(1)}, u32[]{:S(2)}, u32[]{:S(2)}) collective-permute-start(f32[81920]{0:T(1024)S(1)} %slice_select_fusion), channel_id=1, source_target_pairs={{0,32},{32,0},{1,33},{33,1},{2,34},{34,2},{3,35},{35,3},{4,36},{36... | collective-permute-start | bytes 983048 | tf_op jit(solution)/shard_map/ppermute | solution.py:92
  60.6 1.3 %collective-permute-done.2 = f32[81920]{0:T(1024)S(1)} collective-permute-done((f32[81920]{0:T(1024)S(1)}, f32[81920]{0:T(1024)S(1)}, u32[]{:S(2)}, u32[]{:S(2)}) %collective-permute-start.2) | collective-permute-done | bytes 327712 | tf_op jit(solution)/shard_map/ppermute | solution.py:92
  61.9 27.0 %all_to_all.42 = f32[128,1,640]{2,1,0:T(1,128)S(1)} all-to-all(f32[128,1,640]{2,1,0:T(1,128)S(1)} %bitcast.187), channel_id=1, replica_groups=mesh['group'=4,'core'=2,'tile'=32] {'group','tile'}, dimensions={0} | all-to-all | bytes 655360 | tf_op jit(solution)/shard_map/all_to_all | solution.py:93
  89.1 0.9 broadcast_in_dim.32
  90.0 6.2 %all-to-all-start.3 = ((f32[128,1,640]{2,1,0:T(1,128)}), f32[128,1,640]{2,1,0:T(1,128)S(1)}, u32[]{:S(2)}, u32[]{:S(2)}) async-start(f32[128,1,640]{2,1,0:T(1,128)} %broadcast_in_dim.32), calls=%async_computation.3 | async-start | bytes 655360 | tf_op jit(solution)/shard_map/all_to_all | solution.py:95
  96.7 13.4 %all-to-all-done.3 = f32[128,1,640]{2,1,0:T(1,128)S(1)} async-done(((f32[128,1,640]{2,1,0:T(1,128)}), f32[128,1,640]{2,1,0:T(1,128)S(1)}, u32[]{:S(2)}, u32[]{:S(2)}) %all-to-all-start.3) | async-done | bytes 327712 | tf_op jit(solution)/shard_map/all_to_all | solution.py:95
  110.1 3.5 %collective-permute-start.3 = (f32[81920]{0:T(1024)S(1)}, f32[81920]{0:T(1024)S(1)}, u32[]{:S(2)}, u32[]{:S(2)}) collective-permute-start(f32[81920]{0:T(1024)S(1)} %bitcast.183), channel_id=1, source_target_pairs={{0,32},{32,0},{1,33},{33,1},{2,34},{34,2},{3,35},{35,3},{4,36},{36... | collective-permute-start | bytes 983048 | tf_op jit(solution)/shard_map/ppermute | solution.py:97
  113.7 0.6 copy.102
  114.9 0.9 slice.202
  116.2 0.6 fusion.49
  (71 shorter events, 10.0 us)
Async XLA Ops:
  0.6 11.3 %copy-start = (bf16[3,3,32,128]{3,2,1,0:T(8,128)(2,1)S(1)}, bf16[3,3,32,128]{3,2,1,0:T(8,128)(2,1)}, u32[]{:S(2)}) copy-start(bf16[3,3,32,128]{3,2,1,0:T(8,128)(2,1)} %param.17) | copy-start | bytes 221188
  0.6 10.5 %copy-start.1 = (bf16[4,32,256]{2,1,0:T(8,128)(2,1)S(1)}, bf16[4,32,256]{2,1,0:T(8,128)(2,1)}, u32[]{:S(2)}) copy-start(bf16[4,32,256]{2,1,0:T(8,128)(2,1)} %param.11) | copy-start | bytes 196612
  1.6 9.6 %collective-permute-start = (bf16[3,32,256]{2,1,0:T(8,128)(2,1)S(1)}, bf16[3,32,256]{2,1,0:T(8,128)(2,1)S(1)}, u32[]{:S(2)}, u32[]{:S(2)}) collective-permute-start(bf16[3,32,256]{2,1,0:T(8,128)(2,1)S(1)} %get-tuple-element.35), channel_id=1, source_target_pairs={{0,1},{1,2},{2,3},{3,4},{4,5},{5,6},{6,7},{7,8},{8,9},{9,10},{10,1... | collective-permute-start | bytes 147464 | tf_op jit(solution)/shard_map/ppermute | solution.py:19
  5.9 5.3 %collective-permute-start.1 = (bf16[3,32,256]{2,1,0:T(8,128)(2,1)S(1)}, bf16[3,32,256]{2,1,0:T(8,128)(2,1)S(1)}, u32[]{:S(2)}, u32[]{:S(2)}) collective-permute-start(bf16[3,32,256]{2,1,0:T(8,128)(2,1)S(1)} %get-tuple-element.34), channel_id=1, source_target_pairs={{1,0},{2,1},{3,2},{4,3},{5,4},{6,5},{7,6},{8,7},{9,8},{10,9},{11,1... | collective-permute-start | bytes 147464 | tf_op jit(solution)/shard_map/ppermute | solution.py:20
  18.9 0.9 copy-start.2
  18.9 0.9 copy-start.3
  20.8 17.6 %all-to-all-start = ((bf16[32,2,4,256]{3,2,1,0:T(4,128)(2,1)}), bf16[32,2,4,256]{3,2,1,0:T(4,128)(2,1)S(1)}, u32[]{:S(2)}, u32[]{:S(2)}) async-start(bf16[32,2,4,256]{3,2,1,0:T(4,128)(2,1)} %copy.82), calls=%async_computation | async-start | bytes 262144 | tf_op jit(solution)/shard_map/all_to_all | solution.py:158
  41.4 13.1 %all-to-all-start.1 = ((bf16[4,16,4,256]{3,2,0,1:T(4,128)(2,1)}), bf16[4,16,4,256]{3,2,0,1:T(4,128)(2,1)S(1)}, u32[]{:S(2)}, u32[]{:S(2)}) async-start(bf16[4,16,4,256]{3,2,0,1:T(4,128)(2,1)} %copy.88), calls=%async_computation.1 | async-start | bytes 262144 | tf_op jit(solution)/shard_map/all_to_all | solution.py:181
  59.3 2.5 %collective-permute-start.2 = (f32[81920]{0:T(1024)S(1)}, f32[81920]{0:T(1024)S(1)}, u32[]{:S(2)}, u32[]{:S(2)}) collective-permute-start(f32[81920]{0:T(1024)S(1)} %slice_select_fusion), channel_id=1, source_target_pairs={{0,32},{32,0},{1,33},{33,1},{2,34},{34,2},{3,35},{35,3},{4,36},{36... | collective-permute-start | bytes 983048 | tf_op jit(solution)/shard_map/ppermute | solution.py:92
  90.0 20.1 %all-to-all-start.3 = ((f32[128,1,640]{2,1,0:T(1,128)}), f32[128,1,640]{2,1,0:T(1,128)S(1)}, u32[]{:S(2)}, u32[]{:S(2)}) async-start(f32[128,1,640]{2,1,0:T(1,128)} %broadcast_in_dim.32), calls=%async_computation.3 | async-start | bytes 655360 | tf_op jit(solution)/shard_map/all_to_all | solution.py:95
  110.1 4.7 %collective-permute-start.3 = (f32[81920]{0:T(1024)S(1)}, f32[81920]{0:T(1024)S(1)}, u32[]{:S(2)}, u32[]{:S(2)}) collective-permute-start(f32[81920]{0:T(1024)S(1)} %bitcast.183), channel_id=1, source_target_pairs={{0,32},{32,0},{1,33},{33,1},{2,34},{34,2},{3,35},{35,3},{4,36},{36... | collective-permute-start | bytes 983048 | tf_op jit(solution)/shard_map/ppermute | solution.py:97

commit v14 on v12

--- a/solution.py
+++ b/solution.py
@@ -14,10 +14,8 @@
         devices, length = (lax.axis_size(axis), x.shape[dim])
         up = [(i, (i + 1) % devices) for i in range(devices - 1)]
         down = [(j, i) for i, j in up]
-        last = lax.slice_in_dim(x, length - width, length, axis=dim)
-        first = lax.slice_in_dim(x, 0, width, axis=dim)
-        before = lax.ppermute(last, axis, up)
-        after = lax.ppermute(first, axis, down)
+        before = lax.slice_in_dim(lax.ppermute(x, axis, up), length - width, length, axis=dim)
+        after = lax.slice_in_dim(lax.ppermute(x, axis, down), 0, width, axis=dim)
         x = jnp.concatenate([before, x, after], axis=dim)
     return x
 

time: 117 us -> 116 us (level)
  no operation moved by 1% of the time
where the time goes in v14:
time: 116 us
  blocking collectives  46.7 us (40%)
  starting transfers between devices  23.6 us (20%)
  waiting for transfers between devices  17.4 us (15%)
  matrix products  11.4 us (10%)
  local copies, waits for them, and re-layouts  8.12 us (7%)
  other arithmetic  6.7 us (6%)
  between operations  1.76 us (2%)
    all_to_all x1, blocking collectives, all_reduce_sum(): lax.all_to_all(half.reshape(devices, width), peers, 0, 0, tiled=True)  27 us
    all_to_all x1, blocking collectives, all_reduce_sum(): lax.all_to_all(jnp.broadcast_to(own, (devices, width)), peers, 0, 0, tile...  19.7 us
    all_to_all x1, starting transfers between devices, on_device(): lax.all_to_all(sample_prediction, MEMBER, split_axis=0, concat_axis=1, ti...  8.74 us
    all_to_all x1, waiting for transfers between devices, on_device(): lax.all_to_all(cot_share, MEMBER, split_axis=1, concat_axis=0, tiled=True)  8.71 us
    all_to_all x1, waiting for transfers between devices, on_device(): lax.all_to_all(sample_prediction, MEMBER, split_axis=0, concat_axis=1, ti...  6.9 us
    dot_general x6, matrix products, feature_conv(): jnp.einsum('mrwc,cd->mrwd', shifted[:, i:i + out_rows], kernel[i].reshape...  4.72 us
    ppermute x1, starting transfers between devices, extended(): lax.ppermute(x, axis, up)  4.49 us
    all_to_all x1, starting transfers between devices, on_device(): lax.all_to_all(cot_share, MEMBER, split_axis=1, concat_axis=0, tiled=True)  4.35 us
  transfers between devices with their start and end apart: 6, of which 4 were waited for; matrix products, arithmetic and copies ran while one was open for 5% of the time, Pallas kernels for 0%

profile of v14, /device:TPU:1, one launch (start us, length us, event | category | flops | bytes accessed | tf_op | source)
XLA Modules:
  0.0 115.7 jit_solution(16159178789868517133)
XLA Ops:
  0.7 4.5 %collective-permute-start = (bf16[4,32,256]{2,1,0:T(8,128)(2,1)}, bf16[4,32,256]{2,1,0:T(8,128)(2,1)S(1)}, u32[]{:S(2)}, u32[]{:S(2)}) collective-permute-start(bf16[4,32,256]{2,1,0:T(8,128)(2,1)} %param.11), channel_id=1, source_target_pairs={{0,1},{1,2},{2,3},{3,4},{4,5},{5,6},{6,7},{7,8},{8,9},{9,10},{10,1... | collective-permute-start | bytes 196616 | tf_op jit(solution)/shard_map/ppermute | solution.py:17
  5.2 1.3 %collective-permute-start.1 = (bf16[4,32,256]{2,1,0:T(8,128)(2,1)}, bf16[4,32,256]{2,1,0:T(8,128)(2,1)S(1)}, u32[]{:S(2)}, u32[]{:S(2)}) collective-permute-start(bf16[4,32,256]{2,1,0:T(8,128)(2,1)} %param.11), channel_id=1, source_target_pairs={{1,0},{2,1},{3,2},{4,3},{5,4},{6,5},{7,6},{8,7},{9,8},{10,9},{11,1... | collective-permute-start | bytes 196616 | tf_op jit(solution)/shard_map/ppermute | solution.py:18
  6.5 0.9 convert_bitcast_fusion
  7.3 0.9 fusion.54
  8.2 0.8 fusion.70
  9.1 1.0 fusion.68
  10.2 1.0 fusion.67
  13.1 0.9 fusion.22
  14.0 0.6 pad_slice_fusion.1
  14.6 0.8 fusion.65
  15.4 0.8 fusion.66
  16.2 1.2 fusion.21
  17.8 0.6 fusion.64
  18.4 0.6 convolution_add_fusion.1
  19.0 0.8 add_convert_fusion
  20.2 0.8 copy.97
  20.9 8.7 %all-to-all-start = ((bf16[32,2,4,256]{3,2,1,0:T(4,128)(2,1)}), bf16[32,2,4,256]{3,2,1,0:T(4,128)(2,1)S(1)}, u32[]{:S(2)}, u32[]{:S(2)}) async-start(bf16[32,2,4,256]{3,2,1,0:T(4,128)(2,1)} %copy.97), calls=%async_computation | async-start | bytes 262144 | tf_op jit(solution)/shard_map/all_to_all | solution.py:156
  29.7 0.7 convert_bitcast_fusion.1
  31.1 6.9 %all-to-all-done = bf16[32,2,4,256]{3,2,1,0:T(4,128)(2,1)S(1)} async-done(((bf16[32,2,4,256]{3,2,1,0:T(4,128)(2,1)}), bf16[32,2,4,256]{3,2,1,0:T(4,128)(2,1)S(1)}, u32[]{:S(2)}, u32[]{:S(2)}) %all-to-all-start) | async-done | bytes 131104 | tf_op jit(solution)/shard_map/all_to_all | solution.py:156
  38.1 2.3 %fusion.1 = (f32[4,16,4,256]{3,2,1,0:T(4,128)S(1)}, f32[4,4,256]{2,1,0:T(4,128)S(1)}) fusion(f32[4,16,4,256]{3,1,2,0:T(8,128)S(1)} %copy.100, f32[4,16,4,256]{3,2,1,0:T(4,128)S(1)} %bitcast.175), kind=kLoop, calls=%fused_computation.3 | loop fusion | flops 5173248 | bytes 802816 | tf_op jit(solution)/shard_map/reduce_sum | solution.py:166
  40.6 0.7 copy.102
  41.3 4.3 %all-to-all-start.1 = ((bf16[4,16,4,256]{3,2,0,1:T(4,128)(2,1)}), bf16[4,16,4,256]{3,2,0,1:T(4,128)(2,1)S(1)}, u32[]{:S(2)}, u32[]{:S(2)}) async-start(bf16[4,16,4,256]{3,2,0,1:T(4,128)(2,1)} %copy.102), calls=%async_computation.1 | async-start | bytes 262144 | tf_op jit(solution)/shard_map/all_to_all | solution.py:178
  45.7 8.7 %all-to-all-done.1 = bf16[4,16,4,256]{3,2,0,1:T(4,128)(2,1)S(1)} async-done(((bf16[4,16,4,256]{3,2,0,1:T(4,128)(2,1)}), bf16[4,16,4,256]{3,2,0,1:T(4,128)(2,1)S(1)}, u32[]{:S(2)}, u32[]{:S(2)}) %all-to-all-start.1) | async-done | bytes 131104 | tf_op jit(solution)/shard_map/all_to_all | solution.py:178
  54.7 0.9 fusion.29
  59.3 1.3 %collective-permute-start.2 = (f32[81920]{0:T(1024)S(1)}, f32[81920]{0:T(1024)S(1)}, u32[]{:S(2)}, u32[]{:S(2)}) collective-permute-start(f32[81920]{0:T(1024)S(1)} %slice_select_fusion), channel_id=1, source_target_pairs={{0,32},{32,0},{1,33},{33,1},{2,34},{34,2},{3,35},{35,3},{4,36},{36... | collective-permute-start | bytes 983048 | tf_op jit(solution)/shard_map/ppermute | solution.py:90
  60.5 1.3 %collective-permute-done.2 = f32[81920]{0:T(1024)S(1)} collective-permute-done((f32[81920]{0:T(1024)S(1)}, f32[81920]{0:T(1024)S(1)}, u32[]{:S(2)}, u32[]{:S(2)}) %collective-permute-start.2) | collective-permute-done | bytes 327712 | tf_op jit(solution)/shard_map/ppermute | solution.py:90
  61.9 27.0 %all_to_all.42 = f32[128,1,640]{2,1,0:T(1,128)S(1)} all-to-all(f32[128,1,640]{2,1,0:T(1,128)S(1)} %bitcast.181), channel_id=1, replica_groups=mesh['group'=4,'core'=2,'tile'=32] {'group','tile'}, dimensions={0} | all-to-all | bytes 655360 | tf_op jit(solution)/shard_map/all_to_all | solution.py:91
  89.3 19.7 %all_to_all.43 = f32[128,1,640]{2,1,0:T(1,128)S(1)} all-to-all(f32[128,1,640]{2,1,0:T(1,128)S(1)} %broadcast_in_dim.29), channel_id=1, replica_groups=mesh['group'=4,'core'=2,'tile'=32] {'group','tile'}, dimensions={0} | all-to-all | bytes 655360 | tf_op jit(solution)/shard_map/all_to_all | solution.py:93
  109.0 3.4 %collective-permute-start.3 = (f32[81920]{0:T(1024)S(1)}, f32[81920]{0:T(1024)S(1)}, u32[]{:S(2)}, u32[]{:S(2)}) collective-permute-start(f32[81920]{0:T(1024)S(1)} %bitcast.177), channel_id=1, source_target_pairs={{0,32},{32,0},{1,33},{33,1},{2,34},{34,2},{3,35},{35,3},{4,36},{36... | collective-permute-start | bytes 983048 | tf_op jit(solution)/shard_map/ppermute | solution.py:95
  112.5 0.6 copy.116
  113.7 0.9 slice.204
  115.1 0.6 fusion.51
  (68 shorter events, 8.5 us)
Async XLA Ops:
  0.6 11.4 %copy-start = (bf16[3,3,32,128]{3,2,1,0:T(8,128)(2,1)S(1)}, bf16[3,3,32,128]{3,2,1,0:T(8,128)(2,1)}, u32[]{:S(2)}) copy-start(bf16[3,3,32,128]{3,2,1,0:T(8,128)(2,1)} %param.17) | copy-start | bytes 221188
  0.6 10.6 %copy-start.1 = (bf16[4,32,256]{2,1,0:T(8,128)(2,1)S(1)}, bf16[4,32,256]{2,1,0:T(8,128)(2,1)}, u32[]{:S(2)}) copy-start(bf16[4,32,256]{2,1,0:T(8,128)(2,1)} %param.11) | copy-start | bytes 196612
  0.7 10.6 %collective-permute-start = (bf16[4,32,256]{2,1,0:T(8,128)(2,1)}, bf16[4,32,256]{2,1,0:T(8,128)(2,1)S(1)}, u32[]{:S(2)}, u32[]{:S(2)}) collective-permute-start(bf16[4,32,256]{2,1,0:T(8,128)(2,1)} %param.11), channel_id=1, source_target_pairs={{0,1},{1,2},{2,3},{3,4},{4,5},{5,6},{6,7},{7,8},{8,9},{9,10},{10,1... | collective-permute-start | bytes 196616 | tf_op jit(solution)/shard_map/ppermute | solution.py:17
  5.2 6.1 %collective-permute-start.1 = (bf16[4,32,256]{2,1,0:T(8,128)(2,1)}, bf16[4,32,256]{2,1,0:T(8,128)(2,1)S(1)}, u32[]{:S(2)}, u32[]{:S(2)}) collective-permute-start(bf16[4,32,256]{2,1,0:T(8,128)(2,1)} %param.11), channel_id=1, source_target_pairs={{1,0},{2,1},{3,2},{4,3},{5,4},{6,5},{7,6},{8,7},{9,8},{10,9},{11,1... | collective-permute-start | bytes 196616 | tf_op jit(solution)/shard_map/ppermute | solution.py:18
  19.0 0.9 copy-start.2
  19.0 0.9 copy-start.3
  20.9 17.1 %all-to-all-start = ((bf16[32,2,4,256]{3,2,1,0:T(4,128)(2,1)}), bf16[32,2,4,256]{3,2,1,0:T(4,128)(2,1)S(1)}, u32[]{:S(2)}, u32[]{:S(2)}) async-start(bf16[32,2,4,256]{3,2,1,0:T(4,128)(2,1)} %copy.97), calls=%async_computation | async-start | bytes 262144 | tf_op jit(solution)/shard_map/all_to_all | solution.py:156
  41.3 13.1 %all-to-all-start.1 = ((bf16[4,16,4,256]{3,2,0,1:T(4,128)(2,1)}), bf16[4,16,4,256]{3,2,0,1:T(4,128)(2,1)S(1)}, u32[]{:S(2)}, u32[]{:S(2)}) async-start(bf16[4,16,4,256]{3,2,0,1:T(4,128)(2,1)} %copy.102), calls=%async_computation.1 | async-start | bytes 262144 | tf_op jit(solution)/shard_map/all_to_all | solution.py:178
  59.3 2.5 %collective-permute-start.2 = (f32[81920]{0:T(1024)S(1)}, f32[81920]{0:T(1024)S(1)}, u32[]{:S(2)}, u32[]{:S(2)}) collective-permute-start(f32[81920]{0:T(1024)S(1)} %slice_select_fusion), channel_id=1, source_target_pairs={{0,32},{32,0},{1,33},{33,1},{2,34},{34,2},{3,35},{35,3},{4,36},{36... | collective-permute-start | bytes 983048 | tf_op jit(solution)/shard_map/ppermute | solution.py:90
  109.0 4.6 %collective-permute-start.3 = (f32[81920]{0:T(1024)S(1)}, f32[81920]{0:T(1024)S(1)}, u32[]{:S(2)}, u32[]{:S(2)}) collective-permute-start(f32[81920]{0:T(1024)S(1)} %bitcast.177), channel_id=1, source_target_pairs={{0,32},{32,0},{1,33},{33,1},{2,34},{34,2},{3,35},{35,3},{4,36},{36... | collective-permute-start | bytes 983048 | tf_op jit(solution)/shard_map/ppermute | solution.py:95

commit v15 on v14

--- a/solution.py
+++ b/solution.py
@@ -182,7 +182,8 @@
     bias_grad = jnp.sum(cotangent.astype(jnp.float32), axis=(1, 2, 3))
     back = jnp.einsum("vmrw,cv->mrwc", cotangent, head_weight, preferred_element_type=jnp.float32)
     unused_out, pullback = jax.vjp(jax.nn.gelu, final_linear_response)
-    d_pre = pullback(back)[0].astype(jnp.bfloat16)
+    slope = lax.optimization_barrier(pullback(jnp.ones_like(final_linear_response))[0])
+    d_pre = (back * slope).astype(jnp.bfloat16)
     second_wide = jnp.pad(second_padded, ((0, 0), (0, 0), (1, 1), (0, 0)))
     rows_of = []
     for i in range(3):

time: 116 us -> 116 us (level)
  no operation moved by 1% of the time
where the time goes in v15:
time: 116 us
  blocking collectives  46.7 us (40%)
  starting transfers between devices  23.6 us (20%)
  waiting for transfers between devices  17.4 us (15%)
  matrix products  11.4 us (10%)
  local copies, waits for them, and re-layouts  8.12 us (7%)
  other arithmetic  6.7 us (6%)
  between operations  1.76 us (2%)
    all_to_all x1, blocking collectives, all_reduce_sum(): lax.all_to_all(half.reshape(devices, width), peers, 0, 0, tiled=True)  27 us
    all_to_all x1, blocking collectives, all_reduce_sum(): lax.all_to_all(jnp.broadcast_to(own, (devices, width)), peers, 0, 0, tile...  19.7 us
    all_to_all x1, starting transfers between devices, on_device(): lax.all_to_all(sample_prediction, MEMBER, split_axis=0, concat_axis=1, ti...  8.75 us
    all_to_all x1, waiting for transfers between devices, on_device(): lax.all_to_all(cot_share, MEMBER, split_axis=1, concat_axis=0, tiled=True)  8.71 us
    all_to_all x1, waiting for transfers between devices, on_device(): lax.all_to_all(sample_prediction, MEMBER, split_axis=0, concat_axis=1, ti...  6.9 us
    dot_general x6, matrix products, feature_conv(): jnp.einsum('mrwc,cd->mrwd', shifted[:, i:i + out_rows], kernel[i].reshape...  5.26 us
    ppermute x1, starting transfers between devices, extended(): lax.ppermute(x, axis, up)  4.49 us
    all_to_all x1, starting transfers between devices, on_device(): lax.all_to_all(cot_share, MEMBER, split_axis=1, concat_axis=0, tiled=True)  4.35 us
  transfers between devices with their start and end apart: 6, of which 4 were waited for; matrix products, arithmetic and copies ran while one was open for 5% of the time, Pallas kernels for 0%

profile of v15, /device:TPU:1, one launch (start us, length us, event | category | flops | bytes accessed | tf_op | source)
XLA Modules:
  0.0 115.7 jit_solution(1448701602072918489)
XLA Ops:
  0.7 4.5 %collective-permute-start = (bf16[4,32,256]{2,1,0:T(8,128)(2,1)}, bf16[4,32,256]{2,1,0:T(8,128)(2,1)S(1)}, u32[]{:S(2)}, u32[]{:S(2)}) collective-permute-start(bf16[4,32,256]{2,1,0:T(8,128)(2,1)} %param.11), channel_id=1, source_target_pairs={{0,1},{1,2},{2,3},{3,4},{4,5},{5,6},{6,7},{7,8},{8,9},{9,10},{10,1... | collective-permute-start | bytes 196616 | tf_op jit(solution)/shard_map/ppermute | solution.py:17
  5.2 1.3 %collective-permute-start.1 = (bf16[4,32,256]{2,1,0:T(8,128)(2,1)}, bf16[4,32,256]{2,1,0:T(8,128)(2,1)S(1)}, u32[]{:S(2)}, u32[]{:S(2)}) collective-permute-start(bf16[4,32,256]{2,1,0:T(8,128)(2,1)} %param.11), channel_id=1, source_target_pairs={{1,0},{2,1},{3,2},{4,3},{5,4},{6,5},{7,6},{8,7},{9,8},{10,9},{11,1... | collective-permute-start | bytes 196616 | tf_op jit(solution)/shard_map/ppermute | solution.py:18
  6.5 0.9 convert_bitcast_fusion
  7.3 0.9 fusion.54
  8.2 0.8 fusion.70
  9.1 1.0 fusion.68
  10.2 1.0 fusion.67
  13.1 0.9 fusion.23
  14.0 0.6 pad_slice_fusion.1
  14.6 0.8 fusion.65
  15.4 0.8 fusion.66
  16.2 1.2 %fusion.22 = bf16[2,6,256,128]{3,2,1,0:T(8,128)(2,1)S(1)} fusion(bf16[384,128,1,1]{1,0,3,2:T(8,128)(2,1)S(1)} %bitcast.189, f32[2,6,256,128]{3,2,1,0:T(8,128)S(1)} %fusion.66, f32[2,6,256,128]{3,2,1,0:T(8,128)S(1)} %fusion.65, pred[6]{0:T(512)(128)(4,1)S(1)} %slice_bitcast_fusion, bf16[2,8,256,128]{3,2,1,0:T(8,128)(2,1)S(1)} %get-tuple-element.21, ...), kind=kOutput, calls=%fused_computation.44 | convolution fusion | flops 316145664 | bytes 7176198 | tf_op jit(solution)/shard_map/mrwc,cd->mrwd/dot_general | solution.py:45
  17.8 0.6 fusion.64
  18.4 0.6 convolution_add_fusion.1
  19.0 1.4 %fusion.29 = (f32[2,4,256,128]{3,2,1,0:T(8,128)S(1)}, bf16[2,4,256,128]{3,2,1,0:T(8,128)(2,1)S(1)}) fusion(bf16[2,8,256,128]{3,2,1,0:T(8,128)(2,1)S(1)} %fusion.23, f32[2,4,256,128]{3,2,1,0:T(8,128)S(1)} %convolution_add_fusion.1, bf16[384,128,1,1]{1,0,3,2:T(8,128)(2,1)S(1)} %bitcast.186, bf16[2,6,256,128]{3,2,1,0:T(8,128)(2,1)S(1)} %get-tuple-element.23, ...), kind=kOutput, calls=%fused_computation.51 | convolution fusion | flops 214171648 | bytes 5603328 | tf_op jit(solution)/shard_map/mrwc,cd->mrwd/dot_general | solution.py:45
  20.7 0.8 copy.97
  21.5 8.8 %all-to-all-start = ((bf16[32,2,4,256]{3,2,1,0:T(4,128)(2,1)}), bf16[32,2,4,256]{3,2,1,0:T(4,128)(2,1)S(1)}, u32[]{:S(2)}, u32[]{:S(2)}) async-start(bf16[32,2,4,256]{3,2,1,0:T(4,128)(2,1)} %copy.97), calls=%async_computation | async-start | bytes 262144 | tf_op jit(solution)/shard_map/all_to_all | solution.py:156
  30.2 0.7 convert_bitcast_fusion.1
  31.6 6.9 %all-to-all-done = bf16[32,2,4,256]{3,2,1,0:T(4,128)(2,1)S(1)} async-done(((bf16[32,2,4,256]{3,2,1,0:T(4,128)(2,1)}), bf16[32,2,4,256]{3,2,1,0:T(4,128)(2,1)S(1)}, u32[]{:S(2)}, u32[]{:S(2)}) %all-to-all-start) | async-done | bytes 131104 | tf_op jit(solution)/shard_map/all_to_all | solution.py:156
  38.6 2.3 %fusion.1 = (f32[4,16,4,256]{3,2,1,0:T(4,128)S(1)}, f32[4,4,256]{2,1,0:T(4,128)S(1)}) fusion(f32[4,16,4,256]{3,1,2,0:T(8,128)S(1)} %copy.100, f32[4,16,4,256]{3,2,1,0:T(4,128)S(1)} %bitcast.175), kind=kLoop, calls=%fused_computation.3 | loop fusion | flops 5173248 | bytes 802816 | tf_op jit(solution)/shard_map/reduce_sum | solution.py:166
  41.2 0.7 copy.102
  41.9 4.3 %all-to-all-start.1 = ((bf16[4,16,4,256]{3,2,0,1:T(4,128)(2,1)}), bf16[4,16,4,256]{3,2,0,1:T(4,128)(2,1)S(1)}, u32[]{:S(2)}, u32[]{:S(2)}) async-start(bf16[4,16,4,256]{3,2,0,1:T(4,128)(2,1)} %copy.102), calls=%async_computation.1 | async-start | bytes 262144 | tf_op jit(solution)/shard_map/all_to_all | solution.py:178
  46.2 8.7 %all-to-all-done.1 = bf16[4,16,4,256]{3,2,0,1:T(4,128)(2,1)S(1)} async-done(((bf16[4,16,4,256]{3,2,0,1:T(4,128)(2,1)}), bf16[4,16,4,256]{3,2,0,1:T(4,128)(2,1)S(1)}, u32[]{:S(2)}, u32[]{:S(2)}) %all-to-all-start.1) | async-done | bytes 131104 | tf_op jit(solution)/shard_map/all_to_all | solution.py:178
  59.3 1.3 %collective-permute-start.2 = (f32[81920]{0:T(1024)S(1)}, f32[81920]{0:T(1024)S(1)}, u32[]{:S(2)}, u32[]{:S(2)}) collective-permute-start(f32[81920]{0:T(1024)S(1)} %slice_select_fusion), channel_id=1, source_target_pairs={{0,32},{32,0},{1,33},{33,1},{2,34},{34,2},{3,35},{35,3},{4,36},{36... | collective-permute-start | bytes 983048 | tf_op jit(solution)/shard_map/ppermute | solution.py:90
  60.6 1.3 %collective-permute-done.2 = f32[81920]{0:T(1024)S(1)} collective-permute-done((f32[81920]{0:T(1024)S(1)}, f32[81920]{0:T(1024)S(1)}, u32[]{:S(2)}, u32[]{:S(2)}) %collective-permute-start.2) | collective-permute-done | bytes 327712 | tf_op jit(solution)/shard_map/ppermute | solution.py:90
  61.9 27.0 %all_to_all.42 = f32[128,1,640]{2,1,0:T(1,128)S(1)} all-to-all(f32[128,1,640]{2,1,0:T(1,128)S(1)} %bitcast.181), channel_id=1, replica_groups=mesh['group'=4,'core'=2,'tile'=32] {'group','tile'}, dimensions={0} | all-to-all | bytes 655360 | tf_op jit(solution)/shard_map/all_to_all | solution.py:91
  89.3 19.7 %all_to_all.43 = f32[128,1,640]{2,1,0:T(1,128)S(1)} all-to-all(f32[128,1,640]{2,1,0:T(1,128)S(1)} %broadcast_in_dim.29), channel_id=1, replica_groups=mesh['group'=4,'core'=2,'tile'=32] {'group','tile'}, dimensions={0} | all-to-all | bytes 655360 | tf_op jit(solution)/shard_map/all_to_all | solution.py:93
  109.0 3.4 %collective-permute-start.3 = (f32[81920]{0:T(1024)S(1)}, f32[81920]{0:T(1024)S(1)}, u32[]{:S(2)}, u32[]{:S(2)}) collective-permute-start(f32[81920]{0:T(1024)S(1)} %bitcast.177), channel_id=1, source_target_pairs={{0,32},{32,0},{1,33},{33,1},{2,34},{34,2},{3,35},{35,3},{4,36},{36... | collective-permute-start | bytes 983048 | tf_op jit(solution)/shard_map/ppermute | solution.py:95
  112.5 0.6 copy.116
  113.1 0.5 collective-permute-done.3
  113.7 0.9 slice.204
  115.1 0.6 fusion.51
  (68 shorter events, 8.3 us)
Async XLA Ops:
  0.6 11.4 %copy-start = (bf16[3,3,32,128]{3,2,1,0:T(8,128)(2,1)S(1)}, bf16[3,3,32,128]{3,2,1,0:T(8,128)(2,1)}, u32[]{:S(2)}) copy-start(bf16[3,3,32,128]{3,2,1,0:T(8,128)(2,1)} %param.17) | copy-start | bytes 221188
  0.6 10.6 %copy-start.1 = (bf16[4,32,256]{2,1,0:T(8,128)(2,1)S(1)}, bf16[4,32,256]{2,1,0:T(8,128)(2,1)}, u32[]{:S(2)}) copy-start(bf16[4,32,256]{2,1,0:T(8,128)(2,1)} %param.11) | copy-start | bytes 196612
  0.7 10.6 %collective-permute-start = (bf16[4,32,256]{2,1,0:T(8,128)(2,1)}, bf16[4,32,256]{2,1,0:T(8,128)(2,1)S(1)}, u32[]{:S(2)}, u32[]{:S(2)}) collective-permute-start(bf16[4,32,256]{2,1,0:T(8,128)(2,1)} %param.11), channel_id=1, source_target_pairs={{0,1},{1,2},{2,3},{3,4},{4,5},{5,6},{6,7},{7,8},{8,9},{9,10},{10,1... | collective-permute-start | bytes 196616 | tf_op jit(solution)/shard_map/ppermute | solution.py:17
  5.2 6.1 %collective-permute-start.1 = (bf16[4,32,256]{2,1,0:T(8,128)(2,1)}, bf16[4,32,256]{2,1,0:T(8,128)(2,1)S(1)}, u32[]{:S(2)}, u32[]{:S(2)}) collective-permute-start(bf16[4,32,256]{2,1,0:T(8,128)(2,1)} %param.11), channel_id=1, source_target_pairs={{1,0},{2,1},{3,2},{4,3},{5,4},{6,5},{7,6},{8,7},{9,8},{10,9},{11,1... | collective-permute-start | bytes 196616 | tf_op jit(solution)/shard_map/ppermute | solution.py:18
  19.0 1.4 %copy-start.2 = (bf16[128,32]{0,1:T(8,128)(2,1)S(1)}, bf16[128,32]{0,1:T(8,128)(2,1)}, u32[]{:S(2)}) copy-start(bf16[128,32]{0,1:T(8,128)(2,1)} %param.20) | copy-start | bytes 24580
  19.0 1.4 %copy-start.3 = (f32[32]{0:T(128)S(1)}, f32[32]{0:T(128)}, u32[]{:S(2)}) copy-start(f32[32]{0:T(128)} %param.21) | copy-start | bytes 388
  21.5 17.1 %all-to-all-start = ((bf16[32,2,4,256]{3,2,1,0:T(4,128)(2,1)}), bf16[32,2,4,256]{3,2,1,0:T(4,128)(2,1)S(1)}, u32[]{:S(2)}, u32[]{:S(2)}) async-start(bf16[32,2,4,256]{3,2,1,0:T(4,128)(2,1)} %copy.97), calls=%async_computation | async-start | bytes 262144 | tf_op jit(solution)/shard_map/all_to_all | solution.py:156
  41.9 13.1 %all-to-all-start.1 = ((bf16[4,16,4,256]{3,2,0,1:T(4,128)(2,1)}), bf16[4,16,4,256]{3,2,0,1:T(4,128)(2,1)S(1)}, u32[]{:S(2)}, u32[]{:S(2)}) async-start(bf16[4,16,4,256]{3,2,0,1:T(4,128)(2,1)} %copy.102), calls=%async_computation.1 | async-start | bytes 262144 | tf_op jit(solution)/shard_map/all_to_all | solution.py:178
  59.3 2.6 %collective-permute-start.2 = (f32[81920]{0:T(1024)S(1)}, f32[81920]{0:T(1024)S(1)}, u32[]{:S(2)}, u32[]{:S(2)}) collective-permute-start(f32[81920]{0:T(1024)S(1)} %slice_select_fusion), channel_id=1, source_target_pairs={{0,32},{32,0},{1,33},{33,1},{2,34},{34,2},{3,35},{35,3},{4,36},{36... | collective-permute-start | bytes 983048 | tf_op jit(solution)/shard_map/ppermute | solution.py:90
  109.0 4.6 %collective-permute-start.3 = (f32[81920]{0:T(1024)S(1)}, f32[81920]{0:T(1024)S(1)}, u32[]{:S(2)}, u32[]{:S(2)}) collective-permute-start(f32[81920]{0:T(1024)S(1)} %bitcast.177), channel_id=1, source_target_pairs={{0,32},{32,0},{1,33},{33,1},{2,34},{34,2},{3,35},{35,3},{4,36},{36... | collective-permute-start | bytes 983048 | tf_op jit(solution)/shard_map/ppermute | solution.py:95

commit v16 on v14

--- a/solution.py
+++ b/solution.py
@@ -162,9 +162,10 @@
         lax.dynamic_slice_in_dim(target, var_start, var_share, 1), (1, 0, 2)
     ).astype(jnp.float32)[:, None]
     pair_differ = sample_group_predictions[:, :, None] - sample_group_predictions[:, None, :]
-    abs_sums = jnp.sum(jnp.abs(pair_differ), axis=2)
     sign_sums = jnp.sum(jnp.sign(pair_differ), axis=2)
-    crps_share = jnp.mean(jnp.abs(sample_group_predictions - truth), axis=1) - jnp.sum(
+    scored, scored_truth = lax.optimization_barrier((sample_group_predictions, truth))
+    abs_sums = jnp.sum(jnp.abs(scored[:, :, None] - scored[:, None, :]), axis=2)
+    crps_share = jnp.mean(jnp.abs(scored - scored_truth), axis=1) - jnp.sum(
         abs_sums, axis=1
     ) / (2 * member_count * (member_count - 1))
     crps_map = jnp.transpose(crps_share, (1, 0, 2))

time: 116 us -> 117 us (level)
  blocking collectives: 46.7 us -> 27 us
  waiting for transfers between devices: 17.4 us -> 30.8 us
  starting transfers between devices: 23.6 us -> 29.8 us
    all_to_all x1 -> x0, blocking collectives: 19.7 us -> none  [all_reduce_sum(): lax.all_to_all(jnp.broadcast_to(own, (devices, width)), peers, 0, 0, tile...]
    all_to_all x0 -> x1, waiting for transfers between devices: none -> 13.4 us  [all_reduce_sum(): lax.all_to_all(jnp.broadcast_to(own, (devices, width)), peers, 0, 0, tile...]
    all_to_all x0 -> x1, starting transfers between devices: none -> 6.18 us  [all_reduce_sum(): lax.all_to_all(jnp.broadcast_to(own, (devices, width)), peers, 0, 0, tile...]
  transfers between devices with their start and end apart: 6 -> 7, of which waited for: 4 -> 5; matrix products, arithmetic and copies ran while one was open for 5% -> 6% of each run, Pallas kernels for 0% -> 0%
where the time goes in v16:
time: 117 us
  waiting for transfers between devices  30.8 us (26%)
  starting transfers between devices  29.8 us (25%)
  blocking collectives  27 us (23%)
  matrix products  11.4 us (10%)
  local copies, waits for them, and re-layouts  8.9 us (8%)
  other arithmetic  6.86 us (6%)
  between operations  1.77 us (2%)
    all_to_all x1, blocking collectives, all_reduce_sum(): lax.all_to_all(half.reshape(devices, width), peers, 0, 0, tiled=True)  27 us
    all_to_all x1, waiting for transfers between devices, all_reduce_sum(): lax.all_to_all(jnp.broadcast_to(own, (devices, width)), peers, 0, 0, tile...  13.4 us
    all_to_all x1, starting transfers between devices, on_device(): lax.all_to_all(sample_prediction, MEMBER, split_axis=0, concat_axis=1, ti...  8.74 us
    all_to_all x1, waiting for transfers between devices, on_device(): lax.all_to_all(cot_share, MEMBER, split_axis=1, concat_axis=0, tiled=True)  8.71 us
    all_to_all x1, waiting for transfers between devices, on_device(): lax.all_to_all(sample_prediction, MEMBER, split_axis=0, concat_axis=1, ti...  6.9 us
    all_to_all x1, starting transfers between devices, all_reduce_sum(): lax.all_to_all(jnp.broadcast_to(own, (devices, width)), peers, 0, 0, tile...  6.18 us
    dot_general x6, matrix products, feature_conv(): jnp.einsum('mrwc,cd->mrwd', shifted[:, i:i + out_rows], kernel[i].reshape...  4.72 us
    ppermute x1, starting transfers between devices, extended(): lax.ppermute(x, axis, up)  4.49 us
  transfers between devices with their start and end apart: 7, of which 5 were waited for; matrix products, arithmetic and copies ran while one was open for 6% of the time, Pallas kernels for 0%

profile of v16, /device:TPU:1, one launch (start us, length us, event | category | flops | bytes accessed | tf_op | source)
XLA Modules:
  0.0 116.5 jit_solution(8169464775064047708)
XLA Ops:
  0.7 4.5 %collective-permute-start = (bf16[4,32,256]{2,1,0:T(8,128)(2,1)}, bf16[4,32,256]{2,1,0:T(8,128)(2,1)S(1)}, u32[]{:S(2)}, u32[]{:S(2)}) collective-permute-start(bf16[4,32,256]{2,1,0:T(8,128)(2,1)} %param.11), channel_id=1, source_target_pairs={{0,1},{1,2},{2,3},{3,4},{4,5},{5,6},{6,7},{7,8},{8,9},{9,10},{10,1... | collective-permute-start | bytes 196616 | tf_op jit(solution)/shard_map/ppermute | solution.py:17
  5.2 1.3 %collective-permute-start.1 = (bf16[4,32,256]{2,1,0:T(8,128)(2,1)}, bf16[4,32,256]{2,1,0:T(8,128)(2,1)S(1)}, u32[]{:S(2)}, u32[]{:S(2)}) collective-permute-start(bf16[4,32,256]{2,1,0:T(8,128)(2,1)} %param.11), channel_id=1, source_target_pairs={{1,0},{2,1},{3,2},{4,3},{5,4},{6,5},{7,6},{8,7},{9,8},{10,9},{11,1... | collective-permute-start | bytes 196616 | tf_op jit(solution)/shard_map/ppermute | solution.py:18
  6.5 0.9 convert_bitcast_fusion
  7.3 0.9 fusion.52
  8.2 0.8 fusion.68
  9.1 1.0 fusion.66
  10.2 1.0 fusion.65
  13.1 0.9 fusion.20
  14.0 0.6 pad_slice_fusion.1
  14.6 0.8 fusion.63
  15.4 0.8 fusion.64
  16.2 1.2 fusion.19
  19.0 0.8 add_convert_fusion
  20.2 0.8 copy.82
  20.9 8.7 %all-to-all-start = ((bf16[32,2,4,256]{3,2,1,0:T(4,128)(2,1)}), bf16[32,2,4,256]{3,2,1,0:T(4,128)(2,1)S(1)}, u32[]{:S(2)}, u32[]{:S(2)}) async-start(bf16[32,2,4,256]{3,2,1,0:T(4,128)(2,1)} %copy.82), calls=%async_computation | async-start | bytes 262144 | tf_op jit(solution)/shard_map/all_to_all | solution.py:156
  29.7 0.7 convert_bitcast_fusion.2
  31.1 6.9 %all-to-all-done = bf16[32,2,4,256]{3,2,1,0:T(4,128)(2,1)S(1)} async-done(((bf16[32,2,4,256]{3,2,1,0:T(4,128)(2,1)}), bf16[32,2,4,256]{3,2,1,0:T(4,128)(2,1)S(1)}, u32[]{:S(2)}, u32[]{:S(2)}) %all-to-all-start) | async-done | bytes 131104 | tf_op jit(solution)/shard_map/all_to_all | solution.py:156
  38.1 2.0 %sign_reduce_fusion = f32[4,16,4,256]{3,2,1,0:T(4,128)S(1)} fusion(f32[4,16,4,256]{3,1,2,0:T(8,128)S(1)} %copy.87, f32[4,16,4,256]{3,2,1,0:T(4,128)S(1)} %bitcast.176), kind=kLoop, calls=%fused_computation | loop fusion | flops 3080192 | bytes 786432 | tf_op jit(solution)/shard_map/reduce_sum | solution.py:165
  40.3 0.7 copy.88
  41.0 4.3 %all-to-all-start.1 = ((bf16[4,16,4,256]{3,2,0,1:T(4,128)(2,1)}), bf16[4,16,4,256]{3,2,0,1:T(4,128)(2,1)S(1)}, u32[]{:S(2)}, u32[]{:S(2)}) async-start(bf16[4,16,4,256]{3,2,0,1:T(4,128)(2,1)} %copy.88), calls=%async_computation.1 | async-start | bytes 262144 | tf_op jit(solution)/shard_map/all_to_all | solution.py:179
  45.4 8.7 %all-to-all-done.1 = bf16[4,16,4,256]{3,2,0,1:T(4,128)(2,1)S(1)} async-done(((bf16[4,16,4,256]{3,2,0,1:T(4,128)(2,1)}), bf16[4,16,4,256]{3,2,0,1:T(4,128)(2,1)S(1)}, u32[]{:S(2)}, u32[]{:S(2)}) %all-to-all-start.1) | async-done | bytes 131104 | tf_op jit(solution)/shard_map/all_to_all | solution.py:179
  54.4 0.9 fusion.27
  59.0 1.3 %collective-permute-start.2 = (f32[81920]{0:T(1024)S(1)}, f32[81920]{0:T(1024)S(1)}, u32[]{:S(2)}, u32[]{:S(2)}) collective-permute-start(f32[81920]{0:T(1024)S(1)} %slice_select_fusion), channel_id=1, source_target_pairs={{0,32},{32,0},{1,33},{33,1},{2,34},{34,2},{3,35},{35,3},{4,36},{36... | collective-permute-start | bytes 983048 | tf_op jit(solution)/shard_map/ppermute | solution.py:90
  60.3 1.3 %collective-permute-done.2 = f32[81920]{0:T(1024)S(1)} collective-permute-done((f32[81920]{0:T(1024)S(1)}, f32[81920]{0:T(1024)S(1)}, u32[]{:S(2)}, u32[]{:S(2)}) %collective-permute-start.2) | collective-permute-done | bytes 327712 | tf_op jit(solution)/shard_map/ppermute | solution.py:90
  61.6 27.0 %all_to_all.42 = f32[128,1,640]{2,1,0:T(1,128)S(1)} all-to-all(f32[128,1,640]{2,1,0:T(1,128)S(1)} %bitcast.187), channel_id=1, replica_groups=mesh['group'=4,'core'=2,'tile'=32] {'group','tile'}, dimensions={0} | all-to-all | bytes 655360 | tf_op jit(solution)/shard_map/all_to_all | solution.py:91
  88.8 0.9 broadcast_in_dim.32
  89.7 6.2 %all-to-all-start.3 = ((f32[128,1,640]{2,1,0:T(1,128)}), f32[128,1,640]{2,1,0:T(1,128)S(1)}, u32[]{:S(2)}, u32[]{:S(2)}) async-start(f32[128,1,640]{2,1,0:T(1,128)} %broadcast_in_dim.32), calls=%async_computation.3 | async-start | bytes 655360 | tf_op jit(solution)/shard_map/all_to_all | solution.py:93
  96.4 13.4 %all-to-all-done.3 = f32[128,1,640]{2,1,0:T(1,128)S(1)} async-done(((f32[128,1,640]{2,1,0:T(1,128)}), f32[128,1,640]{2,1,0:T(1,128)S(1)}, u32[]{:S(2)}, u32[]{:S(2)}) %all-to-all-start.3) | async-done | bytes 327712 | tf_op jit(solution)/shard_map/all_to_all | solution.py:93
  109.8 3.5 %collective-permute-start.3 = (f32[81920]{0:T(1024)S(1)}, f32[81920]{0:T(1024)S(1)}, u32[]{:S(2)}, u32[]{:S(2)}) collective-permute-start(f32[81920]{0:T(1024)S(1)} %bitcast.183), channel_id=1, source_target_pairs={{0,32},{32,0},{1,33},{33,1},{2,34},{34,2},{3,35},{35,3},{4,36},{36... | collective-permute-start | bytes 983048 | tf_op jit(solution)/shard_map/ppermute | solution.py:95
  113.3 0.6 copy.102
  114.6 0.9 slice.204
  115.9 0.6 fusion.49
  (71 shorter events, 10.0 us)
Async XLA Ops:
  0.6 11.4 %copy-start = (bf16[3,3,32,128]{3,2,1,0:T(8,128)(2,1)S(1)}, bf16[3,3,32,128]{3,2,1,0:T(8,128)(2,1)}, u32[]{:S(2)}) copy-start(bf16[3,3,32,128]{3,2,1,0:T(8,128)(2,1)} %param.17) | copy-start | bytes 221188
  0.6 10.6 %copy-start.1 = (bf16[4,32,256]{2,1,0:T(8,128)(2,1)S(1)}, bf16[4,32,256]{2,1,0:T(8,128)(2,1)}, u32[]{:S(2)}) copy-start(bf16[4,32,256]{2,1,0:T(8,128)(2,1)} %param.11) | copy-start | bytes 196612
  0.7 10.6 %collective-permute-start = (bf16[4,32,256]{2,1,0:T(8,128)(2,1)}, bf16[4,32,256]{2,1,0:T(8,128)(2,1)S(1)}, u32[]{:S(2)}, u32[]{:S(2)}) collective-permute-start(bf16[4,32,256]{2,1,0:T(8,128)(2,1)} %param.11), channel_id=1, source_target_pairs={{0,1},{1,2},{2,3},{3,4},{4,5},{5,6},{6,7},{7,8},{8,9},{9,10},{10,1... | collective-permute-start | bytes 196616 | tf_op jit(solution)/shard_map/ppermute | solution.py:17
  5.2 6.1 %collective-permute-start.1 = (bf16[4,32,256]{2,1,0:T(8,128)(2,1)}, bf16[4,32,256]{2,1,0:T(8,128)(2,1)S(1)}, u32[]{:S(2)}, u32[]{:S(2)}) collective-permute-start(bf16[4,32,256]{2,1,0:T(8,128)(2,1)} %param.11), channel_id=1, source_target_pairs={{1,0},{2,1},{3,2},{4,3},{5,4},{6,5},{7,6},{8,7},{9,8},{10,9},{11,1... | collective-permute-start | bytes 196616 | tf_op jit(solution)/shard_map/ppermute | solution.py:18
  19.0 0.9 copy-start.2
  19.0 0.9 copy-start.3
  20.9 17.1 %all-to-all-start = ((bf16[32,2,4,256]{3,2,1,0:T(4,128)(2,1)}), bf16[32,2,4,256]{3,2,1,0:T(4,128)(2,1)S(1)}, u32[]{:S(2)}, u32[]{:S(2)}) async-start(bf16[32,2,4,256]{3,2,1,0:T(4,128)(2,1)} %copy.82), calls=%async_computation | async-start | bytes 262144 | tf_op jit(solution)/shard_map/all_to_all | solution.py:156
  41.0 13.1 %all-to-all-start.1 = ((bf16[4,16,4,256]{3,2,0,1:T(4,128)(2,1)}), bf16[4,16,4,256]{3,2,0,1:T(4,128)(2,1)S(1)}, u32[]{:S(2)}, u32[]{:S(2)}) async-start(bf16[4,16,4,256]{3,2,0,1:T(4,128)(2,1)} %copy.88), calls=%async_computation.1 | async-start | bytes 262144 | tf_op jit(solution)/shard_map/all_to_all | solution.py:179
  59.0 2.6 %collective-permute-start.2 = (f32[81920]{0:T(1024)S(1)}, f32[81920]{0:T(1024)S(1)}, u32[]{:S(2)}, u32[]{:S(2)}) collective-permute-start(f32[81920]{0:T(1024)S(1)} %slice_select_fusion), channel_id=1, source_target_pairs={{0,32},{32,0},{1,33},{33,1},{2,34},{34,2},{3,35},{35,3},{4,36},{36... | collective-permute-start | bytes 983048 | tf_op jit(solution)/shard_map/ppermute | solution.py:90
  89.7 20.1 %all-to-all-start.3 = ((f32[128,1,640]{2,1,0:T(1,128)}), f32[128,1,640]{2,1,0:T(1,128)S(1)}, u32[]{:S(2)}, u32[]{:S(2)}) async-start(f32[128,1,640]{2,1,0:T(1,128)} %broadcast_in_dim.32), calls=%async_computation.3 | async-start | bytes 655360 | tf_op jit(solution)/shard_map/all_to_all | solution.py:93
  109.8 4.7 %collective-permute-start.3 = (f32[81920]{0:T(1024)S(1)}, f32[81920]{0:T(1024)S(1)}, u32[]{:S(2)}, u32[]{:S(2)}) collective-permute-start(f32[81920]{0:T(1024)S(1)} %bitcast.183), channel_id=1, source_target_pairs={{0,32},{32,0},{1,33},{33,1},{2,34},{34,2},{3,35},{35,3},{4,36},{36... | collective-permute-start | bytes 983048 | tf_op jit(solution)/shard_map/ppermute | solution.py:95

commit v17 on v12

--- a/solution.py
+++ b/solution.py
@@ -165,7 +165,9 @@
     ).astype(jnp.float32)[:, None]
     pair_differ = sample_group_predictions[:, :, None] - sample_group_predictions[:, None, :]
     abs_sums = jnp.sum(jnp.abs(pair_differ), axis=2)
-    sign_sums = jnp.sum(jnp.sign(pair_differ), axis=2)
+    sign_sums = jnp.sum(
+        (pair_differ > 0).astype(jnp.float32) - (pair_differ < 0).astype(jnp.float32), axis=2
+    )
     crps_share = jnp.mean(jnp.abs(sample_group_predictions - truth), axis=1) - jnp.sum(
         abs_sums, axis=1
     ) / (2 * member_count * (member_count - 1))

time: 117 us -> 117 us (level)
  no operation moved by 1% of the time
where the time goes in v17:
time: 117 us; the launch traced here: 116 us
  blocking collectives  46.7 us (40%)
  starting transfers between devices  23.9 us (20%)
  waiting for transfers between devices  17.4 us (15%)
  matrix products  11.4 us (10%)
  local copies, waits for them, and re-layouts  9.03 us (8%)
  other arithmetic  5.88 us (5%)
  between operations  1.76 us (2%)
    all_to_all x1, blocking collectives, all_reduce_sum(): lax.all_to_all(half.reshape(devices, width), peers, 0, 0, tiled=True)  27 us
    all_to_all x1, blocking collectives, all_reduce_sum(): lax.all_to_all(jnp.broadcast_to(own, (devices, width)), peers, 0, 0, tile...  19.7 us
    all_to_all x1, starting transfers between devices, on_device(): lax.all_to_all(sample_prediction, MEMBER, split_axis=0, concat_axis=1, ti...  9.22 us
    all_to_all x1, waiting for transfers between devices, on_device(): lax.all_to_all(cot_share, MEMBER, split_axis=1, concat_axis=0, tiled=True)  8.71 us
    all_to_all x1, waiting for transfers between devices, on_device(): lax.all_to_all(sample_prediction, MEMBER, split_axis=0, concat_axis=1, ti...  6.9 us
    dot_general x6, matrix products, feature_conv(): jnp.einsum('mrwc,cd->mrwd', shifted[:, i:i + out_rows], kernel[i].reshape...  4.68 us
    ppermute x1, starting transfers between devices, extended(): before = lax.ppermute(last, axis, up)  4.35 us
    all_to_all x1, starting transfers between devices, on_device(): lax.all_to_all(cot_share, MEMBER, split_axis=1, concat_axis=0, tiled=True)  4.34 us
  transfers between devices with their start and end apart: 6, of which 4 were waited for; matrix products, arithmetic and copies ran while one was open for 5% of the time, Pallas kernels for 0%

profile of v17, /device:TPU:1, one launch (start us, length us, event | category | flops | bytes accessed | tf_op | source)
XLA Modules:
  0.0 116.0 jit_solution(14897799676552649964)
XLA Ops:
  0.7 0.9 fusion.68
  1.6 4.3 %collective-permute-start = (bf16[3,32,256]{2,1,0:T(8,128)(2,1)S(1)}, bf16[3,32,256]{2,1,0:T(8,128)(2,1)S(1)}, u32[]{:S(2)}, u32[]{:S(2)}) collective-permute-start(bf16[3,32,256]{2,1,0:T(8,128)(2,1)S(1)} %get-tuple-element.31), channel_id=1, source_target_pairs={{0,1},{1,2},{2,3},{3,4},{4,5},{5,6},{6,7},{7,8},{8,9},{9,10},{10,1... | collective-permute-start | bytes 147464 | tf_op jit(solution)/shard_map/ppermute | solution.py:19
  5.9 1.3 %collective-permute-start.1 = (bf16[3,32,256]{2,1,0:T(8,128)(2,1)S(1)}, bf16[3,32,256]{2,1,0:T(8,128)(2,1)S(1)}, u32[]{:S(2)}, u32[]{:S(2)}) collective-permute-start(bf16[3,32,256]{2,1,0:T(8,128)(2,1)S(1)} %get-tuple-element.30), channel_id=1, source_target_pairs={{1,0},{2,1},{3,2},{4,3},{5,4},{6,5},{7,6},{8,7},{9,8},{10,9},{11,1... | collective-permute-start | bytes 147464 | tf_op jit(solution)/shard_map/ppermute | solution.py:20
  7.2 0.9 fusion.53
  8.1 0.8 fusion.70
  9.0 1.0 fusion.67
  10.1 1.0 fusion.66
  13.0 0.9 fusion.21
  13.9 0.6 pad_slice_fusion.1
  14.5 0.8 fusion.64
  15.3 0.8 fusion.65
  16.1 1.1 fusion.20
  17.7 0.6 fusion.63
  18.3 0.6 convolution_add_fusion.1
  18.9 0.8 add_convert_fusion
  20.0 0.8 copy.97
  20.8 9.2 %all-to-all-start = ((bf16[32,2,4,256]{3,2,1,0:T(4,128)(2,1)}), bf16[32,2,4,256]{3,2,1,0:T(4,128)(2,1)S(1)}, u32[]{:S(2)}, u32[]{:S(2)}) async-start(bf16[32,2,4,256]{3,2,1,0:T(4,128)(2,1)} %copy.97), calls=%async_computation | async-start | bytes 262144 | tf_op jit(solution)/shard_map/all_to_all | solution.py:158
  30.0 0.7 convert_bitcast_fusion.1
  31.4 6.9 %all-to-all-done = bf16[32,2,4,256]{3,2,1,0:T(4,128)(2,1)S(1)} async-done(((bf16[32,2,4,256]{3,2,1,0:T(4,128)(2,1)}), bf16[32,2,4,256]{3,2,1,0:T(4,128)(2,1)S(1)}, u32[]{:S(2)}, u32[]{:S(2)}) %all-to-all-start) | async-done | bytes 131104 | tf_op jit(solution)/shard_map/all_to_all | solution.py:158
  38.4 2.3 %subtract_reduce_fusion = (f32[4,16,4,256]{3,2,1,0:T(4,128)S(1)}, f32[4,4,256]{2,1,0:T(4,128)S(1)}) fusion(f32[4,16,4,256]{3,1,2,0:T(8,128)S(1)} %copy.100, f32[4,16,4,256]{3,2,1,0:T(4,128)S(1)} %bitcast.175), kind=kLoop, calls=%fused_computation.4 | loop fusion | flops 9367552 | bytes 802816 | tf_op jit(solution)/shard_map/reduce_sum | solution.py:168
  41.0 0.7 copy.102
  41.7 4.3 %all-to-all-start.1 = ((bf16[4,16,4,256]{3,2,0,1:T(4,128)(2,1)}), bf16[4,16,4,256]{3,2,0,1:T(4,128)(2,1)S(1)}, u32[]{:S(2)}, u32[]{:S(2)}) async-start(bf16[4,16,4,256]{3,2,0,1:T(4,128)(2,1)} %copy.102), calls=%async_computation.1 | async-start | bytes 262144 | tf_op jit(solution)/shard_map/all_to_all | solution.py:182
  46.0 8.7 %all-to-all-done.1 = bf16[4,16,4,256]{3,2,0,1:T(4,128)(2,1)S(1)} async-done(((bf16[4,16,4,256]{3,2,0,1:T(4,128)(2,1)}), bf16[4,16,4,256]{3,2,0,1:T(4,128)(2,1)S(1)}, u32[]{:S(2)}, u32[]{:S(2)}) %all-to-all-start.1) | async-done | bytes 131104 | tf_op jit(solution)/shard_map/all_to_all | solution.py:182
  55.0 0.9 fusion.28
  59.6 1.3 %collective-permute-start.2 = (f32[81920]{0:T(1024)S(1)}, f32[81920]{0:T(1024)S(1)}, u32[]{:S(2)}, u32[]{:S(2)}) collective-permute-start(f32[81920]{0:T(1024)S(1)} %slice_select_fusion), channel_id=1, source_target_pairs={{0,32},{32,0},{1,33},{33,1},{2,34},{34,2},{3,35},{35,3},{4,36},{36... | collective-permute-start | bytes 983048 | tf_op jit(solution)/shard_map/ppermute | solution.py:92
  60.9 1.3 %collective-permute-done.2 = f32[81920]{0:T(1024)S(1)} collective-permute-done((f32[81920]{0:T(1024)S(1)}, f32[81920]{0:T(1024)S(1)}, u32[]{:S(2)}, u32[]{:S(2)}) %collective-permute-start.2) | collective-permute-done | bytes 327712 | tf_op jit(solution)/shard_map/ppermute | solution.py:92
  62.2 27.0 %all_to_all.42 = f32[128,1,640]{2,1,0:T(1,128)S(1)} all-to-all(f32[128,1,640]{2,1,0:T(1,128)S(1)} %bitcast.181), channel_id=1, replica_groups=mesh['group'=4,'core'=2,'tile'=32] {'group','tile'}, dimensions={0} | all-to-all | bytes 655360 | tf_op jit(solution)/shard_map/all_to_all | solution.py:93
  89.6 19.7 %all_to_all.43 = f32[128,1,640]{2,1,0:T(1,128)S(1)} all-to-all(f32[128,1,640]{2,1,0:T(1,128)S(1)} %broadcast_in_dim.29), channel_id=1, replica_groups=mesh['group'=4,'core'=2,'tile'=32] {'group','tile'}, dimensions={0} | all-to-all | bytes 655360 | tf_op jit(solution)/shard_map/all_to_all | solution.py:95
  109.4 3.4 %collective-permute-start.3 = (f32[81920]{0:T(1024)S(1)}, f32[81920]{0:T(1024)S(1)}, u32[]{:S(2)}, u32[]{:S(2)}) collective-permute-start(f32[81920]{0:T(1024)S(1)} %bitcast.177), channel_id=1, source_target_pairs={{0,32},{32,0},{1,33},{33,1},{2,34},{34,2},{3,35},{35,3},{4,36},{36... | collective-permute-start | bytes 983048 | tf_op jit(solution)/shard_map/ppermute | solution.py:97
  112.9 0.6 copy.116
  114.0 0.9 slice.202
  115.4 0.6 fusion.50
  (68 shorter events, 8.5 us)
Async XLA Ops:
  0.6 11.3 %copy-start = (bf16[3,3,32,128]{3,2,1,0:T(8,128)(2,1)S(1)}, bf16[3,3,32,128]{3,2,1,0:T(8,128)(2,1)}, u32[]{:S(2)}) copy-start(bf16[3,3,32,128]{3,2,1,0:T(8,128)(2,1)} %param.17) | copy-start | bytes 221188
  0.6 10.5 %copy-start.1 = (bf16[4,32,256]{2,1,0:T(8,128)(2,1)S(1)}, bf16[4,32,256]{2,1,0:T(8,128)(2,1)}, u32[]{:S(2)}) copy-start(bf16[4,32,256]{2,1,0:T(8,128)(2,1)} %param.11) | copy-start | bytes 196612
  1.6 9.6 %collective-permute-start = (bf16[3,32,256]{2,1,0:T(8,128)(2,1)S(1)}, bf16[3,32,256]{2,1,0:T(8,128)(2,1)S(1)}, u32[]{:S(2)}, u32[]{:S(2)}) collective-permute-start(bf16[3,32,256]{2,1,0:T(8,128)(2,1)S(1)} %get-tuple-element.31), channel_id=1, source_target_pairs={{0,1},{1,2},{2,3},{3,4},{4,5},{5,6},{6,7},{7,8},{8,9},{9,10},{10,1... | collective-permute-start | bytes 147464 | tf_op jit(solution)/shard_map/ppermute | solution.py:19
  5.9 5.3 %collective-permute-start.1 = (bf16[3,32,256]{2,1,0:T(8,128)(2,1)S(1)}, bf16[3,32,256]{2,1,0:T(8,128)(2,1)S(1)}, u32[]{:S(2)}, u32[]{:S(2)}) collective-permute-start(bf16[3,32,256]{2,1,0:T(8,128)(2,1)S(1)} %get-tuple-element.30), channel_id=1, source_target_pairs={{1,0},{2,1},{3,2},{4,3},{5,4},{6,5},{7,6},{8,7},{9,8},{10,9},{11,1... | collective-permute-start | bytes 147464 | tf_op jit(solution)/shard_map/ppermute | solution.py:20
  18.9 0.9 copy-start.2
  18.9 0.9 copy-start.3
  20.8 17.6 %all-to-all-start = ((bf16[32,2,4,256]{3,2,1,0:T(4,128)(2,1)}), bf16[32,2,4,256]{3,2,1,0:T(4,128)(2,1)S(1)}, u32[]{:S(2)}, u32[]{:S(2)}) async-start(bf16[32,2,4,256]{3,2,1,0:T(4,128)(2,1)} %copy.97), calls=%async_computation | async-start | bytes 262144 | tf_op jit(solution)/shard_map/all_to_all | solution.py:158
  41.7 13.1 %all-to-all-start.1 = ((bf16[4,16,4,256]{3,2,0,1:T(4,128)(2,1)}), bf16[4,16,4,256]{3,2,0,1:T(4,128)(2,1)S(1)}, u32[]{:S(2)}, u32[]{:S(2)}) async-start(bf16[4,16,4,256]{3,2,0,1:T(4,128)(2,1)} %copy.102), calls=%async_computation.1 | async-start | bytes 262144 | tf_op jit(solution)/shard_map/all_to_all | solution.py:182
  59.6 2.5 %collective-permute-start.2 = (f32[81920]{0:T(1024)S(1)}, f32[81920]{0:T(1024)S(1)}, u32[]{:S(2)}, u32[]{:S(2)}) collective-permute-start(f32[81920]{0:T(1024)S(1)} %slice_select_fusion), channel_id=1, source_target_pairs={{0,32},{32,0},{1,33},{33,1},{2,34},{34,2},{3,35},{35,3},{4,36},{36... | collective-permute-start | bytes 983048 | tf_op jit(solution)/shard_map/ppermute | solution.py:92
  109.4 4.6 %collective-permute-start.3 = (f32[81920]{0:T(1024)S(1)}, f32[81920]{0:T(1024)S(1)}, u32[]{:S(2)}, u32[]{:S(2)}) collective-permute-start(f32[81920]{0:T(1024)S(1)} %bitcast.177), channel_id=1, source_target_pairs={{0,32},{32,0},{1,33},{33,1},{2,34},{34,2},{3,35},{35,3},{4,36},{36... | collective-permute-start | bytes 983048 | tf_op jit(solution)/shard_map/ppermute | solution.py:97
